TPU v7x, 256 devices: a whole 4x4x8 slice. The times are simulated.
256 devices in a mesh: branch: 2 (over z_hi), head: 4 (over x), page: 32 (over y, z_lo, core).
Axes of the slice: x: 4, y: 4, z: 8 (z_hi: 2, z_lo: 4; z = z_hi * 4 + z_lo), core: 2. Of those that a mesh axis runs over, the one named last changes fastest.
Arguments:
- queries: bfloat16 [16384, 4096], P(('branch', 'page'), 'head'), may hold values from -6 to 6
- new_keys: bfloat16 [16384, 512], P(('branch', 'page'), 'head'), may hold values from -6 to 6
- new_values: bfloat16 [16384, 512], P(('branch', 'page'), 'head'), may hold values from -6 to 6
- cache_keys: bfloat16 [128, 64, 512], P(('branch', 'page'), None, 'head'), may hold values from -6 to 6
- cache_values: bfloat16 [128, 64, 512], P(('branch', 'page'), None, 'head'), may hold values from -6 to 6
- block_table: int32 [64, 32], P(('branch', 'page')), may hold values from 0 to 127, as said below
- ancestor_len: int32 [64], P(('branch', 'page')), may hold values from 256 to 2048, as said below
- out_weight: bfloat16 [4096, 8192], P('head', 'page'), may hold values from -0.375 to 0.375
Outputs:
- layer_out: bfloat16 [16384, 8192], P(('branch', 'head'), 'page')
Inputs may be any that keep to these rules, and one draw needn't show every extreme that they name: `block_table`: each row names 32 distinct page ids; its first 4 entries are the same for every branch. `ancestor_len`: every branch's ancestors fill its first 4 pages; some branch reaches the maximum.
All inputs are finite; a program needn't handle non-finite values.
Results may differ from a plain program's by a relative error of at most 0.018.
Values may be sent and summed in bfloat16 or wider, within the bound.
No kernel may reach another device: no remote copies, remote signals or barrier semaphores. Data moves between devices by JAX's collectives and lax.ppermute only.
A program may use at most 64 MiB of HBM per device.

v0:
```python
import math

import jax
import jax.numpy as jnp
from jax import lax
from jax.sharding import PartitionSpec as P

HD = 128
PAGE_TOK = 64
NEW = 256


masked_fill = -1e30


def attend(carried, queries_here, key_block, value_block, usable, score_scale):
    running_max, running_sum, accumulated = carried
    scores = (
        jnp.einsum("kbnd,jkd->kbnj", queries_here, key_block, preferred_element_type=jnp.float32)
        * score_scale
    )
    key_mask = usable[None, :, None, :]
    block_max = jnp.max(jnp.where(key_mask, scores, masked_fill), axis=-1)
    new_max = jnp.maximum(running_max, block_max)
    shrink = jnp.exp(running_max - new_max)
    weights = jnp.where(key_mask, jnp.exp(scores - new_max[..., None]), 0.0).astype(jnp.bfloat16)
    running_sum = running_sum * shrink + jnp.sum(weights.astype(jnp.float32), axis=-1)
    accumulated = accumulated * shrink[..., None] + jnp.einsum(
        "kbnj,jkd->kbnd", weights, value_block, preferred_element_type=jnp.float32
    )
    return (new_max, running_sum, accumulated)


def shards(
    queries, new_keys, new_values, cache_keys, cache_values, block_table, ancestor_len, out_weight
):
    row_count = queries.shape[0]
    branches_here = block_table.shape[0]
    slot_count = block_table.shape[1]
    heads_here = queries.shape[1] // HD
    kv_here = new_keys.shape[1] // HD
    group_size = heads_here // kv_here
    query_span = NEW * group_size
    score_scale = 1.0 / math.sqrt(HD)
    queries_here = (
        queries.reshape(branches_here, NEW, kv_here, group_size, HD)
        .transpose(2, 0, 1, 3, 4)
        .reshape(kv_here, branches_here, query_span, HD)
    )
    own_keys = new_keys.reshape(row_count, kv_here, HD)
    own_values = new_values.reshape(row_count, kv_here, HD)
    token_index = (
        jnp.arange(branches_here, dtype=jnp.int32)[:, None] * NEW
        + jnp.arange(query_span, dtype=jnp.int32)[None, :] // group_size
    )
    key_index = jnp.arange(row_count, dtype=jnp.int32)
    own_mask = (key_index[None, None, :] // NEW == token_index[:, :, None] // NEW) & (
        key_index[None, None, :] <= token_index[:, :, None]
    )
    own_scores = (
        jnp.einsum("kbnd,jkd->kbnj", queries_here, own_keys, preferred_element_type=jnp.float32)
        * score_scale
    )
    start_max = jnp.max(jnp.where(own_mask[None], own_scores, masked_fill), axis=-1)
    own_weights = jnp.where(own_mask[None], jnp.exp(own_scores - start_max[..., None]), 0.0).astype(
        jnp.bfloat16
    )
    start_sum = jnp.sum(own_weights.astype(jnp.float32), axis=-1)
    start_acc = jnp.einsum(
        "kbnj,jkd->kbnd", own_weights, own_values, preferred_element_type=jnp.float32
    )
    slot_first = jnp.arange(slot_count, dtype=jnp.int32) * PAGE_TOK
    slot_limit = jnp.clip(ancestor_len[:, None] - slot_first[None, :], 0, PAGE_TOK)
    carried = (start_max, start_sum, start_acc)
    piece_keys = lax.all_gather(cache_keys, ("branch", "page"), axis=0, tiled=True)
    piece_values = lax.all_gather(cache_values, ("branch", "page"), axis=0, tiled=True)
    page_count = piece_keys.shape[0]
    page_ids = jnp.arange(page_count, dtype=jnp.int32)
    slot_hits = block_table[:, :, None] == page_ids[None, None, :]
    live_tokens = jnp.sum(jnp.where(slot_hits, slot_limit[:, :, None], 0), axis=1)
    usable = jnp.arange(PAGE_TOK, dtype=jnp.int32)[None, None, :] < live_tokens[:, :, None]
    key_total = page_count * PAGE_TOK
    block_len = math.gcd(key_total, 512)
    block_count = key_total // block_len
    key_blocks = piece_keys.reshape(block_count, block_len, kv_here, HD)
    value_blocks = piece_values.reshape(block_count, block_len, kv_here, HD)
    usable_blocks = usable.reshape(branches_here, block_count, block_len).transpose(1, 0, 2)

    def block_step(state, block_item):
        key_block, value_block, usable_block = block_item
        state = attend(state, queries_here, key_block, value_block, usable_block, score_scale)
        return (state, None)

    carried, _ = lax.scan(block_step, carried, (key_blocks, value_blocks, usable_blocks))
    final_max, final_sum, final_acc = carried
    attn_out = (final_acc / final_sum[..., None]).reshape(
        kv_here, branches_here, NEW, group_size, HD
    )
    attn_out = (
        attn_out.transpose(1, 2, 0, 3, 4).reshape(row_count, heads_here * HD).astype(jnp.bfloat16)
    )
    partial_term = jnp.dot(
        lax.all_gather(attn_out, "page", axis=0, tiled=True),
        out_weight,
        preferred_element_type=jnp.float32,
    ).astype(jnp.bfloat16)
    summed = lax.psum_scatter(
        partial_term.astype(jnp.float32).astype(jnp.bfloat16),
        "head",
        scatter_dimension=0,
        tiled=True,
    )
    return summed


def solution(mesh):
    in_specs = (
        P(("branch", "page"), "head"),
        P(("branch", "page"), "head"),
        P(("branch", "page"), "head"),
        P(("branch", "page"), None, "head"),
        P(("branch", "page"), None, "head"),
        P(("branch", "page"), None),
        P(("branch", "page")),
        P("head", "page"),
    )
    out_specs = P(("branch", "head"), "page")
    return jax.shard_map(shards, mesh=mesh, in_specs=in_specs, out_specs=out_specs, check_vma=False)
```

profile of v0, /device:TPU:24, one launch (start us, length us, event | category | flops | bytes accessed | tf_op | source)
XLA Modules:
  0.0 489.3 jit_solution(336189161934628019)
XLA Ops:
  15.0 109.8 %all-gather.4.cloned.1.call-done = bf16[128,64,128]{2,1,0:T(8,128)(2,1)} async-done(((bf16[2,64,128]{2,1,0:T(8,128)(2,1)}), bf16[128,64,128]{2,1,0:T(8,128)(2,1)}) %all-gather.4.cloned.1.call-update) | async-done | bytes 2097168 | tf_op jit(solution)/shard_map/all_gather | solution.py:75
  124.9 114.1 %all-gather.6.cloned.1.call-done = bf16[128,64,128]{2,1,0:T(8,128)(2,1)} async-done(((bf16[2,64,128]{2,1,0:T(8,128)(2,1)}), bf16[128,64,128]{2,1,0:T(8,128)(2,1)}) %all-gather.6.cloned.1.call-update) | async-done | bytes 2097168 | tf_op jit(solution)/shard_map/all_gather | solution.py:76
  239.0 80.6 %while.14 = (s32[]{:T(128)}, f32[1,1,2048]{2,1,0:T(1,128)S(1)}, f32[1,1,2048]{2,1,0:T(1,128)S(1)}, f32[1,1,2048,128]{3,2,1,0:T(8,128)S(1)}, pred[16,1,512]{2,0,1...) while((s32[]{:T(128)}, f32[1,1,2048]{2,1,0:T(1,128)S(1)}, ...), condition=%wide.region_6.7_spmd, body=%wide.region_3.6_spmd.sunk | while | flops 551030784 | bytes 15600241 | solution.py:94
  239.0 1.6 select_reduce_fusion.4
  241.6 2.4 fusion.24
  246.7 2.4 fusion.24
  249.1 1.6 select_reduce_fusion.4
  251.7 2.4 fusion.24
  256.7 2.4 fusion.24
  261.8 2.4 fusion.24
  266.8 2.4 fusion.24
  271.8 2.4 fusion.24
  276.9 2.4 fusion.24
  281.9 2.4 fusion.24
  286.9 2.4 fusion.24
  292.0 2.4 fusion.24
  297.0 2.4 fusion.24
  302.0 2.4 fusion.24
  307.1 2.4 fusion.24
  312.1 2.4 fusion.24
  317.2 2.4 fusion.24
  321.0 99.0 %all-gather.8.cloned.1.call-done = bf16[8192,1024]{1,0:T(8,128)(2,1)} async-done(((bf16[256,1024]{1,0:T(8,128)(2,1)}), bf16[8192,1024]{1,0:T(8,128)(2,1)}) %all-gather.8.cloned.1.call-update) | async-done | bytes 16777232 | tf_op jit(solution)/shard_map/all_gather | solution.py:103
  420.0 12.2 %convolution_convert_fusion = bf16[8192,256]{1,0:T(8,128)(2,1)} fusion(bf16[8192,1024]{1,0:T(8,128)(2,1)} %all-gather.8.cloned.1.call-done, bf16[1024,256]{1,0:T(8,128)(2,1)S(1)} %copy-done), kind=kOutput, calls=%fused_computation.16 | convolution fusion | flops 4297064448 | bytes 21495808 | tf_op jit(solution)/shard_map/dot_general | solution.py:102
  432.3 50.4 %reduce-scatter.2.cloned.1.call-done = bf16[2048,256]{1,0:T(8,128)(2,1)} async-done(((bf16[8192,256]{1,0:T(8,128)(2,1)}), bf16[2048,256]{1,0:T(8,128)(2,1)}) %reduce-scatter.2.cloned.1.call-update) | async-done | bytes 1048592 | tf_op jit(solution)/shard_map/reduce_scatter | solution.py:107
  (122 shorter events, 47.1 us)
Async XLA Ops:
  6.5 413.5 %copy-start = (bf16[1024,256]{1,0:T(8,128)(2,1)S(1)}, bf16[1024,256]{1,0:T(8,128)(2,1)}, u32[]{:S(2)}) copy-start(bf16[1024,256]{1,0:T(8,128)(2,1)} %param.17) | copy-start | bytes 1572868
  6.5 118.3 %all-gather.4.cloned.1.call-start = ((), (), s32[]{:S(2)}) async-start(), calls=%async_computation.1 | async-start | bytes 2129920 | tf_op jit(solution)/shard_map/all_gather | solution.py:75
  7.3 231.8 %all-gather.6.cloned.1.call-start = ((), (), s32[]{:S(2)}) async-start(), calls=%async_computation.2 | async-start | bytes 2129920 | tf_op jit(solution)/shard_map/all_gather | solution.py:76
  8.0 412.0 %all-gather.8.cloned.1.call-start = ((), (), s32[]{:S(2)}) async-start(), calls=%async_computation.3 | async-start | bytes 17301504 | tf_op jit(solution)/shard_map/all_gather | solution.py:103
  9.3 5.2 %copy-start.1 = (bf16[256,128]{1,0:T(8,128)(2,1)S(1)}, bf16[256,128]{1,0:T(8,128)(2,1)}, u32[]{:S(2)}) copy-start(bf16[256,128]{1,0:T(8,128)(2,1)} %param.12) | copy-start | bytes 196612
  321.0 161.8 %reduce-scatter.2.cloned.1.call-start = ((), (), s32[]{:S(2)}) async-start(), calls=%async_computation.4 | async-start | bytes 5242880 | tf_op jit(solution)/shard_map/reduce_scatter | solution.py:107
Sparse Core Ops, SparseCore 0:
  9.2 115.6 all-gather.3
  126.7 112.2 all-gather.5
  321.1 98.8 all-gather.7
  432.4 50.2 reduce-scatter.1
where the time goes:
time: 491 us; the launch traced here: 489 us
  waiting for transfers between devices  375 us (76%)
  matrix products  79 us (16%)
  other arithmetic  16.3 us (3%)
  between operations  13.8 us (3%)
    all_gather x1, waiting for transfers between devices, shards(): lax.all_gather(cache_values, ('branch', 'page'), axis=0, tiled=True)  114 us
    all_gather x1, waiting for transfers between devices, shards(): lax.all_gather(cache_keys, ('branch', 'page'), axis=0, tiled=True)  110 us
    all_gather x1, waiting for transfers between devices, shards(): lax.all_gather(attn_out, 'page', axis=0, tiled=True)  99 us
    reduce_scatter x1, waiting for transfers between devices, shards(): lax.psum_scatter(partial_term.astype(jnp.float32).astype(jnp.bfloat16), '...  50.4 us
    dot_general x16, matrix products, attend(): jnp.einsum('kbnj,jkd->kbnd', weights, value_block, preferred_element_type...  38.5 us
    dot_general x16, matrix products, attend(): jnp.einsum('kbnd,jkd->kbnj', queries_here, key_block, preferred_element_t...  26.3 us
    reduce_sum x16, other arithmetic, attend(): jnp.sum(weights.astype(jnp.float32), axis=-1)  13.8 us
    dot_general x1, matrix products, shards(): jnp.dot(lax.all_gather(attn_out, 'page', axis=0, tiled=True), out_weight,...  12.2 us
  transfers between devices with their start and end apart: 4, of which 4 were waited for; matrix products, arithmetic and copies ran while one was open for 1% of the time, Pallas kernels for 0%

commit v1 on v0

v1 whole, which is shorter than its diff:
```python
import math

import jax
import jax.numpy as jnp
from jax import lax
from jax.sharding import PartitionSpec as P

HD = 128
PAGE_TOK = 64
NEW = 256


masked_fill = -1e30


def shards(
    queries, new_keys, new_values, cache_keys, cache_values, block_table, ancestor_len, out_weight
):
    row_count = queries.shape[0]
    heads_here = queries.shape[1] // HD
    kv_here = new_keys.shape[1] // HD
    group_size = heads_here // kv_here
    slot_count = block_table.shape[1]
    score_scale = 1.0 / math.sqrt(HD)

    q = queries.reshape(row_count, kv_here, group_size, HD).transpose(1, 2, 0, 3)
    own_k = new_keys.reshape(row_count, kv_here, HD).transpose(1, 0, 2)
    own_v = new_values.reshape(row_count, kv_here, HD).transpose(1, 0, 2)

    kv_local = jnp.concatenate([cache_keys, cache_values], axis=-1)
    kv_all = lax.all_gather(kv_local, ("branch", "page"), axis=0, tiled=True)
    kv_sel = jnp.take(kv_all, block_table[0], axis=0)
    anc_len = slot_count * PAGE_TOK
    kv_sel = kv_sel.reshape(anc_len, 2, kv_here, HD)
    anc_k = kv_sel[:, 0].transpose(1, 0, 2)
    anc_v = kv_sel[:, 1].transpose(1, 0, 2)

    own_scores = (
        jnp.einsum("kgnd,kjd->kgnj", q, own_k, preferred_element_type=jnp.float32) * score_scale
    )
    anc_scores = (
        jnp.einsum("kgnd,kjd->kgnj", q, anc_k, preferred_element_type=jnp.float32) * score_scale
    )
    places = jnp.arange(row_count, dtype=jnp.int32)
    own_mask = places[None, :] <= places[:, None]
    anc_mask = jnp.arange(anc_len, dtype=jnp.int32) < ancestor_len[0]
    own_m = jnp.where(own_mask[None, None], own_scores, masked_fill)
    anc_m = jnp.where(anc_mask[None, None, None, :], anc_scores, masked_fill)
    row_max = jnp.maximum(jnp.max(own_m, axis=-1), jnp.max(anc_m, axis=-1))[..., None]
    own_w = jnp.where(own_mask[None, None], jnp.exp(own_scores - row_max), 0.0).astype(jnp.bfloat16)
    anc_w = jnp.where(anc_mask[None, None, None, :], jnp.exp(anc_scores - row_max), 0.0).astype(
        jnp.bfloat16
    )
    denom = jnp.sum(own_w.astype(jnp.float32), axis=-1) + jnp.sum(anc_w.astype(jnp.float32), axis=-1)
    summed = jnp.einsum(
        "kgnj,kjd->kgnd", own_w, own_v, preferred_element_type=jnp.float32
    ) + jnp.einsum("kgnj,kjd->kgnd", anc_w, anc_v, preferred_element_type=jnp.float32)
    attn = (summed / denom[..., None]).astype(jnp.bfloat16)
    attn_out = attn.transpose(2, 0, 1, 3).reshape(row_count, heads_here * HD)

    partial_term = jnp.dot(
        lax.all_gather(attn_out, "page", axis=0, tiled=True),
        out_weight,
        preferred_element_type=jnp.float32,
    ).astype(jnp.bfloat16)
    summed_out = lax.psum_scatter(partial_term, "head", scatter_dimension=0, tiled=True)
    return summed_out


def solution(mesh):
    in_specs = (
        P(("branch", "page"), "head"),
        P(("branch", "page"), "head"),
        P(("branch", "page"), "head"),
        P(("branch", "page"), None, "head"),
        P(("branch", "page"), None, "head"),
        P(("branch", "page"), None),
        P(("branch", "page")),
        P("head", "page"),
    )
    out_specs = P(("branch", "head"), "page")
    return jax.shard_map(shards, mesh=mesh, in_specs=in_specs, out_specs=out_specs, check_vma=False)
```

time: 491 us -> 331 us (0.67)
  waiting for transfers between devices: 375 us -> 282 us
  matrix products: 79 us -> 20.5 us
  other arithmetic: 16.3 us -> 8.85 us
    all_gather x2 -> x1, waiting for transfers between devices: 224 us -> 112 us  [shards(): kv_all = lax.all_gather(kv_local, ('branch', 'page'), axis=0, tiled=True)]
    dot_general x34 -> x4, matrix products: 66.7 us -> 8.04 us  [the longest x1 2.73 us: shards(): jnp.einsum('kgnd,kjd->kgnj', q, anc_k, preferred_element_type=jnp.float32)]
    all_gather x1, waiting for transfers between devices: 99 us -> 119 us  [shards(): lax.all_gather(attn_out, 'page', axis=0, tiled=True)]
    reduce_sum x18 -> x2, other arithmetic: 15.2 us -> 5.34 us  [the longest x1 4.9 us: shards(): jnp.sum(anc_w.astype(jnp.float32), axis=-1)]
  transfers between devices with their start and end apart: 4 -> 3, of which waited for: 4 -> 3; matrix products, arithmetic and copies ran while one was open for 1% -> 2% of each run, Pallas kernels for 0% -> 0%
where the time goes in v1:
time: 331 us; the launch traced here: 330 us
  waiting for transfers between devices  282 us (85%)
  matrix products  20.5 us (6%)
  between operations  13.9 us (4%)
  other arithmetic  8.85 us (3%)
  local copies, waits for them, and re-layouts  4.65 us (1%)
    all_gather x1, waiting for transfers between devices, shards(): lax.all_gather(attn_out, 'page', axis=0, tiled=True)  119 us
    all_gather x1, waiting for transfers between devices, shards(): kv_all = lax.all_gather(kv_local, ('branch', 'page'), axis=0, tiled=True)  112 us
    reduce_scatter x1, waiting for transfers between devices, shards(): lax.psum_scatter(partial_term, 'head', scatter_dimension=0, tiled=True)  50.3 us
    dot_general x1, matrix products, shards(): jnp.dot(lax.all_gather(attn_out, 'page', axis=0, tiled=True), out_weight,...  12.5 us
  transfers between devices with their start and end apart: 3, of which 3 were waited for; matrix products, arithmetic and copies ran while one was open for 2% of the time, Pallas kernels for 0%

profile of v1, /device:TPU:24, one launch (start us, length us, event | category | flops | bytes accessed | tf_op | source)
XLA Modules:
  0.0 329.8 jit_solution(2238288779565891503)
XLA Ops:
  6.5 1.5 pad_maximum_fusion
  8.0 0.0 all-gather.3.cloned.1.call-update
  8.0 0.0 all-gather.5.cloned.1.call-start
  8.7 0.7 compare_and_fusion
  9.4 0.1 broadcast_in_dim.63
  9.5 0.1 broadcast_in_dim.64
  9.6 1.1 copy.32
  10.7 0.7 fusion.12
  11.4 2.6 select_reduce_fusion.1
  14.1 112.4 %all-gather.3.cloned.1.call-done = bf16[128,64,256]{2,1,0:T(8,128)(2,1)} async-done(((bf16[2,64,256]{2,1,0:T(8,128)(2,1)}), bf16[128,64,256]{2,1,0:T(8,128)(2,1)}) %all-gather.3.cloned.1.call-update) | async-done | bytes 4194320 | tf_op jit(solution)/shard_map/all_gather | solution.py:31
  126.4 2.8 gather_fusion
  129.2 0.3 gather.7
  129.5 0.7 copy_select_fusion
  130.2 2.7 select_reduce_fusion
  133.0 4.9 %convert_reduce_fusion = (f32[8,256]{1,0:T(8,128)S(1)}, bf16[8,256,2048]{1,2,0:T(8,128)(2,1)S(1)}) fusion(f32[8,256]{1,0:T(8,128)S(1)} %max.9, f32[2048,8,256]{2,0,1:T(8,128)S(1)} %get-tuple-element.10, pred[2048]{0:T(1024)(128)(4,1)S(1)} %iota_compare_fusion.1), kind=kLoop, calls=%fused_computation.1 | loop fusion | flops 25163776 | bytes 25184256 | tf_op jit(solution)/shard_map/reduce_sum | solution.py:54
  137.9 1.3 fusion.3
  139.2 0.2 copy-done.1
  139.5 0.4 convert_reduce_fusion.1
  139.9 1.3 fusion.2
  141.3 0.0 all-gather.5.cloned.1.call-update
  141.3 0.2 reduce-scatter.2.cloned.1.call-start
  141.5 118.9 %all-gather.5.cloned.1.call-done = bf16[8192,1024]{0,1:T(8,128)(2,1)} async-done(((bf16[256,1024]{0,1:T(8,128)(2,1)}), bf16[8192,1024]{0,1:T(8,128)(2,1)}) %all-gather.5.cloned.1.call-update) | async-done | bytes 16777232 | tf_op jit(solution)/shard_map/all_gather | solution.py:62
  260.5 12.5 %convolution_convert_fusion = bf16[8192,256]{1,0:T(8,128)(2,1)} fusion(bf16[8192,1024]{0,1:T(8,128)(2,1)} %all-gather.5.cloned.1.call-done, bf16[1024,256]{1,0:T(8,128)(2,1)S(1)} %copy-done), kind=kOutput, calls=%fused_computation.4 | convolution fusion | flops 4297064448 | bytes 21495808 | tf_op jit(solution)/shard_map/dot_general | solution.py:61
  273.0 50.3 %reduce-scatter.2.cloned.1.call-done = bf16[2048,256]{1,0:T(8,128)(2,1)} async-done(((bf16[8192,256]{1,0:T(8,128)(2,1)}), bf16[2048,256]{1,0:T(8,128)(2,1)}) %reduce-scatter.2.cloned.1.call-update) | async-done | bytes 1048592 | tf_op jit(solution)/shard_map/reduce_scatter | solution.py:66
  (12 shorter events, 0.1 us)
Async XLA Ops:
  6.5 253.9 %copy-start = (bf16[1024,256]{1,0:T(8,128)(2,1)S(1)}, bf16[1024,256]{1,0:T(8,128)(2,1)}, u32[]{:S(2)}) copy-start(bf16[1024,256]{1,0:T(8,128)(2,1)} %param.15) | copy-start | bytes 1572868
  6.5 119.9 %all-gather.3.cloned.1.call-start = ((), (), s32[]{:S(2)}) async-start(), calls=%async_computation.1 | async-start | bytes 4259840 | tf_op jit(solution)/shard_map/all_gather | solution.py:31
  8.0 252.4 %all-gather.5.cloned.1.call-start = ((), (), s32[]{:S(2)}) async-start(), calls=%async_computation.2 | async-start | bytes 17301504 | tf_op jit(solution)/shard_map/all_gather | solution.py:62
  137.9 1.6 copy-start.1
  137.9 2.0 copy-start.2
  141.3 182.0 %reduce-scatter.2.cloned.1.call-start = ((), (), s32[]{:S(2)}) async-start(), calls=%async_computation.3 | async-start | bytes 5242880 | tf_op jit(solution)/shard_map/reduce_scatter | solution.py:66
Sparse Core Ops, SparseCore 0:
  9.2 117.1 all-gather.2
  141.4 119.0 all-gather.4
  273.1 50.1 reduce-scatter.1

commit v2 on v1

--- a/solution.py
+++ b/solution.py
@@ -2,7 +2,9 @@
 
 import jax
 import jax.numpy as jnp
+import numpy as np
 from jax import lax
+from jax.sharding import Mesh
 from jax.sharding import PartitionSpec as P
 
 HD = 128
@@ -11,6 +13,9 @@
 
 
 masked_fill = -1e30
+
+PAGE_AXES = ("y", "zl", "core")
+ROWS_AXES = ("zl", "core")
 
 
 def shards(
@@ -21,15 +26,28 @@
     kv_here = new_keys.shape[1] // HD
     group_size = heads_here // kv_here
     slot_count = block_table.shape[1]
+    pages_here = cache_keys.shape[0]
     score_scale = 1.0 / math.sqrt(HD)
+    n_head = lax.axis_size("head")
+    n_y = lax.axis_size("y")
+    n_zl = lax.axis_size("zl")
+    n_core = lax.axis_size("core")
+    n_chips = lax.axis_size("branch") * n_y * n_zl
+
+    w_group = lax.all_gather(out_weight, "y", axis=1, tiled=True)
 
     q = queries.reshape(row_count, kv_here, group_size, HD).transpose(1, 2, 0, 3)
     own_k = new_keys.reshape(row_count, kv_here, HD).transpose(1, 0, 2)
     own_v = new_values.reshape(row_count, kv_here, HD).transpose(1, 0, 2)
 
     kv_local = jnp.concatenate([cache_keys, cache_values], axis=-1)
-    kv_all = lax.all_gather(kv_local, ("branch", "page"), axis=0, tiled=True)
-    kv_sel = jnp.take(kv_all, block_table[0], axis=0)
+    kv_chips = lax.all_gather(kv_local, ("branch", "y", "zl"), axis=0, tiled=True)
+    kv_all = lax.all_gather(kv_chips, "core", axis=0, tiled=True)
+    page = block_table[0]
+    owner = page // pages_here
+    slot = page % pages_here
+    position = ((owner % n_core) * n_chips + owner // n_core) * pages_here + slot
+    kv_sel = jnp.take(kv_all, position, axis=0)
     anc_len = slot_count * PAGE_TOK
     kv_sel = kv_sel.reshape(anc_len, 2, kv_here, HD)
     anc_k = kv_sel[:, 0].transpose(1, 0, 2)
@@ -58,25 +76,35 @@
     attn = (summed / denom[..., None]).astype(jnp.bfloat16)
     attn_out = attn.transpose(2, 0, 1, 3).reshape(row_count, heads_here * HD)
 
-    partial_term = jnp.dot(
-        lax.all_gather(attn_out, "page", axis=0, tiled=True),
-        out_weight,
-        preferred_element_type=jnp.float32,
-    ).astype(jnp.bfloat16)
-    summed_out = lax.psum_scatter(partial_term, "head", scatter_dimension=0, tiled=True)
-    return summed_out
+    attn_rows = lax.all_gather(attn_out, ROWS_AXES, axis=0, tiled=True)
+    partial_term = jnp.dot(attn_rows, w_group, preferred_element_type=jnp.float32).astype(
+        jnp.bfloat16
+    )
+    summed_out = lax.psum_scatter(partial_term, "head", scatter_dimension=1, tiled=True)
+    swap = [(a * n_y + b, b * n_y + a) for a in range(n_head) for b in range(n_y)]
+    return lax.ppermute(summed_out, ("head", "y"), swap)
 
 
 def solution(mesh):
+    n_page = mesh.shape["page"]
+    devices = np.asarray(mesh.devices)
+    n_core = 2
+    n_y = 4
+    n_zl = n_page // (n_y * n_core)
+    fine = Mesh(
+        devices.reshape(mesh.shape["branch"], mesh.shape["head"], n_y, n_zl, n_core),
+        ("branch", "head") + PAGE_AXES,
+    )
+    rows = ("branch",) + PAGE_AXES
     in_specs = (
-        P(("branch", "page"), "head"),
-        P(("branch", "page"), "head"),
-        P(("branch", "page"), "head"),
-        P(("branch", "page"), None, "head"),
-        P(("branch", "page"), None, "head"),
-        P(("branch", "page"), None),
-        P(("branch", "page")),
-        P("head", "page"),
+        P(rows, "head"),
+        P(rows, "head"),
+        P(rows, "head"),
+        P(rows, None, "head"),
+        P(rows, None, "head"),
+        P(rows, None),
+        P(rows),
+        P("head", PAGE_AXES),
     )
-    out_specs = P(("branch", "head"), "page")
-    return jax.shard_map(shards, mesh=mesh, in_specs=in_specs, out_specs=out_specs, check_vma=False)
+    out_specs = P(("branch", "head"), PAGE_AXES)
+    return jax.shard_map(shards, mesh=fine, in_specs=in_specs, out_specs=out_specs, check_vma=False)

time: 331 us -> 389 us (1.18)
  waiting for transfers between devices: 282 us -> 341 us
  matrix products: 20.5 us -> 16.6 us
    ppermute x0 -> x1, waiting for transfers between devices: none -> 50 us  [shards(): return lax.ppermute(summed_out, ('head', 'y'), swap)]
    all_gather x2 -> x4, waiting for transfers between devices: 231 us -> 240 us  [the longest x1 144 us: shards(): lax.all_gather(kv_local, ('branch', 'y', 'zl'), axis=0, tiled=True)]
  transfers between devices with their start and end apart: 3 -> 6, of which waited for: 3 -> 6; matrix products, arithmetic and copies ran while one was open for 2% -> 5% of each run, Pallas kernels for 0% -> 0%
where the time goes in v2:
time: 389 us; the launch traced here: 388 us
  waiting for transfers between devices  341 us (88%)
  matrix products  16.6 us (4%)
  between operations  13.9 us (4%)
  other arithmetic  8.87 us (2%)
  local copies, waits for them, and re-layouts  5.37 us (1%)
    all_gather x1, waiting for transfers between devices, shards(): lax.all_gather(kv_local, ('branch', 'y', 'zl'), axis=0, tiled=True)  144 us
    all_gather x1, waiting for transfers between devices, shards(): attn_rows = lax.all_gather(attn_out, ROWS_AXES, axis=0, tiled=True)  56.3 us
    ppermute x1, waiting for transfers between devices, shards(): return lax.ppermute(summed_out, ('head', 'y'), swap)  50 us
    reduce_scatter x1, waiting for transfers between devices, shards(): lax.psum_scatter(partial_term, 'head', scatter_dimension=1, tiled=True)  49.9 us
    all_gather x1, waiting for transfers between devices, shards(): w_group = lax.all_gather(out_weight, 'y', axis=1, tiled=True)  24.1 us
    all_gather x1, waiting for transfers between devices, shards(): kv_all = lax.all_gather(kv_chips, 'core', axis=0, tiled=True)  15.9 us
    dot_general x1, matrix products, shards(): jnp.dot(attn_rows, w_group, preferred_element_type=jnp.float32)  9.38 us
  transfers between devices with their start and end apart: 6, of which 6 were waited for; matrix products, arithmetic and copies ran while one was open for 5% of the time, Pallas kernels for 0%

profile of v2, /device:TPU:24, one launch (start us, length us, event | category | flops | bytes accessed | tf_op | source)
XLA Modules:
  0.0 388.4 jit_solution(4264888585378731705)
XLA Ops:
  6.5 1.4 pad_maximum_fusion
  8.1 143.6 %all-gather.5.cloned.1.call-done = bf16[64,64,256]{2,1,0:T(8,128)(2,1)} async-done(((bf16[2,64,256]{2,1,0:T(8,128)(2,1)}), bf16[64,64,256]{2,1,0:T(8,128)(2,1)}) %all-gather.5.cloned.1.call-update) | async-done | bytes 2097168 | tf_op jit(solution)/shard_map/all_gather | solution.py:44
  151.7 0.7 all-gather.11.cloned.1.call-update
  152.5 0.7 fusion.18
  153.2 0.7 compare_and_fusion
  153.9 1.1 copy.32
  155.8 1.8 select_reduce_fusion.1
  157.7 15.9 %all-gather.7.cloned.1.call-done = bf16[128,64,256]{2,1,0:T(8,128)(2,1)} async-done(((bf16[64,64,256]{2,1,0:T(8,128)(2,1)}), bf16[128,64,256]{2,1,0:T(8,128)(2,1)}) %all-gather.7.cloned.1.call-update) | async-done | bytes 4194320 | tf_op jit(solution)/shard_map/all_gather | solution.py:45
  173.6 2.8 gather_fusion
  176.4 0.3 gather.7
  176.7 0.7 copy_select_fusion
  177.4 2.7 select_reduce_fusion
  180.1 0.4 convert_reduce_fusion.1
  180.6 4.9 %convert_reduce_fusion = (f32[8,256]{1,0:T(8,128)S(1)}, bf16[8,256,2048]{1,2,0:T(8,128)(2,1)S(1)}) fusion(f32[8,256]{1,0:T(8,128)S(1)} %max.9, f32[2048,8,256]{2,0,1:T(8,128)S(1)} %get-tuple-element.10, pred[2048]{0:T(1024)(128)(4,1)S(1)} %iota_compare_fusion.1), kind=kLoop, calls=%fused_computation.1 | loop fusion | flops 25163776 | bytes 25184256 | tf_op jit(solution)/shard_map/reduce_sum | solution.py:72
  185.5 1.3 fusion.3
  186.9 1.4 fusion.2
  188.2 0.2 reduce-scatter.2.cloned.1.call-start
  188.5 24.1 %all-gather.11.cloned.1.call-done = bf16[1024,1024]{1,0:T(8,128)(2,1)} async-done(((bf16[1024,256]{1,0:T(8,128)(2,1)}), bf16[1024,1024]{1,0:T(8,128)(2,1)}) %all-gather.11.cloned.1.call-update) | async-done | bytes 2097168 | tf_op jit(solution)/shard_map/all_gather | solution.py:37
  212.5 56.3 %all-gather.9.cloned.1.call-done = bf16[2048,1024]{0,1:T(8,128)(2,1)} async-done(((bf16[256,1024]{0,1:T(8,128)(2,1)}), bf16[2048,1024]{0,1:T(8,128)(2,1)}) %all-gather.9.cloned.1.call-update) | async-done | bytes 4194320 | tf_op jit(solution)/shard_map/all_gather | solution.py:79
  268.9 9.4 %convolution_convert_fusion = bf16[2048,1024]{1,0:T(8,128)(2,1)} fusion(bf16[2048,1024]{0,1:T(8,128)(2,1)} %all-gather.9.cloned.1.call-done, bf16[1024,1024]{1,0:T(8,128)(2,1)} %all-gather.11.cloned.1.call-done), kind=kOutput, calls=%fused_computation.5 | convolution fusion | flops 4297064448 | bytes 10485760 | tf_op jit(solution)/shard_map/dot_general | solution.py:80
  278.3 49.9 %reduce-scatter.2.cloned.1.call-done = bf16[2048,256]{1,0:T(8,128)(2,1)} async-done(((bf16[2048,1024]{1,0:T(8,128)(2,1)}), bf16[2048,256]{1,0:T(8,128)(2,1)}) %reduce-scatter.2.cloned.1.call-update) | async-done | bytes 1048592 | tf_op jit(solution)/shard_map/reduce_scatter | solution.py:83
  328.1 2.7 collective-permute-start
  330.8 50.0 %collective-permute-done = bf16[2048,256]{1,0:T(8,128)(2,1)S(1)} collective-permute-done((bf16[2048,256]{1,0:T(8,128)(2,1)}, bf16[2048,256]{1,0:T(8,128)(2,1)S(1)}, u32[]{:S(2)}, u32[]{:S(2)}) %collective-permute-start) | collective-permute-done | bytes 1048608 | tf_op jit(solution)/shard_map/ppermute | solution.py:85
  380.9 1.0 copy.48
  (21 shorter events, 0.4 us)
Async XLA Ops:
  6.5 149.3 %copy-start = (bf16[256,128]{1,0:T(8,128)(2,1)S(1)}, bf16[256,128]{1,0:T(8,128)(2,1)}, u32[]{:S(2)}) copy-start(bf16[256,128]{1,0:T(8,128)(2,1)} %param.9) | copy-start | bytes 196612
  6.5 145.1 %all-gather.5.cloned.1.call-start = ((), (), s32[]{:S(2)}) async-start(), calls=%async_computation.1 | async-start | bytes 2162688 | tf_op jit(solution)/shard_map/all_gather | solution.py:44
  8.0 165.6 %all-gather.7.cloned.1.call-start = ((), (), s32[]{:S(2)}) async-start(), calls=%async_computation.2 | async-start | bytes 6291456 | tf_op jit(solution)/shard_map/all_gather | solution.py:45
  151.7 60.9 %all-gather.11.cloned.1.call-start = ((), (), s32[]{:S(2)}) async-start(), calls=%async_computation.4 | async-start | bytes 2621440 | tf_op jit(solution)/shard_map/all_gather | solution.py:37
  152.4 116.4 %all-gather.9.cloned.1.call-start = ((), (), s32[]{:S(2)}) async-start(), calls=%async_computation.3 | async-start | bytes 4718592 | tf_op jit(solution)/shard_map/all_gather | solution.py:79
  177.4 2.8 copy-start.1
  185.5 1.3 copy-start.2
  188.2 139.9 %reduce-scatter.2.cloned.1.call-start = ((), (), s32[]{:S(2)}) async-start(), calls=%async_computation.5 | async-start | bytes 5242880 | tf_op jit(solution)/shard_map/reduce_scatter | solution.py:83
  328.1 52.7 %collective-permute-start = (bf16[2048,256]{1,0:T(8,128)(2,1)}, bf16[2048,256]{1,0:T(8,128)(2,1)S(1)}, u32[]{:S(2)}, u32[]{:S(2)}) collective-permute-start(bf16[2048,256]{1,0:T(8,128)(2,1)} %reduce-scatter.2.cloned.1.call-done), channel_id=1, source_target_pairs={{0,0},{8,32},{16,64},{24,96},{32,8},{40,40},{48,72},{56,104},{64,1... | collective-permute-start | bytes 3145736 | tf_op jit(solution)/shard_map/ppermute | solution.py:85
Sparse Core Ops, SparseCore 0:
  9.1 142.4 all-gather.4
  153.4 20.0 all-gather.6
  175.4 37.1 all-gather.10
  214.1 54.6 all-gather.8
  278.4 49.7 reduce-scatter.1

commit v3 on v2

--- a/solution.py
+++ b/solution.py
@@ -2,10 +2,10 @@
 
 import jax
 import jax.numpy as jnp
-import numpy as np
 from jax import lax
 from jax.sharding import Mesh
 from jax.sharding import PartitionSpec as P
+import numpy as np
 
 HD = 128
 PAGE_TOK = 64
@@ -13,9 +13,6 @@
 
 
 masked_fill = -1e30
-
-PAGE_AXES = ("y", "zl", "core")
-ROWS_AXES = ("zl", "core")
 
 
 def shards(
@@ -26,28 +23,15 @@
     kv_here = new_keys.shape[1] // HD
     group_size = heads_here // kv_here
     slot_count = block_table.shape[1]
-    pages_here = cache_keys.shape[0]
     score_scale = 1.0 / math.sqrt(HD)
-    n_head = lax.axis_size("head")
-    n_y = lax.axis_size("y")
-    n_zl = lax.axis_size("zl")
-    n_core = lax.axis_size("core")
-    n_chips = lax.axis_size("branch") * n_y * n_zl
-
-    w_group = lax.all_gather(out_weight, "y", axis=1, tiled=True)
 
     q = queries.reshape(row_count, kv_here, group_size, HD).transpose(1, 2, 0, 3)
     own_k = new_keys.reshape(row_count, kv_here, HD).transpose(1, 0, 2)
     own_v = new_values.reshape(row_count, kv_here, HD).transpose(1, 0, 2)
 
     kv_local = jnp.concatenate([cache_keys, cache_values], axis=-1)
-    kv_chips = lax.all_gather(kv_local, ("branch", "y", "zl"), axis=0, tiled=True)
-    kv_all = lax.all_gather(kv_chips, "core", axis=0, tiled=True)
-    page = block_table[0]
-    owner = page // pages_here
-    slot = page % pages_here
-    position = ((owner % n_core) * n_chips + owner // n_core) * pages_here + slot
-    kv_sel = jnp.take(kv_all, position, axis=0)
+    kv_all = lax.all_gather(kv_local, ("branch",) + PAGE_AXES, axis=0, tiled=True)
+    kv_sel = jnp.take(kv_all, block_table[0], axis=0)
     anc_len = slot_count * PAGE_TOK
     kv_sel = kv_sel.reshape(anc_len, 2, kv_here, HD)
     anc_k = kv_sel[:, 0].transpose(1, 0, 2)
@@ -76,23 +60,33 @@
     attn = (summed / denom[..., None]).astype(jnp.bfloat16)
     attn_out = attn.transpose(2, 0, 1, 3).reshape(row_count, heads_here * HD)
 
-    attn_rows = lax.all_gather(attn_out, ROWS_AXES, axis=0, tiled=True)
-    partial_term = jnp.dot(attn_rows, w_group, preferred_element_type=jnp.float32).astype(
-        jnp.bfloat16
-    )
-    summed_out = lax.psum_scatter(partial_term, "head", scatter_dimension=1, tiled=True)
-    swap = [(a * n_y + b, b * n_y + a) for a in range(n_head) for b in range(n_y)]
-    return lax.ppermute(summed_out, ("head", "y"), swap)
+    n_y = lax.axis_size("y")
+    n_zl = lax.axis_size("zl")
+    n_core = lax.axis_size("core")
+    attn_chips = lax.all_gather(attn_out, ("y", "zl"), axis=0, tiled=True)
+    attn_all = lax.all_gather(attn_chips, "core", axis=0, tiled=True)
+    attn_all = attn_all.reshape(n_core, n_y, n_zl * row_count, attn_all.shape[1])
+    partial_term = jnp.einsum(
+        "cyrk,kf->ycrf", attn_all, out_weight, preferred_element_type=jnp.float32
+    ).astype(jnp.bfloat16)
+    cols = partial_term.shape[-1]
+    partial_term = partial_term.reshape(-1, cols)
+    summed_out = lax.psum_scatter(partial_term, "head", scatter_dimension=0, tiled=True)
+    summed_out = summed_out.reshape(n_core, n_zl, row_count, cols).transpose(1, 0, 2, 3)
+    return summed_out.reshape(n_zl * n_core * row_count, cols)
+
+
+PAGE_AXES = ("y", "zl", "core")
 
 
 def solution(mesh):
     n_page = mesh.shape["page"]
-    devices = np.asarray(mesh.devices)
     n_core = 2
     n_y = 4
-    n_zl = n_page // (n_y * n_core)
     fine = Mesh(
-        devices.reshape(mesh.shape["branch"], mesh.shape["head"], n_y, n_zl, n_core),
+        np.asarray(mesh.devices).reshape(
+            mesh.shape["branch"], mesh.shape["head"], n_y, n_page // (n_y * n_core), n_core
+        ),
         ("branch", "head") + PAGE_AXES,
     )
     rows = ("branch",) + PAGE_AXES

time: 389 us -> 458 us (1.18)
  waiting for transfers between devices: 341 us -> 383 us
  local copies, waits for them, and re-layouts: 5.37 us -> 31.5 us
    all_gather x4 -> x3, waiting for transfers between devices: 240 us -> 332 us  [the longest x1 185 us: shards(): attn_chips = lax.all_gather(attn_out, ('y', 'zl'), axis=0, tiled=True)]
    ppermute x1 -> x0, waiting for transfers between devices: 50 us -> none  [shards(): return lax.ppermute(summed_out, ('head', 'y'), swap)]
    all_gather x0 -> x1, local copies, waits for them, and re-layouts: none -> 22.4 us  [shards(): attn_all = lax.all_gather(attn_chips, 'core', axis=0, tiled=True)]
  transfers between devices with their start and end apart: 6 -> 4, of which waited for: 6 -> 4; matrix products, arithmetic and copies ran while one was open for 5% -> 1% of each run, Pallas kernels for 0% -> 0%
where the time goes in v3:
time: 458 us; the launch traced here: 456 us
  waiting for transfers between devices  383 us (84%)
  local copies, waits for them, and re-layouts  31.5 us (7%)
  matrix products  18.3 us (4%)
  between operations  13.9 us (3%)
  other arithmetic  8.85 us (2%)
    all_gather x1, waiting for transfers between devices, shards(): attn_chips = lax.all_gather(attn_out, ('y', 'zl'), axis=0, tiled=True)  185 us
    all_gather x1, waiting for transfers between devices, shards(): lax.all_gather(kv_local, ('branch',) + PAGE_AXES, axis=0, tiled=True)  112 us
    reduce_scatter x1, waiting for transfers between devices, shards(): lax.psum_scatter(partial_term, 'head', scatter_dimension=0, tiled=True)  50.8 us
    all_gather x1, waiting for transfers between devices, shards(): attn_all = lax.all_gather(attn_chips, 'core', axis=0, tiled=True)  34.6 us
    all_gather x1, local copies, waits for them, and re-layouts, shards(): attn_all = lax.all_gather(attn_chips, 'core', axis=0, tiled=True)  22.4 us
    dot_general x1, matrix products, shards(): jnp.einsum('cyrk,kf->ycrf', attn_all, out_weight, preferred_element_type=...  10.3 us
  transfers between devices with their start and end apart: 4, of which 4 were waited for; matrix products, arithmetic and copies ran while one was open for 1% of the time, Pallas kernels for 0%

profile of v3, /device:TPU:24, one launch (start us, length us, event | category | flops | bytes accessed | tf_op | source)
XLA Modules:
  0.0 456.1 jit_solution(12174638787259535330)
XLA Ops:
  6.5 1.5 pad_maximum_fusion
  8.7 0.7 compare_and_fusion
  9.5 0.1 broadcast_in_dim.64
  9.6 1.1 copy.48
  10.7 0.7 fusion.13
  11.4 2.6 select_reduce_fusion.1
  14.0 112.4 %all-gather.4.cloned.1.call-done = bf16[128,64,256]{2,1,0:T(8,128)(2,1)} async-done(((bf16[2,64,256]{2,1,0:T(8,128)(2,1)}), bf16[128,64,256]{2,1,0:T(8,128)(2,1)}) %all-gather.4.cloned.1.call-update) | async-done | bytes 4194320 | tf_op jit(solution)/shard_map/all_gather | solution.py:33
  126.4 2.8 gather_fusion
  129.2 0.3 gather.7
  129.5 0.7 copy_select_fusion
  130.2 2.8 select_reduce_fusion
  133.0 4.9 %convert_reduce_fusion = (f32[8,256]{1,0:T(8,128)S(1)}, bf16[8,256,2048]{1,2,0:T(8,128)(2,1)S(1)}) fusion(f32[8,256]{1,0:T(8,128)S(1)} %max.9, f32[2048,8,256]{2,0,1:T(8,128)S(1)} %get-tuple-element.10, pred[2048]{0:T(1024)(128)(4,1)S(1)} %iota_compare_fusion.1), kind=kLoop, calls=%fused_computation.1 | loop fusion | flops 25163776 | bytes 25184256 | tf_op jit(solution)/shard_map/reduce_sum | solution.py:56
  137.9 1.3 fusion.3
  139.2 0.2 copy-done.1
  139.5 0.4 convert_reduce_fusion.1
  139.9 1.3 fusion.2
  141.4 185.4 %all-gather.6.cloned.1.call-done = bf16[4096,1024]{0,1:T(8,128)(2,1)} async-done(((bf16[256,1024]{0,1:T(8,128)(2,1)}), bf16[4096,1024]{0,1:T(8,128)(2,1)}) %all-gather.6.cloned.1.call-update) | async-done | bytes 8388624 | tf_op jit(solution)/shard_map/all_gather | solution.py:66
  326.8 0.2 reduce-scatter.2.cloned.1.call-start
  327.0 34.6 %all-gather.8.cloned.1.call-done = bf16[8192,1024]{0,1:T(8,128)(2,1)} async-done(((bf16[4096,1024]{0,1:T(8,128)(2,1)}), bf16[8192,1024]{0,1:T(8,128)(2,1)}) %all-gather.8.cloned.1.call-update) | async-done | bytes 16777232 | tf_op jit(solution)/shard_map/all_gather | solution.py:67
  361.6 22.4 %copy.38 = bf16[8192,1024]{1,0:T(8,128)(2,1)} copy(bf16[8192,1024]{0,1:T(8,128)(2,1)} %all-gather.8.cloned.1.call-done) | data formatting | bytes 33554432 | tf_op jit(solution)/shard_map/all_gather | solution.py:67
  383.9 10.3 %convert_bitcast_fusion = bf16[4,2,1024,256]{3,2,0,1:T(8,128)(2,1)S(1)} fusion(bf16[2,4,1024,1024]{3,2,1,0:T(8,128)(2,1)} %bitcast.66, bf16[1024,256]{1,0:T(8,128)(2,1)S(1)} %copy-done), kind=kOutput, calls=%fused_computation.5 | convolution fusion | flops 4297064448 | bytes 21495808 | tf_op jit(solution)/shard_map/cyrk,kf->ycrf/dot_general | solution.py:69
  394.3 2.2 copy.39
  396.5 50.8 %reduce-scatter.2.cloned.1.call-done = bf16[2048,256]{1,0:T(8,128)(2,1)} async-done(((bf16[8192,256]{1,0:T(8,128)(2,1)}), bf16[2048,256]{1,0:T(8,128)(2,1)}) %reduce-scatter.2.cloned.1.call-update) | async-done | bytes 1048592 | tf_op jit(solution)/shard_map/reduce_scatter | solution.py:74
  447.3 2.3 copy.40
  (18 shorter events, 0.3 us)
Async XLA Ops:
  6.5 377.4 %copy-start = (bf16[1024,256]{1,0:T(8,128)(2,1)S(1)}, bf16[1024,256]{1,0:T(8,128)(2,1)}, u32[]{:S(2)}) copy-start(bf16[1024,256]{1,0:T(8,128)(2,1)} %param.15) | copy-start | bytes 1572868
  6.5 119.9 %all-gather.4.cloned.1.call-start = ((), (), s32[]{:S(2)}) async-start(), calls=%async_computation.1 | async-start | bytes 4259840 | tf_op jit(solution)/shard_map/all_gather | solution.py:33
  8.0 318.7 %all-gather.6.cloned.1.call-start = ((), (), s32[]{:S(2)}) async-start(), calls=%async_computation.2 | async-start | bytes 8912896 | tf_op jit(solution)/shard_map/all_gather | solution.py:66
  137.9 1.6 copy-start.1
  137.9 2.0 copy-start.2
  141.3 220.2 %all-gather.8.cloned.1.call-start = ((), (), s32[]{:S(2)}) async-start(), calls=%async_computation.3 | async-start | bytes 25165824 | tf_op jit(solution)/shard_map/all_gather | solution.py:67
  326.8 120.5 %reduce-scatter.2.cloned.1.call-start = ((), (), s32[]{:S(2)}) async-start(), calls=%async_computation.4 | async-start | bytes 5242880 | tf_op jit(solution)/shard_map/reduce_scatter | solution.py:74
Sparse Core Ops, SparseCore 0:
  9.2 117.1 all-gather.3
  141.4 185.2 all-gather.5
  328.6 32.9 all-gather.7
  396.6 50.6 reduce-scatter.1

commit v4 on v1

--- a/solution.py
+++ b/solution.py
@@ -58,13 +58,24 @@
     attn = (summed / denom[..., None]).astype(jnp.bfloat16)
     attn_out = attn.transpose(2, 0, 1, 3).reshape(row_count, heads_here * HD)
 
-    partial_term = jnp.dot(
-        lax.all_gather(attn_out, "page", axis=0, tiled=True),
-        out_weight,
-        preferred_element_type=jnp.float32,
-    ).astype(jnp.bfloat16)
-    summed_out = lax.psum_scatter(partial_term, "head", scatter_dimension=0, tiled=True)
-    return summed_out
+    n_head = lax.axis_size("head")
+    chunk = row_count // CHUNKS
+    pieces = []
+    for index in range(CHUNKS):
+        rows_here = attn_out[index * chunk:(index + 1) * chunk]
+        gathered = lax.all_gather(rows_here, "page", axis=0, tiled=True)
+        partial_term = jnp.dot(gathered, out_weight, preferred_element_type=jnp.float32).astype(
+            jnp.bfloat16
+        )
+        cols = partial_term.shape[1]
+        partial_term = partial_term.reshape(n_head, -1, cols)
+        arrived = lax.all_to_all(partial_term, "head", 0, 0, tiled=True)
+        pieces.append(jnp.sum(arrived.astype(jnp.float32), axis=0).astype(jnp.bfloat16))
+    out = jnp.stack(pieces).reshape(CHUNKS, -1, chunk, pieces[0].shape[-1])
+    return out.transpose(1, 0, 2, 3).reshape(-1, out.shape[-1])
+
+
+CHUNKS = 4
 
 
 def solution(mesh):

time: 331 us -> 429 us (1.30)
  waiting for transfers between devices: 282 us -> 348 us
  starting transfers between devices: 0.27 us -> 17.5 us
  matrix products: 20.5 us -> 26.4 us
  other arithmetic: 8.85 us -> 13.4 us
    all_gather x1 -> x4, waiting for transfers between devices: 119 us -> 222 us  [shards(): gathered = lax.all_gather(rows_here, 'page', axis=0, tiled=True)]
    reduce_scatter x1 -> x0, waiting for transfers between devices: 50.3 us -> none  [shards(): lax.psum_scatter(partial_term, 'head', scatter_dimension=0, tiled=True)]
    all_to_all x0 -> x4, starting transfers between devices: none -> 17.3 us  [shards(): arrived = lax.all_to_all(partial_term, 'head', 0, 0, tiled=True)]
    all_to_all x0 -> x4, waiting for transfers between devices: none -> 13.7 us  [shards(): arrived = lax.all_to_all(partial_term, 'head', 0, 0, tiled=True)]
    dot_general x1 -> x4, matrix products: 12.5 us -> 17.7 us  [shards(): jnp.dot(gathered, out_weight, preferred_element_type=jnp.float32)]
  transfers between devices with their start and end apart: 3 -> 9, of which waited for: 3 -> 6; matrix products, arithmetic and copies ran while one was open for 2% -> 6% of each run, Pallas kernels for 0% -> 0%
where the time goes in v4:
time: 429 us; the launch traced here: 427 us
  waiting for transfers between devices  348 us (81%)
  matrix products  26.4 us (6%)
  starting transfers between devices  17.5 us (4%)
  between operations  14 us (3%)
  other arithmetic  13.4 us (3%)
  local copies, waits for them, and re-layouts  7.53 us (2%)
    all_gather x4, waiting for transfers between devices, shards(): gathered = lax.all_gather(rows_here, 'page', axis=0, tiled=True)  222 us
    all_gather x1, waiting for transfers between devices, shards(): kv_all = lax.all_gather(kv_local, ('branch', 'page'), axis=0, tiled=True)  112 us
    dot_general x4, matrix products, shards(): jnp.dot(gathered, out_weight, preferred_element_type=jnp.float32)  17.7 us
    all_to_all x4, starting transfers between devices, shards(): arrived = lax.all_to_all(partial_term, 'head', 0, 0, tiled=True)  17.3 us
    all_to_all x4, waiting for transfers between devices, shards(): arrived = lax.all_to_all(partial_term, 'head', 0, 0, tiled=True)  13.7 us
  transfers between devices with their start and end apart: 9, of which 6 were waited for; matrix products, arithmetic and copies ran while one was open for 6% of the time, Pallas kernels for 0%

profile of v4, /device:TPU:24, one launch (start us, length us, event | category | flops | bytes accessed | tf_op | source)
XLA Modules:
  0.0 426.7 jit_solution(6707926422451223846)
XLA Ops:
  6.5 1.5 pad_maximum_fusion.1
  9.6 1.1 copy.30
  11.4 2.6 select_reduce_fusion.1
  14.0 112.4 %all-gather.6.cloned.1.call-done = bf16[128,64,256]{2,1,0:T(8,128)(2,1)} async-done(((bf16[2,64,256]{2,1,0:T(8,128)(2,1)}), bf16[128,64,256]{2,1,0:T(8,128)(2,1)}) %all-gather.6.cloned.1.call-update) | async-done | bytes 4194320 | tf_op jit(solution)/shard_map/all_gather | solution.py:31
  126.4 2.8 gather_fusion
  130.2 2.8 select_reduce_fusion
  133.0 4.9 %convert_reduce_fusion = (f32[8,256]{1,0:T(8,128)S(1)}, bf16[8,256,2048]{1,2,0:T(8,128)(2,1)S(1)}) fusion(f32[8,256]{1,0:T(8,128)S(1)} %max.9, f32[2048,8,256]{2,0,1:T(8,128)S(1)} %get-tuple-element.14, pred[2048]{0:T(1024)(128)(4,1)S(1)} %iota_compare_fusion.1), kind=kLoop, calls=%fused_computation.1 | loop fusion | flops 25163776 | bytes 25184256 | tf_op jit(solution)/shard_map/reduce_sum | solution.py:54
  137.9 2.4 fusion.4
  145.0 58.8 %all-gather.8.cloned.1.call-done = bf16[2048,1024]{1,0:T(8,128)(2,1)} async-done(((bf16[64,1024]{1,0:T(8,128)(2,1)}), bf16[2048,1024]{1,0:T(8,128)(2,1)}) %all-gather.8.cloned.1.call-update) | async-done | bytes 4194320 | tf_op jit(solution)/shard_map/all_gather | solution.py:66
  203.8 4.4 %convolution_convert_fusion.3 = bf16[2048,256]{1,0:T(8,128)(2,1)} fusion(bf16[2048,1024]{1,0:T(8,128)(2,1)} %all-gather.8.cloned.1.call-done, bf16[1024,256]{1,0:T(8,128)(2,1)S(1)} %copy-done), kind=kOutput, calls=%fused_computation.8 | convolution fusion | flops 1074266112 | bytes 5767168 | tf_op jit(solution)/shard_map/dot_general | solution.py:67
  208.2 4.3 all-to-all-start
  212.5 54.3 %all-gather.14.cloned.1.call-done = bf16[2048,1024]{1,0:T(8,128)(2,1)} async-done(((bf16[64,1024]{1,0:T(8,128)(2,1)}), bf16[2048,1024]{1,0:T(8,128)(2,1)}) %all-gather.14.cloned.1.call-update) | async-done | bytes 4194320 | tf_op jit(solution)/shard_map/all_gather | solution.py:66
  266.8 4.4 %convolution_convert_fusion = bf16[2048,256]{1,0:T(8,128)(2,1)} fusion(bf16[2048,1024]{1,0:T(8,128)(2,1)} %all-gather.14.cloned.1.call-done, bf16[1024,256]{1,0:T(8,128)(2,1)S(1)} %copy-done), kind=kOutput, calls=%fused_computation.5 | convolution fusion | flops 1074266112 | bytes 5767168 | tf_op jit(solution)/shard_map/dot_general | solution.py:67
  271.2 4.2 all-to-all-start.3
  275.4 54.4 %all-gather.12.cloned.1.call-done = bf16[2048,1024]{1,0:T(8,128)(2,1)} async-done(((bf16[64,1024]{1,0:T(8,128)(2,1)}), bf16[2048,1024]{1,0:T(8,128)(2,1)}) %all-gather.12.cloned.1.call-update) | async-done | bytes 4194320 | tf_op jit(solution)/shard_map/all_gather | solution.py:66
  329.8 4.5 %convolution_convert_fusion.1 = bf16[2048,256]{1,0:T(8,128)(2,1)} fusion(bf16[2048,1024]{1,0:T(8,128)(2,1)} %all-gather.12.cloned.1.call-done, bf16[1024,256]{1,0:T(8,128)(2,1)S(1)} %copy-done), kind=kOutput, calls=%fused_computation.6 | convolution fusion | flops 1074266112 | bytes 5767168 | tf_op jit(solution)/shard_map/dot_general | solution.py:67
  334.3 4.5 %all-to-all-start.2 = ((bf16[4,512,256]{2,1,0:T(8,128)(2,1)}), bf16[4,512,256]{2,1,0:T(8,128)(2,1)}, u32[]{:S(2)}, u32[]{:S(2)}) async-start(bf16[4,512,256]{2,1,0:T(8,128)(2,1)} %bitcast.97), calls=%async_computation.2 | async-start | bytes 2097152 | tf_op jit(solution)/shard_map/all_to_all | solution.py:72
  338.8 54.3 %all-gather.10.cloned.1.call-done = bf16[2048,1024]{1,0:T(8,128)(2,1)} async-done(((bf16[64,1024]{1,0:T(8,128)(2,1)}), bf16[2048,1024]{1,0:T(8,128)(2,1)}) %all-gather.10.cloned.1.call-update) | async-done | bytes 4194320 | tf_op jit(solution)/shard_map/all_gather | solution.py:66
  393.1 4.4 %convolution_convert_fusion.2 = bf16[2048,256]{1,0:T(8,128)(2,1)} fusion(bf16[2048,1024]{1,0:T(8,128)(2,1)} %all-gather.10.cloned.1.call-done, bf16[1024,256]{1,0:T(8,128)(2,1)S(1)} %copy-done), kind=kOutput, calls=%fused_computation.7 | convolution fusion | flops 1074266112 | bytes 5767168 | tf_op jit(solution)/shard_map/dot_general | solution.py:67
  397.5 4.4 %all-to-all-start.1 = ((bf16[4,512,256]{2,1,0:T(8,128)(2,1)}), bf16[4,512,256]{2,1,0:T(8,128)(2,1)}, u32[]{:S(2)}, u32[]{:S(2)}) async-start(bf16[4,512,256]{2,1,0:T(8,128)(2,1)} %bitcast.98), calls=%async_computation.1 | async-start | bytes 2097152 | tf_op jit(solution)/shard_map/all_to_all | solution.py:72
  402.4 1.5 reduce_sum.70
  403.9 13.7 %all-to-all-done.1 = bf16[4,512,256]{2,1,0:T(8,128)(2,1)} async-done(((bf16[4,512,256]{2,1,0:T(8,128)(2,1)}), bf16[4,512,256]{2,1,0:T(8,128)(2,1)}, u32[]{:S(2)}, u32[]{:S(2)}) %all-to-all-start.1) | async-done | bytes 1048608 | tf_op jit(solution)/shard_map/all_to_all | solution.py:72
  417.6 1.5 reduce_sum.69
  419.0 1.1 pad_maximum_fusion
  (43 shorter events, 7.7 us)
Async XLA Ops:
  6.5 197.3 %copy-start = (bf16[1024,256]{1,0:T(8,128)(2,1)S(1)}, bf16[1024,256]{1,0:T(8,128)(2,1)}, u32[]{:S(2)}) copy-start(bf16[1024,256]{1,0:T(8,128)(2,1)} %param.15) | copy-start | bytes 1572868
  6.5 119.9 %all-gather.6.cloned.1.call-start = ((), (), s32[]{:S(2)}) async-start(), calls=%async_computation.4 | async-start | bytes 4259840 | tf_op jit(solution)/shard_map/all_gather | solution.py:31
  8.0 195.8 %all-gather.8.cloned.1.call-start = ((), (), s32[]{:S(2)}) async-start(), calls=%async_computation.5 | async-start | bytes 4325376 | tf_op jit(solution)/shard_map/all_gather | solution.py:66
  137.9 2.5 copy-start.1
  137.9 2.9 copy-start.2
  142.5 124.3 %all-gather.14.cloned.1.call-start = ((), (), s32[]{:S(2)}) async-start(), calls=%async_computation.8 | async-start | bytes 4325376 | tf_op jit(solution)/shard_map/all_gather | solution.py:66
  143.3 186.5 %all-gather.12.cloned.1.call-start = ((), (), s32[]{:S(2)}) async-start(), calls=%async_computation.7 | async-start | bytes 4325376 | tf_op jit(solution)/shard_map/all_gather | solution.py:66
  144.2 248.9 %all-gather.10.cloned.1.call-start = ((), (), s32[]{:S(2)}) async-start(), calls=%async_computation.6 | async-start | bytes 4325376 | tf_op jit(solution)/shard_map/all_gather | solution.py:66
  208.2 63.0 %all-to-all-start = ((bf16[4,512,256]{2,1,0:T(8,128)(2,1)}), bf16[4,512,256]{2,1,0:T(8,128)(2,1)S(1)}, u32[]{:S(2)}, u32[]{:S(2)}) async-start(bf16[4,512,256]{2,1,0:T(8,128)(2,1)} %bitcast.16), calls=%async_computation | async-start | bytes 2097152 | tf_op jit(solution)/shard_map/all_to_all | solution.py:72
  271.2 63.1 %all-to-all-start.3 = ((bf16[4,512,256]{2,1,0:T(8,128)(2,1)}), bf16[4,512,256]{2,1,0:T(8,128)(2,1)S(1)}, u32[]{:S(2)}, u32[]{:S(2)}) async-start(bf16[4,512,256]{2,1,0:T(8,128)(2,1)} %bitcast.96), calls=%async_computation.3 | async-start | bytes 2097152 | tf_op jit(solution)/shard_map/all_to_all | solution.py:72
  334.3 63.2 %all-to-all-start.2 = ((bf16[4,512,256]{2,1,0:T(8,128)(2,1)}), bf16[4,512,256]{2,1,0:T(8,128)(2,1)}, u32[]{:S(2)}, u32[]{:S(2)}) async-start(bf16[4,512,256]{2,1,0:T(8,128)(2,1)} %bitcast.97), calls=%async_computation.2 | async-start | bytes 2097152 | tf_op jit(solution)/shard_map/all_to_all | solution.py:72
  397.5 20.1 %all-to-all-start.1 = ((bf16[4,512,256]{2,1,0:T(8,128)(2,1)}), bf16[4,512,256]{2,1,0:T(8,128)(2,1)}, u32[]{:S(2)}, u32[]{:S(2)}) async-start(bf16[4,512,256]{2,1,0:T(8,128)(2,1)} %bitcast.98), calls=%async_computation.1 | async-start | bytes 2097152 | tf_op jit(solution)/shard_map/all_to_all | solution.py:72
Sparse Core Ops, SparseCore 0:
  9.2 117.1 all-gather.5
  142.6 61.1 all-gather.7
  205.7 61.0 all-gather.13
  268.5 61.3 all-gather.11
  331.6 61.4 all-gather.9

commit v5 on v1

--- a/solution.py
+++ b/solution.py
@@ -28,7 +28,7 @@
     own_v = new_values.reshape(row_count, kv_here, HD).transpose(1, 0, 2)
 
     kv_local = jnp.concatenate([cache_keys, cache_values], axis=-1)
-    kv_all = lax.all_gather(kv_local, ("branch", "page"), axis=0, tiled=True)
+    kv_all = gather_by_all_to_all(kv_local, ("branch", "page"))
     kv_sel = jnp.take(kv_all, block_table[0], axis=0)
     anc_len = slot_count * PAGE_TOK
     kv_sel = kv_sel.reshape(anc_len, 2, kv_here, HD)
@@ -58,13 +58,20 @@
     attn = (summed / denom[..., None]).astype(jnp.bfloat16)
     attn_out = attn.transpose(2, 0, 1, 3).reshape(row_count, heads_here * HD)
 
+    n_head = lax.axis_size("head")
     partial_term = jnp.dot(
-        lax.all_gather(attn_out, "page", axis=0, tiled=True),
-        out_weight,
-        preferred_element_type=jnp.float32,
+        gather_by_all_to_all(attn_out, "page"), out_weight, preferred_element_type=jnp.float32
     ).astype(jnp.bfloat16)
-    summed_out = lax.psum_scatter(partial_term, "head", scatter_dimension=0, tiled=True)
-    return summed_out
+    cols = partial_term.shape[1]
+    arrived = lax.all_to_all(partial_term.reshape(n_head, -1, cols), "head", 0, 0, tiled=True)
+    return jnp.sum(arrived.astype(jnp.float32), axis=0).astype(jnp.bfloat16)
+
+
+def gather_by_all_to_all(x, axes):
+    count = lax.axis_size(axes)
+    spread = jnp.broadcast_to(x[None], (count,) + x.shape)
+    arrived = lax.all_to_all(spread, axes, 0, 0, tiled=True)
+    return arrived.reshape((count * x.shape[0],) + x.shape[1:])
 
 
 def solution(mesh):

time: 331 us -> 561 us (1.69)
  blocking collectives: 0 us -> 421 us
  waiting for transfers between devices: 282 us -> 93.3 us
  between operations: 13.9 us -> 0.85 us
  starting transfers between devices: 0.27 us -> 12.2 us
  matrix products: 20.5 us -> 11.2 us
    all_to_all x0 -> x2, blocking collectives: none -> 421 us  [the longest x1 367 us: gather_by_all_to_all(): arrived = lax.all_to_all(spread, axes, 0, 0, tiled=True)]
    all_gather x2 -> x0, waiting for transfers between devices: 231 us -> none  [the longest x1 119 us: shards(): lax.all_gather(attn_out, 'page', axis=0, tiled=True)]
    all_to_all x0 -> x1, waiting for transfers between devices: none -> 93.3 us  [gather_by_all_to_all(): arrived = lax.all_to_all(spread, axes, 0, 0, tiled=True)]
    reduce_scatter x1 -> x0, waiting for transfers between devices: 50.3 us -> none  [shards(): lax.psum_scatter(partial_term, 'head', scatter_dimension=0, tiled=True)]
    all_to_all x0 -> x1, starting transfers between devices: none -> 12.2 us  [gather_by_all_to_all(): arrived = lax.all_to_all(spread, axes, 0, 0, tiled=True)]
    dot_general x1, matrix products: 12.5 us -> 4.71 us  [shards(): jnp.dot(gather_by_all_to_all(attn_out, 'page'), out_weight, preferred_ele...]
  transfers between devices with their start and end apart: 3 -> 1, of which waited for: 3 -> 1; matrix products, arithmetic and copies ran while one was open for 2% -> 0% of each run, Pallas kernels for 0% -> 0%
where the time goes in v5:
time: 561 us; the launch traced here: 558 us
  blocking collectives  421 us (75%)
  waiting for transfers between devices  93.3 us (17%)
  starting transfers between devices  12.2 us (2%)
  matrix products  11.2 us (2%)
  other arithmetic  11 us (2%)
  local copies, waits for them, and re-layouts  8.48 us (2%)
    all_to_all x1, blocking collectives, gather_by_all_to_all(): arrived = lax.all_to_all(spread, axes, 0, 0, tiled=True)  367 us
    all_to_all x1, waiting for transfers between devices, gather_by_all_to_all(): arrived = lax.all_to_all(spread, axes, 0, 0, tiled=True)  93.3 us
    all_to_all x1, blocking collectives, shards(): lax.all_to_all(partial_term.reshape(n_head, -1, cols), 'head', 0, 0, tile...  53.8 us
    all_to_all x1, starting transfers between devices, gather_by_all_to_all(): arrived = lax.all_to_all(spread, axes, 0, 0, tiled=True)  12.2 us
  transfers between devices with their start and end apart: 1, of which 1 were waited for; matrix products, arithmetic and copies ran while one was open for 0% of the time, Pallas kernels for 0%

profile of v5, /device:TPU:24, one launch (start us, length us, event | category | flops | bytes accessed | tf_op | source)
XLA Modules:
  0.0 558.2 jit_solution(227054589245767262)
XLA Ops:
  0.0 0.8 pad_maximum_fusion
  0.8 2.5 broadcast_in_dim.79
  3.3 12.2 %all-to-all-start = ((bf16[64,2,64,256]{3,2,1,0:T(8,128)(2,1)}), bf16[64,2,64,256]{3,2,1,0:T(8,128)(2,1)}, u32[]{:S(2)}, u32[]{:S(2)}) async-start(bf16[64,2,64,256]{3,2,1,0:T(8,128)(2,1)} %broadcast_in_dim.79), calls=%async_computation | async-start | bytes 8388608 | tf_op jit(solution)/shard_map/all_to_all | solution.py:73
  16.3 0.1 broadcast_in_dim.76
  16.3 0.1 broadcast_in_dim.77
  16.4 0.1 copy.28
  16.6 1.9 select_reduce_fusion.1
  18.5 93.3 %all-to-all-done = bf16[64,2,64,256]{3,2,1,0:T(8,128)(2,1)} async-done(((bf16[64,2,64,256]{3,2,1,0:T(8,128)(2,1)}), bf16[64,2,64,256]{3,2,1,0:T(8,128)(2,1)}, u32[]{:S(2)}, u32[]{:S(2)}) %all-to-all-start) | async-done | bytes 4194336 | tf_op jit(solution)/shard_map/all_to_all | solution.py:73
  111.8 2.8 gather_fusion
  114.6 0.3 gather.7
  114.9 0.7 copy_select_fusion
  115.5 2.7 select_reduce_fusion
  118.3 4.9 convert_reduce_fusion
  123.2 0.0 copy-start.4
  123.2 1.3 fusion.3
  124.6 0.2 copy-done.1
  124.8 0.4 convert_reduce_fusion.1
  125.3 0.5 fusion.2
  125.8 0.2 copy.21
  126.0 2.2 broadcast_in_dim.85
  128.2 367.5 %all_to_all.15 = bf16[32,256,1024]{2,1,0:T(8,128)(2,1)S(1)} all-to-all(bf16[32,256,1024]{2,1,0:T(8,128)(2,1)S(1)} %broadcast_in_dim.85), channel_id=1, replica_groups=mesh['branch'=2,'head'=4,'page'=32] {'page'}, dimensions={0} | all-to-all | bytes 33554432 | tf_op jit(solution)/shard_map/all_to_all | solution.py:73
  495.7 4.7 convolution_convert_fusion
  500.4 53.8 %all_to_all.16 = bf16[4,2048,256]{2,1,0:T(8,128)(2,1)} all-to-all(bf16[4,2048,256]{2,1,0:T(8,128)(2,1)S(1)} %bitcast.58), channel_id=1, replica_groups=mesh['branch'=2,'head'=4,'page'=32] {'head'}, dimensions={0} | all-to-all | bytes 8388608 | tf_op jit(solution)/shard_map/all_to_all | solution.py:66
  554.2 4.1 reduce_sum.32
  (17 shorter events, 0.1 us)
Async XLA Ops:
  0.0 495.7 %copy-start = (bf16[1024,256]{1,0:T(8,128)(2,1)S(1)}, bf16[1024,256]{1,0:T(8,128)(2,1)}, u32[]{:S(2)}) copy-start(bf16[1024,256]{1,0:T(8,128)(2,1)} %param.15) | copy-start | bytes 1572868
  3.3 12.9 %copy-start.5 = (s32[1,32]{1,0:T(1,128)S(1)}, s32[1,32]{1,0:T(1,128)}, u32[]{:S(2)}) copy-start(s32[1,32]{1,0:T(1,128)} %param.13) | copy-start | bytes 388
  3.3 13.1 %copy-start.2 = (bf16[256,1024]{1,0:T(8,128)(2,1)S(1)}, bf16[256,1024]{1,0:T(8,128)(2,1)}, u32[]{:S(2)}) copy-start(bf16[256,1024]{1,0:T(8,128)(2,1)} %param.8) | copy-start | bytes 1572868
  3.3 13.3 %copy-start.3 = (bf16[256,128]{1,0:T(8,128)(2,1)S(1)}, bf16[256,128]{1,0:T(8,128)(2,1)}, u32[]{:S(2)}) copy-start(bf16[256,128]{1,0:T(8,128)(2,1)} %param.9) | copy-start | bytes 196612
  3.3 108.4 %all-to-all-start = ((bf16[64,2,64,256]{3,2,1,0:T(8,128)(2,1)}), bf16[64,2,64,256]{3,2,1,0:T(8,128)(2,1)}, u32[]{:S(2)}, u32[]{:S(2)}) async-start(bf16[64,2,64,256]{3,2,1,0:T(8,128)(2,1)} %broadcast_in_dim.79), calls=%async_computation | async-start | bytes 8388608 | tf_op jit(solution)/shard_map/all_to_all | solution.py:73
  123.2 1.6 copy-start.1
  123.2 2.0 copy-start.4

commit v6 on v3

--- a/solution.py
+++ b/solution.py
@@ -25,12 +25,14 @@
     slot_count = block_table.shape[1]
     score_scale = 1.0 / math.sqrt(HD)
 
+    w_cols = lax.all_gather(out_weight, ZC, axis=1, tiled=True)
+
     q = queries.reshape(row_count, kv_here, group_size, HD).transpose(1, 2, 0, 3)
     own_k = new_keys.reshape(row_count, kv_here, HD).transpose(1, 0, 2)
     own_v = new_values.reshape(row_count, kv_here, HD).transpose(1, 0, 2)
 
     kv_local = jnp.concatenate([cache_keys, cache_values], axis=-1)
-    kv_all = lax.all_gather(kv_local, ("branch",) + PAGE_AXES, axis=0, tiled=True)
+    kv_all = gather_by_all_to_all(kv_local, ("branch",) + PAGE_AXES)
     kv_sel = jnp.take(kv_all, block_table[0], axis=0)
     anc_len = slot_count * PAGE_TOK
     kv_sel = kv_sel.reshape(anc_len, 2, kv_here, HD)
@@ -60,23 +62,27 @@
     attn = (summed / denom[..., None]).astype(jnp.bfloat16)
     attn_out = attn.transpose(2, 0, 1, 3).reshape(row_count, heads_here * HD)
 
-    n_y = lax.axis_size("y")
-    n_zl = lax.axis_size("zl")
-    n_core = lax.axis_size("core")
-    attn_chips = lax.all_gather(attn_out, ("y", "zl"), axis=0, tiled=True)
-    attn_all = lax.all_gather(attn_chips, "core", axis=0, tiled=True)
-    attn_all = attn_all.reshape(n_core, n_y, n_zl * row_count, attn_all.shape[1])
-    partial_term = jnp.einsum(
-        "cyrk,kf->ycrf", attn_all, out_weight, preferred_element_type=jnp.float32
-    ).astype(jnp.bfloat16)
-    cols = partial_term.shape[-1]
-    partial_term = partial_term.reshape(-1, cols)
-    summed_out = lax.psum_scatter(partial_term, "head", scatter_dimension=0, tiled=True)
-    summed_out = summed_out.reshape(n_core, n_zl, row_count, cols).transpose(1, 0, 2, 3)
-    return summed_out.reshape(n_zl * n_core * row_count, cols)
+    attn_rows = lax.all_gather(attn_out, "y", axis=0, tiled=True)
+    partial_term = jnp.dot(attn_rows, w_cols, preferred_element_type=jnp.float32).astype(
+        jnp.bfloat16
+    )
+    summed = lax.psum_scatter(partial_term, "head", scatter_dimension=0, tiled=True)
+    n_zc = lax.axis_size(ZC)
+    cols = out_weight.shape[1]
+    summed = summed.reshape(row_count, n_zc, cols).transpose(1, 0, 2)
+    arrived = lax.all_to_all(summed, ZC, 0, 0, tiled=True)
+    return arrived.reshape(n_zc * row_count, cols)
+
+
+def gather_by_all_to_all(x, axes):
+    count = lax.axis_size(axes)
+    spread = jnp.broadcast_to(x[None], (count,) + x.shape)
+    arrived = lax.all_to_all(spread, axes, 0, 0, tiled=True)
+    return arrived.reshape((count * x.shape[0],) + x.shape[1:])
 
 
 PAGE_AXES = ("y", "zl", "core")
+ZC = ("zl", "core")
 
 
 def solution(mesh):

time: 458 us -> 303 us (0.66)
  waiting for transfers between devices: 383 us -> 212 us
  blocking collectives: 0 us -> 31.2 us
  local copies, waits for them, and re-layouts: 31.5 us -> 8.1 us
  starting transfers between devices: 0.3 us -> 12.5 us
    all_gather x3 -> x2, waiting for transfers between devices: 332 us -> 31.7 us  [the longest x1 31.7 us: shards(): attn_rows = lax.all_gather(attn_out, 'y', axis=0, tiled=True)]
    all_to_all x0 -> x1, waiting for transfers between devices: none -> 129 us  [gather_by_all_to_all(): arrived = lax.all_to_all(spread, axes, 0, 0, tiled=True)]
    all_to_all x0 -> x1, blocking collectives: none -> 31.2 us  [shards(): arrived = lax.all_to_all(summed, ZC, 0, 0, tiled=True)]
    all_gather x1 -> x0, local copies, waits for them, and re-layouts: 22.4 us -> none  [shards(): attn_all = lax.all_gather(attn_chips, 'core', axis=0, tiled=True)]
    all_to_all x0 -> x1, starting transfers between devices: none -> 12.2 us  [gather_by_all_to_all(): arrived = lax.all_to_all(spread, axes, 0, 0, tiled=True)]
  transfers between devices with their start and end apart: 4 -> 4, of which waited for: 4 -> 3; matrix products, arithmetic and copies ran while one was open for 1% -> 6% of each run, Pallas kernels for 0% -> 0%
where the time goes in v6:
time: 303 us; the launch traced here: 301 us
  waiting for transfers between devices  212 us (70%)
  blocking collectives  31.2 us (10%)
  matrix products  16.6 us (5%)
  between operations  14 us (5%)
  starting transfers between devices  12.5 us (4%)
  local copies, waits for them, and re-layouts  8.1 us (3%)
  other arithmetic  6.89 us (2%)
    all_to_all x1, waiting for transfers between devices, gather_by_all_to_all(): arrived = lax.all_to_all(spread, axes, 0, 0, tiled=True)  129 us
    reduce_scatter x1, waiting for transfers between devices, shards(): lax.psum_scatter(partial_term, 'head', scatter_dimension=0, tiled=True)  51.2 us
    all_gather x1, waiting for transfers between devices, shards(): attn_rows = lax.all_gather(attn_out, 'y', axis=0, tiled=True)  31.7 us
    all_to_all x1, blocking collectives, shards(): arrived = lax.all_to_all(summed, ZC, 0, 0, tiled=True)  31.2 us
    all_to_all x1, starting transfers between devices, gather_by_all_to_all(): arrived = lax.all_to_all(spread, axes, 0, 0, tiled=True)  12.2 us
    dot_general x1, matrix products, shards(): jnp.dot(attn_rows, w_cols, preferred_element_type=jnp.float32)  9.36 us
  transfers between devices with their start and end apart: 4, of which 3 were waited for; matrix products, arithmetic and copies ran while one was open for 6% of the time, Pallas kernels for 0%

profile of v6, /device:TPU:24, one launch (start us, length us, event | category | flops | bytes accessed | tf_op | source)
XLA Modules:
  0.0 301.5 jit_solution(3341380753456593637)
XLA Ops:
  6.5 0.8 pad_maximum_fusion
  7.4 2.5 broadcast_in_dim.72
  9.8 12.2 %all-to-all-start = ((bf16[64,2,64,256]{3,2,1,0:T(8,128)(2,1)}), bf16[64,2,64,256]{3,2,1,0:T(8,128)(2,1)}, u32[]{:S(2)}, u32[]{:S(2)}) async-start(bf16[64,2,64,256]{3,2,1,0:T(8,128)(2,1)} %broadcast_in_dim.72), calls=%async_computation | async-start | bytes 8388608 | tf_op jit(solution)/shard_map/all_to_all | solution.py:80
  22.1 0.7 all-gather.5.cloned.1.call-update
  22.9 0.1 copy.36
  23.6 0.1 broadcast_in_dim.69
  23.7 0.1 broadcast_in_dim.70
  23.9 1.8 select_reduce_fusion.1
  25.7 128.7 %all-to-all-done = bf16[64,2,64,256]{3,2,1,0:T(8,128)(2,1)} async-done(((bf16[64,2,64,256]{3,2,1,0:T(8,128)(2,1)}), bf16[64,2,64,256]{3,2,1,0:T(8,128)(2,1)}, u32[]{:S(2)}, u32[]{:S(2)}) %all-to-all-start) | async-done | bytes 4194336 | tf_op jit(solution)/shard_map/all_to_all | solution.py:80
  154.4 2.8 gather_fusion
  157.2 0.3 gather.7
  157.5 0.7 copy_select_fusion
  158.2 2.7 select_reduce_fusion
  160.9 0.4 convert_reduce_fusion.1
  161.4 4.9 %convert_reduce_fusion = (f32[8,256]{1,0:T(8,128)S(1)}, bf16[8,256,2048]{1,2,0:T(8,128)(2,1)S(1)}) fusion(f32[8,256]{1,0:T(8,128)S(1)} %max.9, f32[2048,8,256]{2,0,1:T(8,128)S(1)} %get-tuple-element.10, pred[2048]{0:T(1024)(128)(4,1)S(1)} %iota_compare_fusion.1), kind=kLoop, calls=%fused_computation.1 | loop fusion | flops 25163776 | bytes 25184256 | tf_op jit(solution)/shard_map/reduce_sum | solution.py:58
  166.3 1.3 fusion.3
  167.7 1.4 fusion.2
  169.0 0.2 reduce-scatter.2.cloned.1.call-start
  169.3 31.7 %all-gather.3.cloned.1.call-done = bf16[1024,1024]{0,1:T(8,128)(2,1)} async-done(((bf16[256,1024]{0,1:T(8,128)(2,1)}), bf16[1024,1024]{0,1:T(8,128)(2,1)}) %all-gather.3.cloned.1.call-update) | async-done | bytes 2097168 | tf_op jit(solution)/shard_map/all_gather | solution.py:65
  200.9 9.4 %convolution_convert_fusion = bf16[1024,2048]{1,0:T(8,128)(2,1)} fusion(bf16[1024,1024]{0,1:T(8,128)(2,1)} %all-gather.3.cloned.1.call-done, bf16[1024,2048]{1,0:T(8,128)(2,1)} %all-gather.5.cloned.1.call-done), kind=kOutput, calls=%fused_computation.5 | convolution fusion | flops 4297064448 | bytes 10485760 | tf_op jit(solution)/shard_map/dot_general | solution.py:66
  210.3 51.2 %reduce-scatter.2.cloned.1.call-done = bf16[256,2048]{1,0:T(8,128)(2,1)} async-done(((bf16[1024,2048]{1,0:T(8,128)(2,1)}), bf16[256,2048]{1,0:T(8,128)(2,1)}) %reduce-scatter.2.cloned.1.call-update) | async-done | bytes 1048592 | tf_op jit(solution)/shard_map/reduce_scatter | solution.py:69
  261.5 1.3 copy.51
  262.8 31.2 %all_to_all.10 = bf16[8,256,256]{2,1,0:T(8,128)(2,1)S(1)} all-to-all(bf16[8,256,256]{2,1,0:T(8,128)(2,1)S(1)} %bitcast.63), channel_id=1, replica_groups=mesh['branch'=2,'head'=4,'y'=4,'zl'=4,'core'=2] {'zl','core'}, dimensions={0} | all-to-all | bytes 2097152 | tf_op jit(solution)/shard_map/all_to_all | solution.py:73
  294.0 1.0 copy.54
  (22 shorter events, 0.2 us)
Async XLA Ops:
  6.5 17.3 %copy-start = (bf16[256,128]{1,0:T(8,128)(2,1)S(1)}, bf16[256,128]{1,0:T(8,128)(2,1)}, u32[]{:S(2)}) copy-start(bf16[256,128]{1,0:T(8,128)(2,1)} %param.9) | copy-start | bytes 196612
  9.8 13.0 %copy-start.2 = (bf16[256,1024]{1,0:T(8,128)(2,1)S(1)}, bf16[256,1024]{1,0:T(8,128)(2,1)}, u32[]{:S(2)}) copy-start(bf16[256,1024]{1,0:T(8,128)(2,1)} %param.8) | copy-start | bytes 1572868
  9.8 13.8 %copy-start.4 = (s32[1,32]{1,0:T(1,128)S(1)}, s32[1,32]{1,0:T(1,128)}, u32[]{:S(2)}) copy-start(s32[1,32]{1,0:T(1,128)} %param.13) | copy-start | bytes 388
  9.8 144.6 %all-to-all-start = ((bf16[64,2,64,256]{3,2,1,0:T(8,128)(2,1)}), bf16[64,2,64,256]{3,2,1,0:T(8,128)(2,1)}, u32[]{:S(2)}, u32[]{:S(2)}) async-start(bf16[64,2,64,256]{3,2,1,0:T(8,128)(2,1)} %broadcast_in_dim.72), calls=%async_computation | async-start | bytes 8388608 | tf_op jit(solution)/shard_map/all_to_all | solution.py:80
  22.1 147.2 %all-gather.5.cloned.1.call-start = ((), (), s32[]{:S(2)}) async-start(), calls=%async_computation.4 | async-start | bytes 4718592 | tf_op jit(solution)/shard_map/all_gather | solution.py:28
  22.8 178.1 %all-gather.3.cloned.1.call-start = ((), (), s32[]{:S(2)}) async-start(), calls=%async_computation.3 | async-start | bytes 2621440 | tf_op jit(solution)/shard_map/all_gather | solution.py:65
  158.2 2.8 copy-start.1
  166.3 1.3 copy-start.3
  169.0 92.5 %reduce-scatter.2.cloned.1.call-start = ((), (), s32[]{:S(2)}) async-start(), calls=%async_computation.5 | async-start | bytes 5242880 | tf_op jit(solution)/shard_map/reduce_scatter | solution.py:69
Sparse Core Ops, SparseCore 0:
  24.6 128.9 all-gather.4
  169.2 31.7 all-gather.2
  210.4 50.9 reduce-scatter.1

commit v7 on v6

--- a/solution.py
+++ b/solution.py
@@ -62,7 +62,7 @@
     attn = (summed / denom[..., None]).astype(jnp.bfloat16)
     attn_out = attn.transpose(2, 0, 1, 3).reshape(row_count, heads_here * HD)
 
-    attn_rows = lax.all_gather(attn_out, "y", axis=0, tiled=True)
+    attn_rows = gather_by_all_to_all(attn_out, "y")
     partial_term = jnp.dot(attn_rows, w_cols, preferred_element_type=jnp.float32).astype(
         jnp.bfloat16
     )

time: 303 us -> 294 us (0.970)
  waiting for transfers between devices: 212 us -> 199 us
  starting transfers between devices: 12.5 us -> 16.8 us
    all_gather x1 -> x0, waiting for transfers between devices: 31.7 us -> none  [shards(): attn_rows = lax.all_gather(attn_out, 'y', axis=0, tiled=True)]
    all_to_all x1 -> x2, waiting for transfers between devices: 129 us -> 152 us  [gather_by_all_to_all(): arrived = lax.all_to_all(spread, axes, 0, 0, tiled=True)]
    reduce_scatter x1, waiting for transfers between devices: 51.2 us -> 46.4 us  [shards(): lax.psum_scatter(partial_term, 'head', scatter_dimension=0, tiled=True)]
    all_to_all x1 -> x2, starting transfers between devices: 12.2 us -> 16.7 us  [gather_by_all_to_all(): arrived = lax.all_to_all(spread, axes, 0, 0, tiled=True)]
where the time goes in v7:
time: 294 us; the launch traced here: 293 us
  waiting for transfers between devices  199 us (68%)
  blocking collectives  31.2 us (11%)
  starting transfers between devices  16.8 us (6%)
  matrix products  14.6 us (5%)
  between operations  14.2 us (5%)
  local copies, waits for them, and re-layouts  9.89 us (3%)
  other arithmetic  6.89 us (2%)
    all_to_all x2, waiting for transfers between devices, gather_by_all_to_all(): arrived = lax.all_to_all(spread, axes, 0, 0, tiled=True)  152 us
    reduce_scatter x1, waiting for transfers between devices, shards(): lax.psum_scatter(partial_term, 'head', scatter_dimension=0, tiled=True)  46.4 us
    all_to_all x1, blocking collectives, shards(): arrived = lax.all_to_all(summed, ZC, 0, 0, tiled=True)  31.2 us
    all_to_all x2, starting transfers between devices, gather_by_all_to_all(): arrived = lax.all_to_all(spread, axes, 0, 0, tiled=True)  16.7 us
    dot_general x1, matrix products, shards(): jnp.dot(attn_rows, w_cols, preferred_element_type=jnp.float32)  8.22 us
  transfers between devices with their start and end apart: 4, of which 3 were waited for; matrix products, arithmetic and copies ran while one was open for 6% of the time, Pallas kernels for 0%

profile of v7, /device:TPU:24, one launch (start us, length us, event | category | flops | bytes accessed | tf_op | source)
XLA Modules:
  0.0 292.6 jit_solution(8913617823271286527)
XLA Ops:
  6.5 0.8 pad_maximum_fusion
  7.4 2.5 broadcast_in_dim.79
  9.8 12.2 %all-to-all-start = ((bf16[64,2,64,256]{3,2,1,0:T(8,128)(2,1)}), bf16[64,2,64,256]{3,2,1,0:T(8,128)(2,1)}, u32[]{:S(2)}, u32[]{:S(2)}) async-start(bf16[64,2,64,256]{3,2,1,0:T(8,128)(2,1)} %broadcast_in_dim.79), calls=%async_computation | async-start | bytes 8388608 | tf_op jit(solution)/shard_map/all_to_all | solution.py:80
  22.1 0.7 all-gather.2.cloned.1.call-update
  22.8 0.1 copy.39
  23.8 1.8 select_reduce_fusion.1
  25.7 128.7 %all-to-all-done = bf16[64,2,64,256]{3,2,1,0:T(8,128)(2,1)} async-done(((bf16[64,2,64,256]{3,2,1,0:T(8,128)(2,1)}), bf16[64,2,64,256]{3,2,1,0:T(8,128)(2,1)}, u32[]{:S(2)}, u32[]{:S(2)}) %all-to-all-start) | async-done | bytes 4194336 | tf_op jit(solution)/shard_map/all_to_all | solution.py:80
  154.4 2.8 gather_fusion
  157.2 0.3 gather.7
  157.5 0.7 copy_select_fusion
  158.2 2.7 select_reduce_fusion
  161.0 0.4 convert_reduce_fusion.1
  161.4 4.9 %convert_reduce_fusion = (f32[8,256]{1,0:T(8,128)S(1)}, bf16[8,256,2048]{1,2,0:T(8,128)(2,1)S(1)}) fusion(f32[8,256]{1,0:T(8,128)S(1)} %max.9, f32[2048,8,256]{2,0,1:T(8,128)S(1)} %get-tuple-element.10, pred[2048]{0:T(1024)(128)(4,1)S(1)} %iota_compare_fusion.1), kind=kLoop, calls=%fused_computation.1 | loop fusion | flops 25163776 | bytes 25184256 | tf_op jit(solution)/shard_map/reduce_sum | solution.py:58
  166.3 1.3 fusion.3
  167.7 0.6 fusion.2
  168.2 0.2 copy.30
  168.4 1.6 broadcast_in_dim.85
  170.0 4.5 %all-to-all-start.1 = ((bf16[4,256,1024]{2,1,0:T(8,128)(2,1)}), bf16[4,256,1024]{2,1,0:T(8,128)(2,1)S(1)}, u32[]{:S(2)}, u32[]{:S(2)}) async-start(bf16[4,256,1024]{2,1,0:T(8,128)(2,1)} %broadcast_in_dim.85), calls=%async_computation.1 | async-start | bytes 4194304 | tf_op jit(solution)/shard_map/all_to_all | solution.py:80
  174.5 23.2 %all-to-all-done.1 = bf16[4,256,1024]{2,1,0:T(8,128)(2,1)S(1)} async-done(((bf16[4,256,1024]{2,1,0:T(8,128)(2,1)}), bf16[4,256,1024]{2,1,0:T(8,128)(2,1)S(1)}, u32[]{:S(2)}, u32[]{:S(2)}) %all-to-all-start.1) | async-done | bytes 2097184 | tf_op jit(solution)/shard_map/all_to_all | solution.py:80
  197.7 8.2 %convolution_convert_fusion = bf16[1024,2048]{1,0:T(8,128)(2,1)} fusion(bf16[1024,1024]{1,0:T(8,128)(2,1)S(1)} %bitcast.68, bf16[1024,2048]{1,0:T(8,128)(2,1)} %all-gather.2.cloned.1.call-done), kind=kOutput, calls=%fused_computation.5 | convolution fusion | flops 4297064448 | bytes 10485760 | tf_op jit(solution)/shard_map/dot_general | solution.py:66
  205.9 46.4 %reduce-scatter.2.cloned.1.call-done = bf16[256,2048]{1,0:T(8,128)(2,1)} async-done(((bf16[1024,2048]{1,0:T(8,128)(2,1)}), bf16[256,2048]{1,0:T(8,128)(2,1)}) %reduce-scatter.2.cloned.1.call-update) | async-done | bytes 1048592 | tf_op jit(solution)/shard_map/reduce_scatter | solution.py:69
  252.4 1.3 copy.54
  253.7 31.2 %all_to_all.15 = bf16[8,256,256]{2,1,0:T(8,128)(2,1)S(1)} all-to-all(bf16[8,256,256]{2,1,0:T(8,128)(2,1)S(1)} %bitcast.64), channel_id=1, replica_groups=mesh['branch'=2,'head'=4,'y'=4,'zl'=4,'core'=2] {'zl','core'}, dimensions={0} | all-to-all | bytes 2097152 | tf_op jit(solution)/shard_map/all_to_all | solution.py:73
  284.8 1.0 copy.57
  (23 shorter events, 0.3 us)
Async XLA Ops:
  6.5 17.3 %copy-start = (bf16[256,128]{1,0:T(8,128)(2,1)S(1)}, bf16[256,128]{1,0:T(8,128)(2,1)}, u32[]{:S(2)}) copy-start(bf16[256,128]{1,0:T(8,128)(2,1)} %param.9) | copy-start | bytes 196612
  9.8 13.0 %copy-start.2 = (bf16[256,1024]{1,0:T(8,128)(2,1)S(1)}, bf16[256,1024]{1,0:T(8,128)(2,1)}, u32[]{:S(2)}) copy-start(bf16[256,1024]{1,0:T(8,128)(2,1)} %param.8) | copy-start | bytes 1572868
  9.8 13.8 %copy-start.4 = (s32[1,32]{1,0:T(1,128)S(1)}, s32[1,32]{1,0:T(1,128)}, u32[]{:S(2)}) copy-start(s32[1,32]{1,0:T(1,128)} %param.13) | copy-start | bytes 388
  9.8 144.6 %all-to-all-start = ((bf16[64,2,64,256]{3,2,1,0:T(8,128)(2,1)}), bf16[64,2,64,256]{3,2,1,0:T(8,128)(2,1)}, u32[]{:S(2)}, u32[]{:S(2)}) async-start(bf16[64,2,64,256]{3,2,1,0:T(8,128)(2,1)} %broadcast_in_dim.79), calls=%async_computation | async-start | bytes 8388608 | tf_op jit(solution)/shard_map/all_to_all | solution.py:80
  22.1 152.5 %all-gather.2.cloned.1.call-start = ((), (), s32[]{:S(2)}) async-start(), calls=%async_computation.4 | async-start | bytes 4718592 | tf_op jit(solution)/shard_map/all_gather | solution.py:28
  158.2 2.8 copy-start.1
  166.3 1.3 copy-start.3
  170.0 27.7 %all-to-all-start.1 = ((bf16[4,256,1024]{2,1,0:T(8,128)(2,1)}), bf16[4,256,1024]{2,1,0:T(8,128)(2,1)S(1)}, u32[]{:S(2)}, u32[]{:S(2)}) async-start(bf16[4,256,1024]{2,1,0:T(8,128)(2,1)} %broadcast_in_dim.85), calls=%async_computation.1 | async-start | bytes 4194304 | tf_op jit(solution)/shard_map/all_to_all | solution.py:80
  174.5 77.8 %reduce-scatter.2.cloned.1.call-start = ((), (), s32[]{:S(2)}) async-start(), calls=%async_computation.5 | async-start | bytes 5242880 | tf_op jit(solution)/shard_map/reduce_scatter | solution.py:69
Sparse Core Ops, SparseCore 0:
  24.6 128.9 all-gather.1
  206.1 46.2 reduce-scatter.1

commit v8 on v7

--- a/solution.py
+++ b/solution.py
@@ -25,14 +25,14 @@
     slot_count = block_table.shape[1]
     score_scale = 1.0 / math.sqrt(HD)
 
-    w_cols = lax.all_gather(out_weight, ZC, axis=1, tiled=True)
+    w_stack = gather_by_all_to_all(out_weight[None], ZC)
 
     q = queries.reshape(row_count, kv_here, group_size, HD).transpose(1, 2, 0, 3)
     own_k = new_keys.reshape(row_count, kv_here, HD).transpose(1, 0, 2)
     own_v = new_values.reshape(row_count, kv_here, HD).transpose(1, 0, 2)
 
     kv_local = jnp.concatenate([cache_keys, cache_values], axis=-1)
-    kv_all = gather_by_all_to_all(kv_local, ("branch",) + PAGE_AXES)
+    kv_all = lax.all_gather(kv_local, ("branch",) + PAGE_AXES, axis=0, tiled=True)
     kv_sel = jnp.take(kv_all, block_table[0], axis=0)
     anc_len = slot_count * PAGE_TOK
     kv_sel = kv_sel.reshape(anc_len, 2, kv_here, HD)
@@ -63,9 +63,10 @@
     attn_out = attn.transpose(2, 0, 1, 3).reshape(row_count, heads_here * HD)
 
     attn_rows = gather_by_all_to_all(attn_out, "y")
-    partial_term = jnp.dot(attn_rows, w_cols, preferred_element_type=jnp.float32).astype(
-        jnp.bfloat16
-    )
+    partial_term = jnp.einsum(
+        "rk,jkc->rjc", attn_rows, w_stack, preferred_element_type=jnp.float32
+    ).astype(jnp.bfloat16)
+    partial_term = partial_term.reshape(partial_term.shape[0], -1)
     summed = lax.psum_scatter(partial_term, "head", scatter_dimension=0, tiled=True)
     n_zc = lax.axis_size(ZC)
     cols = out_weight.shape[1]

time: 294 us -> 308 us (1.048)
  blocking collectives: 31.2 us -> 64 us
  starting transfers between devices: 16.8 us -> 6.07 us
  waiting for transfers between devices: 199 us -> 190 us
    all_to_all x2 -> x1, waiting for transfers between devices: 152 us -> 0.01 us  [gather_by_all_to_all(): arrived = lax.all_to_all(spread, axes, 0, 0, tiled=True)]
    all_gather x1, waiting for transfers between devices: 0.01 us -> 142 us  [shards(): lax.all_gather(kv_local, ('branch',) + PAGE_AXES, axis=0, tiled=True)]
    all_to_all x0 -> x1, blocking collectives: none -> 32.8 us  [gather_by_all_to_all(): arrived = lax.all_to_all(spread, axes, 0, 0, tiled=True)]
    all_to_all x2 -> x1, starting transfers between devices: 16.7 us -> 6.03 us  [gather_by_all_to_all(): arrived = lax.all_to_all(spread, axes, 0, 0, tiled=True)]
  transfers between devices with their start and end apart: 4 -> 3, of which waited for: 3 -> 2; matrix products, arithmetic and copies ran while one was open for 6% -> 6% of each run, Pallas kernels for 0% -> 0%
where the time goes in v8:
time: 308 us; the launch traced here: 307 us
  waiting for transfers between devices  190 us (62%)
  blocking collectives  64 us (21%)
  matrix products  14.9 us (5%)
  between operations  14.3 us (5%)
  local copies, waits for them, and re-layouts  10 us (3%)
  other arithmetic  7.51 us (2%)
  starting transfers between devices  6.07 us (2%)
    all_gather x1, waiting for transfers between devices, shards(): lax.all_gather(kv_local, ('branch',) + PAGE_AXES, axis=0, tiled=True)  142 us
    reduce_scatter x1, waiting for transfers between devices, shards(): lax.psum_scatter(partial_term, 'head', scatter_dimension=0, tiled=True)  47.9 us
    all_to_all x1, blocking collectives, gather_by_all_to_all(): arrived = lax.all_to_all(spread, axes, 0, 0, tiled=True)  32.8 us
    all_to_all x1, blocking collectives, shards(): arrived = lax.all_to_all(summed, ZC, 0, 0, tiled=True)  31.2 us
    dot_general x1, matrix products, shards(): jnp.einsum('rk,jkc->rjc', attn_rows, w_stack, preferred_element_type=jnp....  8.47 us
  transfers between devices with their start and end apart: 3, of which 2 were waited for; matrix products, arithmetic and copies ran while one was open for 6% of the time, Pallas kernels for 0%

profile of v8, /device:TPU:24, one launch (start us, length us, event | category | flops | bytes accessed | tf_op | source)
XLA Modules:
  0.0 307.0 jit_solution(14131803237375005520)
XLA Ops:
  6.5 1.4 pad_maximum_fusion
  8.0 1.2 copy.33
  9.3 2.5 broadcast_in_dim.84
  11.8 6.0 %all-to-all-start.1 = ((bf16[8,1,1024,256]{2,3,1,0:T(8,128)(2,1)}), bf16[8,1,1024,256]{2,3,1,0:T(8,128)(2,1)}, u32[]{:S(2)}, u32[]{:S(2)}) async-start(bf16[8,1,1024,256]{2,3,1,0:T(8,128)(2,1)} %broadcast_in_dim.84), calls=%async_computation.1 | async-start | bytes 8388608 | tf_op jit(solution)/shard_map/all_to_all | solution.py:81
  17.9 0.1 copy.41
  18.7 0.1 broadcast_in_dim.76
  18.9 1.8 select_reduce_fusion.1
  20.7 142.3 %all-gather.2.cloned.1.call-done = bf16[128,64,256]{2,1,0:T(8,128)(2,1)} async-done(((bf16[2,64,256]{2,1,0:T(8,128)(2,1)}), bf16[128,64,256]{2,1,0:T(8,128)(2,1)}) %all-gather.2.cloned.1.call-update) | async-done | bytes 4194320 | tf_op jit(solution)/shard_map/all_gather | solution.py:35
  163.0 2.8 gather_fusion
  165.8 0.3 gather.7
  166.1 0.7 copy_select_fusion
  166.8 2.7 select_reduce_fusion
  169.6 0.4 convert_reduce_fusion.1
  170.0 4.9 %convert_reduce_fusion = (f32[8,256]{1,0:T(8,128)S(1)}, bf16[8,256,2048]{1,2,0:T(8,128)(2,1)S(1)}) fusion(f32[8,256]{1,0:T(8,128)S(1)} %max.9, f32[2048,8,256]{2,0,1:T(8,128)S(1)} %get-tuple-element.10, pred[2048]{0:T(1024)(128)(4,1)S(1)} %iota_compare_fusion.1), kind=kLoop, calls=%fused_computation.1 | loop fusion | flops 25163776 | bytes 25184256 | tf_op jit(solution)/shard_map/reduce_sum | solution.py:58
  174.9 1.3 fusion.8
  176.3 0.6 fusion.7
  176.8 0.2 copy.32
  177.1 0.3 broadcast_in_dim.83
  177.3 32.8 %all_to_all.15 = bf16[4,256,1024]{2,1,0:T(8,128)(2,1)S(1)} all-to-all(bf16[4,256,1024]{2,1,0:T(8,128)(2,1)S(1)} %broadcast_in_dim.83), channel_id=1, replica_groups=mesh['branch'=2,'head'=4,'y'=4,'zl'=4,'core'=2] {'y'}, dimensions={0} | all-to-all | bytes 4194304 | tf_op jit(solution)/shard_map/all_to_all | solution.py:81
  210.1 8.5 %fusion.3 = bf16[1024,8,256]{0,2,1:T(8,128)(2,1)} fusion(bf16[1024,1024,1]{1,0,2:T(8,128)(2,1)S(1)} %bitcast.70, bf16[8,1,1024,256]{2,3,1,0:T(8,128)(2,1)} %all-to-all-done.1), kind=kOutput, calls=%fused_computation.7 | convolution fusion | flops 4297064448 | bytes 10485760 | tf_op jit(solution)/shard_map/rk,jkc->rjc/dot_general | solution.py:66
  218.6 47.9 %reduce-scatter.2.cloned.1.call-done = bf16[256,2048]{0,1:T(8,128)(2,1)} async-done(((bf16[1024,2048]{0,1:T(8,128)(2,1)}), bf16[256,2048]{0,1:T(8,128)(2,1)}) %reduce-scatter.2.cloned.1.call-update) | async-done | bytes 1048592 | tf_op jit(solution)/shard_map/reduce_scatter | solution.py:70
  266.6 1.5 copy.34
  268.0 31.2 %all_to_all.16 = bf16[8,256,256]{2,1,0:T(8,128)(2,1)S(1)} all-to-all(bf16[8,256,256]{2,1,0:T(8,128)(2,1)S(1)} %bitcast.66), channel_id=1, replica_groups=mesh['branch'=2,'head'=4,'y'=4,'zl'=4,'core'=2] {'zl','core'}, dimensions={0} | all-to-all | bytes 2097152 | tf_op jit(solution)/shard_map/all_to_all | solution.py:74
  299.2 1.0 copy.57
  (23 shorter events, 0.2 us)
Async XLA Ops:
  6.5 12.3 %copy-start = (bf16[256,128]{1,0:T(8,128)(2,1)S(1)}, bf16[256,128]{1,0:T(8,128)(2,1)}, u32[]{:S(2)}) copy-start(bf16[256,128]{1,0:T(8,128)(2,1)} %param.9) | copy-start | bytes 196612
  6.5 156.5 %all-gather.2.cloned.1.call-start = ((), (), s32[]{:S(2)}) async-start(), calls=%async_computation.4 | async-start | bytes 4259840 | tf_op jit(solution)/shard_map/all_gather | solution.py:35
  11.8 6.1 %copy-start.2 = (bf16[256,1024]{1,0:T(8,128)(2,1)S(1)}, bf16[256,1024]{1,0:T(8,128)(2,1)}, u32[]{:S(2)}) copy-start(bf16[256,1024]{1,0:T(8,128)(2,1)} %param.8) | copy-start | bytes 1572868
  11.8 6.8 %copy-start.4 = (s32[1,32]{1,0:T(1,128)S(1)}, s32[1,32]{1,0:T(1,128)}, u32[]{:S(2)}) copy-start(s32[1,32]{1,0:T(1,128)} %param.13) | copy-start | bytes 388
  11.8 165.3 %all-to-all-start.1 = ((bf16[8,1,1024,256]{2,3,1,0:T(8,128)(2,1)}), bf16[8,1,1024,256]{2,3,1,0:T(8,128)(2,1)}, u32[]{:S(2)}, u32[]{:S(2)}) async-start(bf16[8,1,1024,256]{2,3,1,0:T(8,128)(2,1)} %broadcast_in_dim.84), calls=%async_computation.1 | async-start | bytes 8388608 | tf_op jit(solution)/shard_map/all_to_all | solution.py:81
  17.8 248.8 %reduce-scatter.2.cloned.1.call-start = ((), (), s32[]{:S(2)}) async-start(), calls=%async_computation.5 | async-start | bytes 5242880 | tf_op jit(solution)/shard_map/reduce_scatter | solution.py:70
  166.8 2.8 copy-start.1
  174.9 1.3 copy-start.3
Sparse Core Ops, SparseCore 0:
  9.2 153.7 all-gather.1
  218.7 47.7 reduce-scatter.1

commit v9 on v7

--- a/solution.py
+++ b/solution.py
@@ -25,14 +25,14 @@
     slot_count = block_table.shape[1]
     score_scale = 1.0 / math.sqrt(HD)
 
-    w_cols = lax.all_gather(out_weight, ZC, axis=1, tiled=True)
-
     q = queries.reshape(row_count, kv_here, group_size, HD).transpose(1, 2, 0, 3)
     own_k = new_keys.reshape(row_count, kv_here, HD).transpose(1, 0, 2)
     own_v = new_values.reshape(row_count, kv_here, HD).transpose(1, 0, 2)
 
     kv_local = jnp.concatenate([cache_keys, cache_values], axis=-1)
     kv_all = gather_by_all_to_all(kv_local, ("branch",) + PAGE_AXES)
+    out_weight, kv_all = lax.optimization_barrier((out_weight, kv_all))
+    w_cols = lax.all_gather(out_weight, ZC, axis=1, tiled=True)
     kv_sel = jnp.take(kv_all, block_table[0], axis=0)
     anc_len = slot_count * PAGE_TOK
     kv_sel = kv_sel.reshape(anc_len, 2, kv_here, HD)

time: 294 us -> 265 us (0.901)
  waiting for transfers between devices: 199 us -> 54 us
  blocking collectives: 31.2 us -> 167 us
  starting transfers between devices: 16.8 us -> 0.04 us
  local copies, waits for them, and re-layouts: 9.89 us -> 6.63 us
    all_to_all x2 -> x0, waiting for transfers between devices: 152 us -> none  [gather_by_all_to_all(): arrived = lax.all_to_all(spread, axes, 0, 0, tiled=True)]
    all_to_all x0 -> x2, blocking collectives: none -> 136 us  [gather_by_all_to_all(): arrived = lax.all_to_all(spread, axes, 0, 0, tiled=True)]
    all_to_all x2 -> x0, starting transfers between devices: 16.7 us -> none  [gather_by_all_to_all(): arrived = lax.all_to_all(spread, axes, 0, 0, tiled=True)]
    all_gather x1, waiting for transfers between devices: 0.01 us -> 3.82 us  [shards(): w_cols = lax.all_gather(out_weight, ZC, axis=1, tiled=True)]
    reduce_scatter x1, waiting for transfers between devices: 46.4 us -> 50.2 us  [shards(): lax.psum_scatter(partial_term, 'head', scatter_dimension=0, tiled=True)]
    broadcast_in_dim x3, local copies, waits for them, and re-layouts: 4.25 us -> 0.99 us  [gather_by_all_to_all(): spread = jnp.broadcast_to(x[None], (count,) + x.shape)]
  transfers between devices with their start and end apart: 4 -> 2, of which waited for: 3 -> 2; matrix products, arithmetic and copies ran while one was open for 6% -> 6% of each run, Pallas kernels for 0% -> 0%
where the time goes in v9:
time: 265 us; the launch traced here: 264 us
  blocking collectives  167 us (63%)
  waiting for transfers between devices  54 us (20%)
  matrix products  14.7 us (6%)
  between operations  14.3 us (5%)
  other arithmetic  6.89 us (3%)
  local copies, waits for them, and re-layouts  6.63 us (3%)
    all_to_all x2, blocking collectives, gather_by_all_to_all(): arrived = lax.all_to_all(spread, axes, 0, 0, tiled=True)  136 us
    reduce_scatter x1, waiting for transfers between devices, shards(): lax.psum_scatter(partial_term, 'head', scatter_dimension=0, tiled=True)  50.2 us
    all_to_all x1, blocking collectives, shards(): arrived = lax.all_to_all(summed, ZC, 0, 0, tiled=True)  31.2 us
    dot_general x1, matrix products, shards(): jnp.dot(attn_rows, w_cols, preferred_element_type=jnp.float32)  8.22 us
  transfers between devices with their start and end apart: 2, of which 2 were waited for; matrix products, arithmetic and copies ran while one was open for 6% of the time, Pallas kernels for 0%

profile of v9, /device:TPU:24, one launch (start us, length us, event | category | flops | bytes accessed | tf_op | source)
XLA Modules:
  0.0 264.0 jit_solution(16052534370370649451)
XLA Ops:
  6.5 0.8 pad_maximum_fusion
  7.4 0.5 broadcast_in_dim.79
  7.9 108.2 %all_to_all.15 = bf16[64,2,64,256]{3,2,1,0:T(8,128)(2,1)} all-to-all(bf16[64,2,64,256]{3,2,1,0:T(8,128)(2,1)S(1)} %broadcast_in_dim.79), channel_id=1, replica_groups=mesh['branch'=2,'head'=4,'y'=4,'zl'=4,'core'=2] {'branch','y','zl','core'}, dimensions={0} | all-to-all | bytes 8388608 | tf_op jit(solution)/shard_map/all_to_all | solution.py:80
  116.2 0.1 broadcast_in_dim.76
  116.3 0.1 broadcast_in_dim.77
  116.4 0.1 copy.39
  117.2 1.9 select_reduce_fusion.1
  119.1 2.8 %gather_fusion = bf16[32,64,256]{2,1,0:T(8,128)(2,1)S(1)} fusion(bf16[128,64,256]{2,1,0:T(8,128)(2,1)} %bitcast.64, s32[1024]{0:T(1024)S(1)} %pad_clamp_fusion), kind=kCustom, calls=%fused_computation | custom fusion | bytes 2097280 | tf_op jit(solution)/shard_map/jit(_take)/gather | solution.py:36
  121.9 0.3 gather.7
  122.2 0.7 copy_select_fusion
  122.9 2.7 %select_reduce_fusion = (f32[8,256]{1,0:T(8,128)S(1)}, f32[2048,8,256]{2,0,1:T(8,128)S(1)}) fusion(pred[2048]{0:T(1024)(128)(4,1)S(1)} %iota_compare_fusion.1, bf16[256,1,8,128]{3,2,0,1:T(8,128)(2,1)S(1)} %bitcast.68, bf16[2048,2,1,128]{3,0,2,1:T(8,128)(2,1)S(1)} %copy_select_fusion), kind=kOutput, calls=%fused_computation.3 | convolution fusion | flops 1086322688 | bytes 17836032 | tf_op jit(solution)/shard_map/kgnd,kjd->kgnj/dot_general | solution.py:46
  125.6 0.4 convert_reduce_fusion.1
  126.1 4.9 %convert_reduce_fusion = (f32[8,256]{1,0:T(8,128)S(1)}, bf16[8,256,2048]{1,2,0:T(8,128)(2,1)S(1)}) fusion(f32[8,256]{1,0:T(8,128)S(1)} %max.9, f32[2048,8,256]{2,0,1:T(8,128)S(1)} %get-tuple-element.14, pred[2048]{0:T(1024)(128)(4,1)S(1)} %iota_compare_fusion.1), kind=kLoop, calls=%fused_computation.1 | loop fusion | flops 25163776 | bytes 25184256 | tf_op jit(solution)/shard_map/reduce_sum | solution.py:58
  131.0 1.3 fusion.3
  132.4 0.6 fusion.2
  132.9 0.2 copy.30
  133.1 0.3 broadcast_in_dim.85
  133.4 28.1 %all_to_all.16 = bf16[4,256,1024]{2,1,0:T(8,128)(2,1)S(1)} all-to-all(bf16[4,256,1024]{2,1,0:T(8,128)(2,1)S(1)} %broadcast_in_dim.85), channel_id=1, replica_groups=mesh['branch'=2,'head'=4,'y'=4,'zl'=4,'core'=2] {'y'}, dimensions={0} | all-to-all | bytes 4194304 | tf_op jit(solution)/shard_map/all_to_all | solution.py:80
  161.5 3.8 %all-gather.2.cloned.1.call-done = bf16[1024,2048]{1,0:T(8,128)(2,1)} async-done(((bf16[1024,256]{1,0:T(8,128)(2,1)}), bf16[1024,2048]{1,0:T(8,128)(2,1)}) %all-gather.2.cloned.1.call-update) | async-done | bytes 4194320 | tf_op jit(solution)/shard_map/all_gather | solution.py:35
  165.3 8.2 %convolution_convert_fusion = bf16[1024,2048]{1,0:T(8,128)(2,1)} fusion(bf16[1024,1024]{1,0:T(8,128)(2,1)S(1)} %bitcast.69, bf16[1024,2048]{1,0:T(8,128)(2,1)} %all-gather.2.cloned.1.call-done), kind=kOutput, calls=%fused_computation.5 | convolution fusion | flops 4297064448 | bytes 10485760 | tf_op jit(solution)/shard_map/dot_general | solution.py:66
  173.6 50.2 %reduce-scatter.2.cloned.1.call-done = bf16[256,2048]{1,0:T(8,128)(2,1)} async-done(((bf16[1024,2048]{1,0:T(8,128)(2,1)}), bf16[256,2048]{1,0:T(8,128)(2,1)}) %reduce-scatter.2.cloned.1.call-update) | async-done | bytes 1048592 | tf_op jit(solution)/shard_map/reduce_scatter | solution.py:69
  223.7 1.3 copy.54
  225.0 31.2 %all_to_all.17 = bf16[8,256,256]{2,1,0:T(8,128)(2,1)S(1)} all-to-all(bf16[8,256,256]{2,1,0:T(8,128)(2,1)S(1)} %bitcast.65), channel_id=1, replica_groups=mesh['branch'=2,'head'=4,'y'=4,'zl'=4,'core'=2] {'zl','core'}, dimensions={0} | all-to-all | bytes 2097152 | tf_op jit(solution)/shard_map/all_to_all | solution.py:73
  256.2 1.0 copy.57
  (21 shorter events, 0.2 us)
Async XLA Ops:
  6.5 110.7 %copy-start = (bf16[256,128]{1,0:T(8,128)(2,1)S(1)}, bf16[256,128]{1,0:T(8,128)(2,1)}, u32[]{:S(2)}) copy-start(bf16[256,128]{1,0:T(8,128)(2,1)} %param.9) | copy-start | bytes 196612
  6.5 158.8 %all-gather.2.cloned.1.call-start = ((), (), s32[]{:S(2)}) async-start(), calls=%async_computation.4 | async-start | bytes 4718592 | tf_op jit(solution)/shard_map/all_gather | solution.py:35
  7.9 108.3 %copy-start.4 = (s32[1,32]{1,0:T(1,128)S(1)}, s32[1,32]{1,0:T(1,128)}, u32[]{:S(2)}) copy-start(s32[1,32]{1,0:T(1,128)} %param.13) | copy-start | bytes 388
  7.9 108.5 %copy-start.2 = (bf16[256,1024]{1,0:T(8,128)(2,1)S(1)}, bf16[256,1024]{1,0:T(8,128)(2,1)}, u32[]{:S(2)}) copy-start(bf16[256,1024]{1,0:T(8,128)(2,1)} %param.8) | copy-start | bytes 1572868
  116.1 107.6 %reduce-scatter.2.cloned.1.call-start = ((), (), s32[]{:S(2)}) async-start(), calls=%async_computation.5 | async-start | bytes 5242880 | tf_op jit(solution)/shard_map/reduce_scatter | solution.py:69
  122.9 2.8 %copy-start.1 = (f32[8,256,256]{1,2,0:T(8,128)S(1)}, f32[8,256,256]{1,2,0:T(8,128)}, u32[]{:S(2)}) copy-start(f32[8,256,256]{1,2,0:T(8,128)} %get-tuple-element.12) | copy-start | bytes 6291460
  131.0 1.3 copy-start.3
Sparse Core Ops, SparseCore 0:
  116.3 49.0 all-gather.1
  173.7 49.9 reduce-scatter.1

commit v10 on v9

--- a/solution.py
+++ b/solution.py
@@ -30,10 +30,16 @@
     own_v = new_values.reshape(row_count, kv_here, HD).transpose(1, 0, 2)
 
     kv_local = jnp.concatenate([cache_keys, cache_values], axis=-1)
-    kv_all = gather_by_all_to_all(kv_local, ("branch",) + PAGE_AXES)
+    kv_chips = gather_by_all_to_all(kv_local, ("branch", "y", "zl"))
+    kv_all = gather_by_all_to_all(kv_chips, "core")
     out_weight, kv_all = lax.optimization_barrier((out_weight, kv_all))
     w_cols = lax.all_gather(out_weight, ZC, axis=1, tiled=True)
-    kv_sel = jnp.take(kv_all, block_table[0], axis=0)
+    pages_here = cache_keys.shape[0]
+    n_core = lax.axis_size("core")
+    n_chips = lax.axis_size(("branch", "y", "zl"))
+    owner = block_table[0] // pages_here
+    position = ((owner % n_core) * n_chips + owner // n_core) * pages_here + block_table[0] % pages_here
+    kv_sel = jnp.take(kv_all, position, axis=0)
     anc_len = slot_count * PAGE_TOK
     kv_sel = kv_sel.reshape(anc_len, 2, kv_here, HD)
     anc_k = kv_sel[:, 0].transpose(1, 0, 2)

time: 265 us -> 227 us (0.86)
  blocking collectives: 167 us -> 130 us
    all_to_all x2 -> x3, blocking collectives: 136 us -> 98.6 us  [gather_by_all_to_all(): arrived = lax.all_to_all(spread, axes, 0, 0, tiled=True)]
  transfers between devices with their start and end apart: 2 -> 2, of which waited for: 2 -> 2; matrix products, arithmetic and copies ran while one was open for 6% -> 7% of each run, Pallas kernels for 0% -> 0%
where the time goes in v10:
time: 227 us; the launch traced here: 226 us
  blocking collectives  130 us (57%)
  waiting for transfers between devices  53.6 us (24%)
  matrix products  14.7 us (6%)
  between operations  14.3 us (6%)
  other arithmetic  6.93 us (3%)
  local copies, waits for them, and re-layouts  6.9 us (3%)
    all_to_all x3, blocking collectives, gather_by_all_to_all(): arrived = lax.all_to_all(spread, axes, 0, 0, tiled=True)  98.6 us
    reduce_scatter x1, waiting for transfers between devices, shards(): lax.psum_scatter(partial_term, 'head', scatter_dimension=0, tiled=True)  50.1 us
    all_to_all x1, blocking collectives, shards(): arrived = lax.all_to_all(summed, ZC, 0, 0, tiled=True)  31.2 us
    dot_general x1, matrix products, shards(): jnp.dot(attn_rows, w_cols, preferred_element_type=jnp.float32)  8.22 us
    reduce_sum x1, other arithmetic, shards(): jnp.sum(anc_w.astype(jnp.float32), axis=-1)  4.9 us
  transfers between devices with their start and end apart: 2, of which 2 were waited for; matrix products, arithmetic and copies ran while one was open for 7% of the time, Pallas kernels for 0%

profile of v10, /device:TPU:24, one launch (start us, length us, event | category | flops | bytes accessed | tf_op | source)
XLA Modules:
  0.0 226.2 jit_solution(11783293337691834057)
XLA Ops:
  6.5 0.8 pad_maximum_fusion
  7.4 0.2 broadcast_in_dim.86
  7.6 60.7 %all_to_all.20 = bf16[32,2,64,256]{3,2,1,0:T(8,128)(2,1)S(1)} all-to-all(bf16[32,2,64,256]{3,2,1,0:T(8,128)(2,1)S(1)} %broadcast_in_dim.86), channel_id=1, replica_groups=mesh['branch'=2,'head'=4,'y'=4,'zl'=4,'core'=2] {'branch','y','zl'}, dimensions={0} | all-to-all | bytes 4194304 | tf_op jit(solution)/shard_map/all_to_all | solution.py:86
  68.3 0.5 broadcast_in_dim.88
  68.9 8.3 %all_to_all.21 = bf16[2,64,64,256]{3,2,1,0:T(8,128)(2,1)} all-to-all(bf16[2,64,64,256]{3,2,1,0:T(8,128)(2,1)S(1)} %broadcast_in_dim.88), channel_id=1, replica_groups=mesh['branch'=2,'head'=4,'y'=4,'zl'=4,'core'=2] {'core'}, dimensions={0} | all-to-all | bytes 8388608 | tf_op jit(solution)/shard_map/all_to_all | solution.py:86
  77.4 0.1 copy.39
  78.3 1.9 select_reduce_fusion.1
  80.2 2.8 %gather_fusion = bf16[32,64,256]{2,1,0:T(8,128)(2,1)S(1)} fusion(bf16[128,64,256]{2,1,0:T(8,128)(2,1)} %bitcast.92, s32[1024]{0:T(1024)S(1)} %pad_clamp_fusion), kind=kCustom, calls=%fused_computation | custom fusion | bytes 2097280 | tf_op jit(solution)/shard_map/jit(_take)/gather | solution.py:42
  83.0 0.3 gather.7
  83.3 0.7 copy_select_fusion
  84.0 2.7 %select_reduce_fusion = (f32[8,256]{1,0:T(8,128)S(1)}, f32[2048,8,256]{2,0,1:T(8,128)S(1)}) fusion(pred[2048]{0:T(1024)(128)(4,1)S(1)} %iota_compare_fusion.1, bf16[256,1,8,128]{3,2,0,1:T(8,128)(2,1)S(1)} %bitcast.96, bf16[2048,2,1,128]{3,0,2,1:T(8,128)(2,1)S(1)} %copy_select_fusion), kind=kOutput, calls=%fused_computation.3 | convolution fusion | flops 1086322688 | bytes 17836032 | tf_op jit(solution)/shard_map/kgnd,kjd->kgnj/dot_general | solution.py:52
  86.7 0.4 convert_reduce_fusion.1
  87.2 4.9 %convert_reduce_fusion = (f32[8,256]{1,0:T(8,128)S(1)}, bf16[8,256,2048]{1,2,0:T(8,128)(2,1)S(1)}) fusion(f32[8,256]{1,0:T(8,128)S(1)} %max.9, f32[2048,8,256]{2,0,1:T(8,128)S(1)} %get-tuple-element.14, pred[2048]{0:T(1024)(128)(4,1)S(1)} %iota_compare_fusion.1), kind=kLoop, calls=%fused_computation.1 | loop fusion | flops 25163776 | bytes 25184256 | tf_op jit(solution)/shard_map/reduce_sum | solution.py:64
  92.1 1.3 fusion.3
  93.4 0.6 fusion.2
  94.0 0.2 copy.30
  94.2 0.3 broadcast_in_dim.94
  94.5 29.6 %all_to_all.22 = bf16[4,256,1024]{2,1,0:T(8,128)(2,1)S(1)} all-to-all(bf16[4,256,1024]{2,1,0:T(8,128)(2,1)S(1)} %broadcast_in_dim.94), channel_id=1, replica_groups=mesh['branch'=2,'head'=4,'y'=4,'zl'=4,'core'=2] {'y'}, dimensions={0} | all-to-all | bytes 4194304 | tf_op jit(solution)/shard_map/all_to_all | solution.py:86
  124.1 3.5 %all-gather.2.cloned.1.call-done = bf16[1024,2048]{1,0:T(8,128)(2,1)} async-done(((bf16[1024,256]{1,0:T(8,128)(2,1)}), bf16[1024,2048]{1,0:T(8,128)(2,1)}) %all-gather.2.cloned.1.call-update) | async-done | bytes 4194320 | tf_op jit(solution)/shard_map/all_gather | solution.py:36
  127.6 8.2 %convolution_convert_fusion = bf16[1024,2048]{1,0:T(8,128)(2,1)} fusion(bf16[1024,1024]{1,0:T(8,128)(2,1)S(1)} %bitcast.97, bf16[1024,2048]{1,0:T(8,128)(2,1)} %all-gather.2.cloned.1.call-done), kind=kOutput, calls=%fused_computation.5 | convolution fusion | flops 4297064448 | bytes 10485760 | tf_op jit(solution)/shard_map/dot_general | solution.py:72
  135.8 50.1 %reduce-scatter.2.cloned.1.call-done = bf16[256,2048]{1,0:T(8,128)(2,1)} async-done(((bf16[1024,2048]{1,0:T(8,128)(2,1)}), bf16[256,2048]{1,0:T(8,128)(2,1)}) %reduce-scatter.2.cloned.1.call-update) | async-done | bytes 1048592 | tf_op jit(solution)/shard_map/reduce_scatter | solution.py:75
  185.9 1.3 copy.54
  187.2 31.2 %all_to_all.23 = bf16[8,256,256]{2,1,0:T(8,128)(2,1)S(1)} all-to-all(bf16[8,256,256]{2,1,0:T(8,128)(2,1)S(1)} %bitcast.93), channel_id=1, replica_groups=mesh['branch'=2,'head'=4,'y'=4,'zl'=4,'core'=2] {'zl','core'}, dimensions={0} | all-to-all | bytes 2097152 | tf_op jit(solution)/shard_map/all_to_all | solution.py:79
  218.3 1.0 copy.57
  (23 shorter events, 0.4 us)
Async XLA Ops:
  6.5 71.7 %copy-start = (bf16[256,128]{1,0:T(8,128)(2,1)S(1)}, bf16[256,128]{1,0:T(8,128)(2,1)}, u32[]{:S(2)}) copy-start(bf16[256,128]{1,0:T(8,128)(2,1)} %param.9) | copy-start | bytes 196612
  6.5 121.0 %all-gather.2.cloned.1.call-start = ((), (), s32[]{:S(2)}) async-start(), calls=%async_computation.5 | async-start | bytes 4718592 | tf_op jit(solution)/shard_map/all_gather | solution.py:36
  68.8 8.4 %copy-start.4 = (s32[1,32]{1,0:T(1,128)S(1)}, s32[1,32]{1,0:T(1,128)}, u32[]{:S(2)}) copy-start(s32[1,32]{1,0:T(1,128)} %param.13) | copy-start | bytes 388
  68.9 8.6 %copy-start.2 = (bf16[256,1024]{1,0:T(8,128)(2,1)S(1)}, bf16[256,1024]{1,0:T(8,128)(2,1)}, u32[]{:S(2)}) copy-start(bf16[256,1024]{1,0:T(8,128)(2,1)} %param.8) | copy-start | bytes 1572868
  77.2 108.7 %reduce-scatter.2.cloned.1.call-start = ((), (), s32[]{:S(2)}) async-start(), calls=%async_computation.6 | async-start | bytes 5242880 | tf_op jit(solution)/shard_map/reduce_scatter | solution.py:75
  83.9 2.8 %copy-start.1 = (f32[8,256,256]{1,2,0:T(8,128)S(1)}, f32[8,256,256]{1,2,0:T(8,128)}, u32[]{:S(2)}) copy-start(f32[8,256,256]{1,2,0:T(8,128)} %get-tuple-element.12) | copy-start | bytes 6291460
  92.1 1.3 copy-start.3
Sparse Core Ops, SparseCore 0:
  77.3 50.2 all-gather.1
  135.9 49.9 reduce-scatter.1

commit v11 on v10

--- a/solution.py
+++ b/solution.py
@@ -72,7 +72,14 @@
     partial_term = jnp.dot(attn_rows, w_cols, preferred_element_type=jnp.float32).astype(
         jnp.bfloat16
     )
-    summed = lax.psum_scatter(partial_term, "head", scatter_dimension=0, tiled=True)
+    n_head = lax.axis_size("head")
+    half = partial_term.shape[1] // 2
+    by_scatter = lax.psum_scatter(partial_term[:, :half], "head", scatter_dimension=0, tiled=True)
+    arrived = lax.all_to_all(
+        partial_term[:, half:].reshape(n_head, -1, half), "head", 0, 0, tiled=True
+    )
+    by_exchange = jnp.sum(arrived.astype(jnp.float32), axis=0).astype(jnp.bfloat16)
+    summed = jnp.concatenate([by_scatter, by_exchange], axis=1)
     n_zc = lax.axis_size(ZC)
     cols = out_weight.shape[1]
     summed = summed.reshape(row_count, n_zc, cols).transpose(1, 0, 2)

time: 227 us -> 226 us (level)
  waiting for transfers between devices: 53.6 us -> 4.66 us
  blocking collectives: 130 us -> 176 us
    reduce_scatter x1, waiting for transfers between devices: 50.1 us -> 1.15 us  [shards(): lax.psum_scatter(partial_term[:, :half], 'head', scatter_dimension=0, til...]
    all_to_all x0 -> x1, blocking collectives: none -> 47.8 us  [shards(): lax.all_to_all(partial_term[:, half:].reshape(n_head, -1, half), 'head',...]
    slice x0 -> x1, local copies, waits for them, and re-layouts: none -> 2.39 us  [shards(): partial_term[:, :half]]
where the time goes in v11:
time: 226 us; the launch traced here: 225 us
  blocking collectives  176 us (78%)
  between operations  14.3 us (6%)
  matrix products  13.4 us (6%)
  other arithmetic  8.47 us (4%)
  local copies, waits for them, and re-layouts  8.07 us (4%)
  waiting for transfers between devices  4.66 us (2%)
    all_to_all x3, blocking collectives, gather_by_all_to_all(): arrived = lax.all_to_all(spread, axes, 0, 0, tiled=True)  98.6 us
    all_to_all x1, blocking collectives, shards(): lax.all_to_all(partial_term[:, half:].reshape(n_head, -1, half), 'head',...  47.8 us
    all_to_all x1, blocking collectives, shards(): arrived = lax.all_to_all(summed, ZC, 0, 0, tiled=True)  29.7 us
    dot_general x1, matrix products, shards(): jnp.dot(attn_rows, w_cols, preferred_element_type=jnp.float32)  6.88 us
    reduce_sum x1, other arithmetic, shards(): jnp.sum(anc_w.astype(jnp.float32), axis=-1)  4.9 us
  transfers between devices with their start and end apart: 2, of which 2 were waited for; matrix products, arithmetic and copies ran while one was open for 7% of the time, Pallas kernels for 0%

profile of v11, /device:TPU:24, one launch (start us, length us, event | category | flops | bytes accessed | tf_op | source)
XLA Modules:
  0.0 225.0 jit_solution(2026471354995644073)
XLA Ops:
  6.5 0.8 pad_maximum_fusion.1
  7.6 60.7 %all_to_all.25 = bf16[32,2,64,256]{3,2,1,0:T(8,128)(2,1)S(1)} all-to-all(bf16[32,2,64,256]{3,2,1,0:T(8,128)(2,1)S(1)} %broadcast_in_dim.86), channel_id=1, replica_groups=mesh['branch'=2,'head'=4,'y'=4,'zl'=4,'core'=2] {'branch','y','zl'}, dimensions={0} | all-to-all | bytes 4194304 | tf_op jit(solution)/shard_map/all_to_all | solution.py:93
  68.3 0.5 broadcast_in_dim.88
  68.9 8.3 %all_to_all.26 = bf16[2,64,64,256]{3,2,1,0:T(8,128)(2,1)} all-to-all(bf16[2,64,64,256]{3,2,1,0:T(8,128)(2,1)S(1)} %broadcast_in_dim.88), channel_id=1, replica_groups=mesh['branch'=2,'head'=4,'y'=4,'zl'=4,'core'=2] {'core'}, dimensions={0} | all-to-all | bytes 8388608 | tf_op jit(solution)/shard_map/all_to_all | solution.py:93
  78.3 1.9 select_reduce_fusion.1
  80.2 2.8 %gather_fusion = bf16[32,64,256]{2,1,0:T(8,128)(2,1)S(1)} fusion(bf16[128,64,256]{2,1,0:T(8,128)(2,1)} %bitcast.94, s32[1024]{0:T(1024)S(1)} %pad_clamp_fusion), kind=kCustom, calls=%fused_computation | custom fusion | bytes 2097280 | tf_op jit(solution)/shard_map/jit(_take)/gather | solution.py:42
  83.0 0.3 gather.7
  83.3 0.7 copy_select_fusion
  84.0 2.7 %select_reduce_fusion = (f32[8,256]{1,0:T(8,128)S(1)}, f32[2048,8,256]{2,0,1:T(8,128)S(1)}) fusion(pred[2048]{0:T(1024)(128)(4,1)S(1)} %iota_compare_fusion.1, bf16[256,1,8,128]{3,2,0,1:T(8,128)(2,1)S(1)} %bitcast.99, bf16[2048,2,1,128]{3,0,2,1:T(8,128)(2,1)S(1)} %copy_select_fusion), kind=kOutput, calls=%fused_computation.3 | convolution fusion | flops 1086322688 | bytes 17836032 | tf_op jit(solution)/shard_map/kgnd,kjd->kgnj/dot_general | solution.py:52
  86.7 0.4 convert_reduce_fusion.1
  87.2 4.9 %convert_reduce_fusion = (f32[8,256]{1,0:T(8,128)S(1)}, bf16[8,256,2048]{1,2,0:T(8,128)(2,1)S(1)}) fusion(f32[8,256]{1,0:T(8,128)S(1)} %max.9, f32[2048,8,256]{2,0,1:T(8,128)S(1)} %get-tuple-element.16, pred[2048]{0:T(1024)(128)(4,1)S(1)} %iota_compare_fusion.1), kind=kLoop, calls=%fused_computation.1 | loop fusion | flops 25163776 | bytes 25184256 | tf_op jit(solution)/shard_map/reduce_sum | solution.py:64
  92.1 1.3 fusion.3
  93.4 0.6 fusion.2
  94.2 0.3 broadcast_in_dim.94
  94.5 29.6 %all_to_all.27 = bf16[4,256,1024]{2,1,0:T(8,128)(2,1)S(1)} all-to-all(bf16[4,256,1024]{2,1,0:T(8,128)(2,1)S(1)} %broadcast_in_dim.94), channel_id=1, replica_groups=mesh['branch'=2,'head'=4,'y'=4,'zl'=4,'core'=2] {'y'}, dimensions={0} | all-to-all | bytes 4194304 | tf_op jit(solution)/shard_map/all_to_all | solution.py:93
  124.1 3.5 %all-gather.2.cloned.1.call-done = bf16[1024,2048]{1,0:T(8,128)(2,1)} async-done(((bf16[1024,256]{1,0:T(8,128)(2,1)}), bf16[1024,2048]{1,0:T(8,128)(2,1)}) %all-gather.2.cloned.1.call-update) | async-done | bytes 4194320 | tf_op jit(solution)/shard_map/all_gather | solution.py:36
  127.6 6.9 %convolution_convert_fusion = bf16[1024,2048]{1,0:T(8,128)(2,1)S(1)} fusion(bf16[1024,1024]{1,0:T(8,128)(2,1)S(1)} %bitcast.100, bf16[1024,2048]{1,0:T(8,128)(2,1)} %all-gather.2.cloned.1.call-done), kind=kOutput, calls=%fused_computation.5 | convolution fusion | flops 4297064448 | bytes 10485760 | tf_op jit(solution)/shard_map/dot_general | solution.py:72
  134.5 2.4 %fusion.20 = (bf16[1024,1024]{1,0:T(8,128)(2,1)}, bf16[1024,1024]{1,0:T(8,128)(2,1)}) fusion(bf16[1024,2048]{1,0:T(8,128)(2,1)S(1)} %convolution_convert_fusion), kind=kLoop, calls=%fused_computation.62 | loop fusion | bytes 8388608 | tf_op jit(solution)/shard_map/slice | solution.py:77
  136.9 47.8 %all_to_all.28 = bf16[4,256,1024]{2,1,0:T(8,128)(2,1)S(1)} all-to-all(bf16[4,256,1024]{2,1,0:T(8,128)(2,1)} %bitcast.93), channel_id=1, replica_groups=mesh['branch'=2,'head'=4,'y'=4,'zl'=4,'core'=2] {'head'}, dimensions={0} | all-to-all | bytes 4194304 | tf_op jit(solution)/shard_map/all_to_all | solution.py:78
  184.7 0.4 reduce_sum.32
  185.1 1.2 reduce-scatter.2.cloned.1.call-done
  186.3 1.1 pad_maximum_fusion
  187.5 29.7 %all_to_all.29 = bf16[8,256,256]{2,1,0:T(8,128)(2,1)S(1)} all-to-all(bf16[8,256,256]{2,1,0:T(8,128)(2,1)S(1)} %bitcast.96), channel_id=1, replica_groups=mesh['branch'=2,'head'=4,'y'=4,'zl'=4,'core'=2] {'zl','core'}, dimensions={0} | all-to-all | bytes 2097152 | tf_op jit(solution)/shard_map/all_to_all | solution.py:86
  217.2 1.0 copy.57
  (29 shorter events, 1.0 us)
Async XLA Ops:
  6.5 71.7 %copy-start = (bf16[256,128]{1,0:T(8,128)(2,1)S(1)}, bf16[256,128]{1,0:T(8,128)(2,1)}, u32[]{:S(2)}) copy-start(bf16[256,128]{1,0:T(8,128)(2,1)} %param.9) | copy-start | bytes 196612
  6.5 121.0 %all-gather.2.cloned.1.call-start = ((), (), s32[]{:S(2)}) async-start(), calls=%async_computation.6 | async-start | bytes 4718592 | tf_op jit(solution)/shard_map/all_gather | solution.py:36
  68.8 8.4 %copy-start.5 = (s32[1,32]{1,0:T(1,128)S(1)}, s32[1,32]{1,0:T(1,128)}, u32[]{:S(2)}) copy-start(s32[1,32]{1,0:T(1,128)} %param.13) | copy-start | bytes 388
  68.9 8.6 %copy-start.3 = (bf16[256,1024]{1,0:T(8,128)(2,1)S(1)}, bf16[256,1024]{1,0:T(8,128)(2,1)}, u32[]{:S(2)}) copy-start(bf16[256,1024]{1,0:T(8,128)(2,1)} %param.8) | copy-start | bytes 1572868
  77.2 109.1 %reduce-scatter.2.cloned.1.call-start = ((), (), s32[]{:S(2)}) async-start(), calls=%async_computation.7 | async-start | bytes 2621440 | tf_op jit(solution)/shard_map/reduce_scatter | solution.py:77
  83.9 2.8 %copy-start.2 = (f32[8,256,256]{1,2,0:T(8,128)S(1)}, f32[8,256,256]{1,2,0:T(8,128)}, u32[]{:S(2)}) copy-start(f32[8,256,256]{1,2,0:T(8,128)} %get-tuple-element.14) | copy-start | bytes 6291460
  92.1 1.3 copy-start.4
  187.5 30.7 %copy-start.1 = (bf16[256,128]{1,0:T(8,128)(2,1)S(1)}, bf16[256,128]{1,0:T(8,128)(2,1)}, u32[]{:S(2)}) copy-start(bf16[256,128]{1,0:T(8,128)(2,1)} %param.9) | copy-start | bytes 196612
Sparse Core Ops, SparseCore 0:
  77.3 50.2 all-gather.1
  137.0 49.2 reduce-scatter.1

commit v12 on v10

--- a/solution.py
+++ b/solution.py
@@ -45,15 +45,37 @@
     anc_k = kv_sel[:, 0].transpose(1, 0, 2)
     anc_v = kv_sel[:, 1].transpose(1, 0, 2)
 
+    places = jnp.arange(row_count, dtype=jnp.int32)
+    own_mask = places[None, :] <= places[:, None]
+    anc_mask = jnp.arange(anc_len, dtype=jnp.int32) < ancestor_len[0]
+    split = group_size // 2
+    partial_f32 = None
+    for lower in (0, split):
+        q_half = q[:, lower:lower + split]
+        attn_half = attend(q_half, own_k, own_v, anc_k, anc_v, own_mask, anc_mask, score_scale)
+        attn_half = attn_half.transpose(2, 0, 1, 3).reshape(row_count, kv_here * split * HD)
+        rows_half = gather_by_all_to_all(attn_half, "y")
+        w_half = w_cols.reshape(kv_here, group_size, HD, -1)[:, lower:lower + split]
+        term = jnp.dot(
+            rows_half, w_half.reshape(kv_here * split * HD, -1), preferred_element_type=jnp.float32
+        )
+        partial_f32 = term if partial_f32 is None else partial_f32 + term
+    partial_term = partial_f32.astype(jnp.bfloat16)
+    summed = lax.psum_scatter(partial_term, "head", scatter_dimension=0, tiled=True)
+    n_zc = lax.axis_size(ZC)
+    cols = out_weight.shape[1]
+    summed = summed.reshape(row_count, n_zc, cols).transpose(1, 0, 2)
+    arrived = lax.all_to_all(summed, ZC, 0, 0, tiled=True)
+    return arrived.reshape(n_zc * row_count, cols)
+
+
+def attend(q, own_k, own_v, anc_k, anc_v, own_mask, anc_mask, score_scale):
     own_scores = (
         jnp.einsum("kgnd,kjd->kgnj", q, own_k, preferred_element_type=jnp.float32) * score_scale
     )
     anc_scores = (
         jnp.einsum("kgnd,kjd->kgnj", q, anc_k, preferred_element_type=jnp.float32) * score_scale
     )
-    places = jnp.arange(row_count, dtype=jnp.int32)
-    own_mask = places[None, :] <= places[:, None]
-    anc_mask = jnp.arange(anc_len, dtype=jnp.int32) < ancestor_len[0]
     own_m = jnp.where(own_mask[None, None], own_scores, masked_fill)
     anc_m = jnp.where(anc_mask[None, None, None, :], anc_scores, masked_fill)
     row_max = jnp.maximum(jnp.max(own_m, axis=-1), jnp.max(anc_m, axis=-1))[..., None]
@@ -65,19 +87,7 @@
     summed = jnp.einsum(
         "kgnj,kjd->kgnd", own_w, own_v, preferred_element_type=jnp.float32
     ) + jnp.einsum("kgnj,kjd->kgnd", anc_w, anc_v, preferred_element_type=jnp.float32)
-    attn = (summed / denom[..., None]).astype(jnp.bfloat16)
-    attn_out = attn.transpose(2, 0, 1, 3).reshape(row_count, heads_here * HD)
-
-    attn_rows = gather_by_all_to_all(attn_out, "y")
-    partial_term = jnp.dot(attn_rows, w_cols, preferred_element_type=jnp.float32).astype(
-        jnp.bfloat16
-    )
-    summed = lax.psum_scatter(partial_term, "head", scatter_dimension=0, tiled=True)
-    n_zc = lax.axis_size(ZC)
-    cols = out_weight.shape[1]
-    summed = summed.reshape(row_count, n_zc, cols).transpose(1, 0, 2)
-    arrived = lax.all_to_all(summed, ZC, 0, 0, tiled=True)
-    return arrived.reshape(n_zc * row_count, cols)
+    return (summed / denom[..., None]).astype(jnp.bfloat16)
 
 
 def gather_by_all_to_all(x, axes):

time: 227 us -> 235 us (1.035)
  blocking collectives: 130 us -> 100 us
  starting transfers between devices: 0.04 us -> 10.8 us
  waiting for transfers between devices: 53.6 us -> 62.8 us
  local copies, waits for them, and re-layouts: 6.9 us -> 14.9 us
  matrix products: 14.7 us -> 22.4 us
    all_to_all x3 -> x2, blocking collectives: 98.6 us -> 68.8 us  [gather_by_all_to_all(): arrived = lax.all_to_all(spread, axes, 0, 0, tiled=True)]
    all_to_all x0 -> x2, waiting for transfers between devices: none -> 11.5 us  [gather_by_all_to_all(): arrived = lax.all_to_all(spread, axes, 0, 0, tiled=True)]
    all_to_all x0 -> x2, starting transfers between devices: none -> 10.8 us  [gather_by_all_to_all(): arrived = lax.all_to_all(spread, axes, 0, 0, tiled=True)]
    dot_general x5 -> x10, matrix products: 14.7 us -> 22.4 us  [the longest x2 13.3 us: shards(): jnp.dot(rows_half, w_half.reshape(kv_here * split * HD, -1), preferred_el...]
    gather x2, local copies, waits for them, and re-layouts: 3.09 us -> 5.91 us  [shards(): kv_sel = jnp.take(kv_all, position, axis=0)]
    slice x0 -> x1, local copies, waits for them, and re-layouts: none -> 2.71 us  [shards(): w_half = w_cols.reshape(kv_here, group_size, HD, -1)[:, lower:lower + split]]
  transfers between devices with their start and end apart: 2 -> 4, of which waited for: 2 -> 4; matrix products, arithmetic and copies ran while one was open for 7% -> 15% of each run, Pallas kernels for 0% -> 0%
where the time goes in v12:
time: 235 us; the launch traced here: 234 us
  blocking collectives  100 us (43%)
  waiting for transfers between devices  62.8 us (27%)
  matrix products  22.4 us (10%)
  local copies, waits for them, and re-layouts  14.9 us (6%)
  between operations  14.3 us (6%)
  starting transfers between devices  10.8 us (5%)
  other arithmetic  8.77 us (4%)
    all_to_all x2, blocking collectives, gather_by_all_to_all(): arrived = lax.all_to_all(spread, axes, 0, 0, tiled=True)  68.8 us
    reduce_scatter x1, waiting for transfers between devices, shards(): lax.psum_scatter(partial_term, 'head', scatter_dimension=0, tiled=True)  48.4 us
    all_to_all x1, blocking collectives, shards(): arrived = lax.all_to_all(summed, ZC, 0, 0, tiled=True)  31.2 us
    dot_general x2, matrix products, shards(): jnp.dot(rows_half, w_half.reshape(kv_here * split * HD, -1), preferred_el...  13.3 us
    all_to_all x2, waiting for transfers between devices, gather_by_all_to_all(): arrived = lax.all_to_all(spread, axes, 0, 0, tiled=True)  11.5 us
    all_to_all x2, starting transfers between devices, gather_by_all_to_all(): arrived = lax.all_to_all(spread, axes, 0, 0, tiled=True)  10.8 us
    gather x2, local copies, waits for them, and re-layouts, shards(): kv_sel = jnp.take(kv_all, position, axis=0)  5.91 us
    reduce_sum x1, other arithmetic, attend(): jnp.sum(anc_w.astype(jnp.float32), axis=-1)  5.91 us
  transfers between devices with their start and end apart: 4, of which 4 were waited for; matrix products, arithmetic and copies ran while one was open for 15% of the time, Pallas kernels for 0%

profile of v12, /device:TPU:24, one launch (start us, length us, event | category | flops | bytes accessed | tf_op | source)
XLA Modules:
  0.0 233.9 jit_solution(11858586136612899843)
XLA Ops:
  6.5 0.8 pad_maximum_fusion
  7.6 60.7 %all_to_all.25 = bf16[32,2,64,256]{3,2,1,0:T(8,128)(2,1)S(1)} all-to-all(bf16[32,2,64,256]{3,2,1,0:T(8,128)(2,1)S(1)} %broadcast_in_dim.119), channel_id=1, replica_groups=mesh['branch'=2,'head'=4,'y'=4,'zl'=4,'core'=2] {'branch','y','zl'}, dimensions={0} | all-to-all | bytes 4194304 | tf_op jit(solution)/shard_map/all_to_all | solution.py:96
  68.9 8.2 %all_to_all.26 = bf16[2,64,64,256]{3,2,1,0:T(8,128)(2,1)} all-to-all(bf16[2,64,64,256]{3,2,1,0:T(8,128)(2,1)S(1)} %broadcast_in_dim.121), channel_id=1, replica_groups=mesh['branch'=2,'head'=4,'y'=4,'zl'=4,'core'=2] {'core'}, dimensions={0} | all-to-all | bytes 8388608 | tf_op jit(solution)/shard_map/all_to_all | solution.py:96
  79.1 3.8 %gather_fusion = bf16[32,64,256]{2,1,0:T(8,128)(2,1)} fusion(bf16[128,64,256]{2,1,0:T(8,128)(2,1)} %bitcast.114, s32[1024]{0:T(1024)S(1)} %pad_clamp_fusion), kind=kCustom, calls=%fused_computation | custom fusion | bytes 2097280 | tf_op jit(solution)/shard_map/jit(_take)/gather | solution.py:42
  82.9 2.1 gather.7
  85.1 1.5 copy_select_fusion
  86.6 1.3 fusion.7
  87.9 2.6 %select_reduce_fusion = (f32[4,256]{1,0:T(4,128)S(1)}, f32[4,256]{1,0:T(4,128)S(1)}, f32[2048,4,256]{2,0,1:T(8,128)S(1)}) fusion(pred[2048]{0:T(1024)(128)(4,1)S(1)} %iota_compare_fusion.1, f32[2048,4,256]{2,0,1:T(8,128)S(1)} %fusion.7, bf16[1,8,256,128]{3,2,1,0:T(8,128)(2,1)S(1)} %bitcast.118, bf16[2048,2,1,128]{3,0,2,1:T(8,128)(2,1)S(1)} %copy_select_fusion), kind=kOutput, calls=%fused_computation.4 | convolution fusion | flops 549451776 | bytes 17573888 | tf_op jit(solution)/shard_map/kgnd,kjd->kgnj/dot_general | solution.py:77
  90.9 5.9 %convert_reduce_fusion = (f32[4,256]{1,0:T(4,128)S(1)}, bf16[4,256,2048]{1,2,0:T(8,128)(2,1)}, f32[4,256]{1,0:T(4,128)S(1)}, bf16[4,256,2048]{1,2,0:T(8,128)(2,1)S(1)}) fusion(f32[4,256]{1,0:T(4,128)S(1)} %max.19, f32[2048,4,256]{2,0,1:T(8,128)S(1)} %get-tuple-element.24, pred[2048]{0:T(1024)(128)(4,1)S(1)} %iota_compare_fusion.1, f32[4,256]{1,0:T(4,128)S(1)} %max.18, ...), kind=kLoop, calls=%fused_computation.2 | loop fusion | flops 25163776 | bytes 25184256 | tf_op jit(solution)/shard_map/reduce_sum | solution.py:86
  98.1 1.1 broadcast_in_dim.127
  99.1 5.2 %all-to-all-start.2 = ((bf16[4,256,512]{2,1,0:T(8,128)(2,1)}), bf16[4,256,512]{2,1,0:T(8,128)(2,1)S(1)}, u32[]{:S(2)}, u32[]{:S(2)}) async-start(bf16[4,256,512]{2,1,0:T(8,128)(2,1)} %broadcast_in_dim.127), calls=%async_computation.2 | async-start | bytes 2097152 | tf_op jit(solution)/shard_map/all_to_all | solution.py:96
  104.7 3.2 %fusion.4 = bf16[4,256,128]{1,2,0:T(8,128)(2,1)S(1)} fusion(f32[4,256,128]{1,2,0:T(8,128)S(1)} %fusion.8, bf16[4,256,2048]{1,2,0:T(8,128)(2,1)} %get-tuple-element.16, bf16[2048,2,1,128]{3,0,2,1:T(8,128)(2,1)} %copy-done.2, f32[4,256]{1,0:T(4,128)S(1)} %add.147), kind=kOutput, calls=%fused_computation.16 | convolution fusion | flops 537264128 | bytes 5509120 | tf_op jit(solution)/shard_map/kgnj,kjd->kgnd/dot_general | solution.py:89
  108.0 9.9 %all-to-all-done.2 = bf16[4,256,512]{2,1,0:T(8,128)(2,1)S(1)} async-done(((bf16[4,256,512]{2,1,0:T(8,128)(2,1)}), bf16[4,256,512]{2,1,0:T(8,128)(2,1)S(1)}, u32[]{:S(2)}, u32[]{:S(2)}) %all-to-all-start.2) | async-done | bytes 1048608 | tf_op jit(solution)/shard_map/all_to_all | solution.py:96
  118.0 1.2 broadcast_in_dim.129
  119.2 5.6 %all-to-all-start.3 = ((bf16[4,256,512]{2,1,0:T(8,128)(2,1)}), bf16[4,256,512]{2,1,0:T(8,128)(2,1)S(1)}, u32[]{:S(2)}, u32[]{:S(2)}) async-start(bf16[4,256,512]{2,1,0:T(8,128)(2,1)} %broadcast_in_dim.129), calls=%async_computation.3 | async-start | bytes 2097152 | tf_op jit(solution)/shard_map/all_to_all | solution.py:96
  124.8 2.8 %all-gather.2.cloned.1.call-done = bf16[1024,2048]{1,0:T(8,128)(2,1)} async-done(((bf16[1024,256]{1,0:T(8,128)(2,1)}), bf16[1024,2048]{1,0:T(8,128)(2,1)}) %all-gather.2.cloned.1.call-update) | async-done | bytes 4194320 | tf_op jit(solution)/shard_map/all_gather | solution.py:36
  127.6 2.7 %fusion.25 = (bf16[1,4,128,2048]{3,2,1,0:T(8,128)(2,1)S(1)}, bf16[1,4,128,2048]{3,2,1,0:T(8,128)(2,1)S(1)}) fusion(bf16[1,8,128,2048]{3,2,1,0:T(8,128)(2,1)} %bitcast.119), kind=kLoop, calls=%fused_computation.76 | loop fusion | bytes 8388608 | tf_op jit(solution)/shard_map/slice | solution.py:58
  130.3 5.6 %fusion.26 = f32[1024,2048]{1,0:T(8,128)} fusion(bf16[1024,512]{1,0:T(8,128)(2,1)S(1)} %bitcast.125, bf16[512,2048]{1,0:T(8,128)(2,1)S(1)} %bitcast.124), kind=kOutput, calls=%fused_computation.77 | convolution fusion | flops 2147483648 | bytes 11534336 | tf_op jit(solution)/shard_map/dot_general | solution.py:59
  135.9 1.6 all-to-all-done.3
  137.5 7.7 %add_convert_fusion = bf16[1024,2048]{1,0:T(8,128)(2,1)} fusion(f32[1024,2048]{1,0:T(8,128)} %fusion.26, bf16[1024,512]{1,0:T(8,128)(2,1)S(1)} %bitcast.126, bf16[512,2048]{1,0:T(8,128)(2,1)S(1)} %bitcast.123), kind=kOutput, calls=%fused_computation.1 | convolution fusion | flops 2151677952 | bytes 15728640 | tf_op jit(solution)/shard_map/dot_general | solution.py:59
  145.3 48.4 %reduce-scatter.2.cloned.1.call-done = bf16[256,2048]{1,0:T(8,128)(2,1)} async-done(((bf16[1024,2048]{1,0:T(8,128)(2,1)}), bf16[256,2048]{1,0:T(8,128)(2,1)}) %reduce-scatter.2.cloned.1.call-update) | async-done | bytes 1048592 | tf_op jit(solution)/shard_map/reduce_scatter | solution.py:64
  193.6 1.3 copy.63
  194.9 31.2 %all_to_all.27 = bf16[8,256,256]{2,1,0:T(8,128)(2,1)S(1)} all-to-all(bf16[8,256,256]{2,1,0:T(8,128)(2,1)S(1)} %bitcast.120), channel_id=1, replica_groups=mesh['branch'=2,'head'=4,'y'=4,'zl'=4,'core'=2] {'zl','core'}, dimensions={0} | all-to-all | bytes 2097152 | tf_op jit(solution)/shard_map/all_to_all | solution.py:68
  226.1 1.0 copy.66
  (43 shorter events, 4.3 us)
Async XLA Ops:
  6.5 71.9 %copy-start = (bf16[256,128]{1,0:T(8,128)(2,1)S(1)}, bf16[256,128]{1,0:T(8,128)(2,1)}, u32[]{:S(2)}) copy-start(bf16[256,128]{1,0:T(8,128)(2,1)} %param.9) | copy-start | bytes 196612
  6.5 121.1 %all-gather.2.cloned.1.call-start = ((), (), s32[]{:S(2)}) async-start(), calls=%async_computation.6 | async-start | bytes 4718592 | tf_op jit(solution)/shard_map/all_gather | solution.py:36
  68.3 8.7 %copy-start.7 = (s32[1,32]{1,0:T(1,128)S(1)}, s32[1,32]{1,0:T(1,128)}, u32[]{:S(2)}) copy-start(s32[1,32]{1,0:T(1,128)} %param.13) | copy-start | bytes 388
  68.3 8.9 %copy-start.5 = (bf16[256,1024]{1,0:T(8,128)(2,1)S(1)}, bf16[256,1024]{1,0:T(8,128)(2,1)}, u32[]{:S(2)}) copy-start(bf16[256,1024]{1,0:T(8,128)(2,1)} %param.8) | copy-start | bytes 1572868
  86.6 10.5 %copy-start.2 = (bf16[2048,2,1,128]{3,0,2,1:T(8,128)(2,1)}, bf16[2048,2,1,128]{3,0,2,1:T(8,128)(2,1)S(1)}, u32[]{:S(2)}) copy-start(bf16[2048,2,1,128]{3,0,2,1:T(8,128)(2,1)S(1)} %copy_select_fusion) | copy-start | bytes 3145732
  90.9 5.9 %copy-start.6 = (bf16[256,128]{1,0:T(8,128)(2,1)S(1)}, bf16[256,128]{1,0:T(8,128)(2,1)}, u32[]{:S(2)}) copy-start(bf16[256,128]{1,0:T(8,128)(2,1)} %param.10) | copy-start | bytes 196612
  99.1 18.8 %all-to-all-start.2 = ((bf16[4,256,512]{2,1,0:T(8,128)(2,1)}), bf16[4,256,512]{2,1,0:T(8,128)(2,1)S(1)}, u32[]{:S(2)}, u32[]{:S(2)}) async-start(bf16[4,256,512]{2,1,0:T(8,128)(2,1)} %broadcast_in_dim.127), calls=%async_computation.2 | async-start | bytes 2097152 | tf_op jit(solution)/shard_map/all_to_all | solution.py:96
  118.0 9.7 %copy-start.3 = (bf16[4,256,512]{2,1,0:T(8,128)(2,1)}, bf16[4,256,512]{2,1,0:T(8,128)(2,1)S(1)}, u32[]{:S(2)}) copy-start(bf16[4,256,512]{2,1,0:T(8,128)(2,1)S(1)} %all-to-all-done.2) | copy-start | bytes 3145732
  119.2 18.3 %all-to-all-start.3 = ((bf16[4,256,512]{2,1,0:T(8,128)(2,1)}), bf16[4,256,512]{2,1,0:T(8,128)(2,1)S(1)}, u32[]{:S(2)}, u32[]{:S(2)}) async-start(bf16[4,256,512]{2,1,0:T(8,128)(2,1)} %broadcast_in_dim.129), calls=%async_computation.3 | async-start | bytes 2097152 | tf_op jit(solution)/shard_map/all_to_all | solution.py:96
  124.8 68.9 %reduce-scatter.2.cloned.1.call-start = ((), (), s32[]{:S(2)}) async-start(), calls=%async_computation.7 | async-start | bytes 5242880 | tf_op jit(solution)/shard_map/reduce_scatter | solution.py:64
  127.6 2.7 %copy-start.4 = (bf16[4,256,512]{2,1,0:T(8,128)(2,1)S(1)}, bf16[4,256,512]{2,1,0:T(8,128)(2,1)}, u32[]{:S(2)}) copy-start(bf16[4,256,512]{2,1,0:T(8,128)(2,1)} %copy-done.3) | copy-start | bytes 3145732
  137.5 89.6 %copy-start.1 = (bf16[256,128]{1,0:T(8,128)(2,1)S(1)}, bf16[256,128]{1,0:T(8,128)(2,1)}, u32[]{:S(2)}) copy-start(bf16[256,128]{1,0:T(8,128)(2,1)} %param.9) | copy-start | bytes 196612
Sparse Core Ops, SparseCore 0:
  77.1 50.4 all-gather.1
  145.4 48.1 reduce-scatter.1

commit v13 on v10

--- a/solution.py
+++ b/solution.py
@@ -31,14 +31,16 @@
 
     kv_local = jnp.concatenate([cache_keys, cache_values], axis=-1)
     kv_chips = gather_by_all_to_all(kv_local, ("branch", "y", "zl"))
-    kv_all = gather_by_all_to_all(kv_chips, "core")
+    n_core = lax.axis_size("core")
+    kv_other = lax.ppermute(kv_chips, "core", [(c, (c + 1) % n_core) for c in range(n_core)])
+    kv_all = jnp.concatenate([kv_chips, kv_other], axis=0)
     out_weight, kv_all = lax.optimization_barrier((out_weight, kv_all))
     w_cols = lax.all_gather(out_weight, ZC, axis=1, tiled=True)
     pages_here = cache_keys.shape[0]
-    n_core = lax.axis_size("core")
     n_chips = lax.axis_size(("branch", "y", "zl"))
     owner = block_table[0] // pages_here
-    position = ((owner % n_core) * n_chips + owner // n_core) * pages_here + block_table[0] % pages_here
+    other_core = (owner % n_core != lax.axis_index("core")).astype(jnp.int32)
+    position = (other_core * n_chips + owner // n_core) * pages_here + block_table[0] % pages_here
     kv_sel = jnp.take(kv_all, position, axis=0)
     anc_len = slot_count * PAGE_TOK
     kv_sel = kv_sel.reshape(anc_len, 2, kv_here, HD)

time: 227 us -> 225 us (level)
  blocking collectives: 130 us -> 121 us
  waiting for transfers between devices: 53.6 us -> 57.7 us
  other arithmetic: 6.93 us -> 9.25 us
    all_to_all x3 -> x2, blocking collectives: 98.6 us -> 90.3 us  [gather_by_all_to_all(): arrived = lax.all_to_all(spread, axes, 0, 0, tiled=True)]
    ppermute x0 -> x1, waiting for transfers between devices: none -> 4.16 us  [shards(): lax.ppermute(kv_chips, 'core', [(c, (c + 1) % n_core) for c in range(n_co...]
    concatenate x0 -> x1, other arithmetic: none -> 2.33 us  [shards(): kv_all = jnp.concatenate([kv_chips, kv_other], axis=0)]
  transfers between devices with their start and end apart: 2 -> 3, of which waited for: 2 -> 3; matrix products, arithmetic and copies ran while one was open for 7% -> 7% of each run, Pallas kernels for 0% -> 0%
where the time goes in v13:
time: 225 us; the launch traced here: 224 us
  blocking collectives  121 us (54%)
  waiting for transfers between devices  57.7 us (26%)
  matrix products  14.7 us (7%)
  between operations  14.2 us (6%)
  other arithmetic  9.25 us (4%)
  local copies, waits for them, and re-layouts  6.36 us (3%)
    all_to_all x2, blocking collectives, gather_by_all_to_all(): arrived = lax.all_to_all(spread, axes, 0, 0, tiled=True)  90.3 us
    reduce_scatter x1, waiting for transfers between devices, shards(): lax.psum_scatter(partial_term, 'head', scatter_dimension=0, tiled=True)  50.1 us
    all_to_all x1, blocking collectives, shards(): arrived = lax.all_to_all(summed, ZC, 0, 0, tiled=True)  31.2 us
    dot_general x1, matrix products, shards(): jnp.dot(attn_rows, w_cols, preferred_element_type=jnp.float32)  8.21 us
    reduce_sum x1, other arithmetic, shards(): jnp.sum(anc_w.astype(jnp.float32), axis=-1)  4.9 us
  transfers between devices with their start and end apart: 3, of which 3 were waited for; matrix products, arithmetic and copies ran while one was open for 7% of the time, Pallas kernels for 0%

profile of v13, /device:TPU:24, one launch (start us, length us, event | category | flops | bytes accessed | tf_op | source)
XLA Modules:
  0.0 223.8 jit_solution(3072295578543433506)
XLA Ops:
  6.5 0.8 pad_maximum_fusion.1
  7.4 0.2 broadcast_in_dim.79
  7.6 60.7 %all_to_all.15 = bf16[32,2,64,256]{3,2,1,0:T(8,128)(2,1)S(1)} all-to-all(bf16[32,2,64,256]{3,2,1,0:T(8,128)(2,1)S(1)} %broadcast_in_dim.79), channel_id=1, replica_groups=mesh['branch'=2,'head'=4,'y'=4,'zl'=4,'core'=2] {'branch','y','zl'}, dimensions={0} | all-to-all | bytes 4194304 | tf_op jit(solution)/shard_map/all_to_all | solution.py:88
  68.3 4.2 %collective-permute-done = bf16[64,64,256]{2,1,0:T(8,128)(2,1)S(1)} collective-permute-done((bf16[64,64,256]{2,1,0:T(8,128)(2,1)S(1)}, bf16[64,64,256]{2,1,0:T(8,128)(2,1)S(1)}, u32[]{:S(2)}, u32[]{:S(2)}) %collective-permute-start) | collective-permute-done | bytes 2097184 | tf_op jit(solution)/shard_map/ppermute | solution.py:35
  72.5 2.3 %pad_maximum_fusion = bf16[128,64,256]{2,1,0:T(8,128)(2,1)} fusion(bf16[64,64,256]{2,1,0:T(8,128)(2,1)S(1)} %collective-permute-done, bf16[64,64,256]{2,1,0:T(8,128)(2,1)S(1)} %bitcast.91), kind=kLoop, calls=%fused_computation.5 | loop fusion | flops 2097152 | bytes 8388608 | tf_op jit(solution)/shard_map/concatenate | solution.py:36
  75.1 0.1 copy.39
  75.9 1.9 select_reduce_fusion.1
  77.8 2.8 %gather_fusion = bf16[32,64,256]{2,1,0:T(8,128)(2,1)S(1)} fusion(bf16[128,64,256]{2,1,0:T(8,128)(2,1)} %pad_maximum_fusion, s32[1024]{0:T(1024)S(1)} %pad_clamp_fusion), kind=kCustom, calls=%fused_computation | custom fusion | bytes 2097280 | tf_op jit(solution)/shard_map/jit(_take)/gather | solution.py:44
  80.6 0.3 gather.7
  80.9 0.7 copy_select_fusion
  81.6 2.7 %select_reduce_fusion = (f32[8,256]{1,0:T(8,128)S(1)}, f32[2048,8,256]{2,0,1:T(8,128)S(1)}) fusion(pred[2048]{0:T(1024)(128)(4,1)S(1)} %iota_compare_fusion.1, bf16[256,1,8,128]{3,2,0,1:T(8,128)(2,1)S(1)} %bitcast.95, bf16[2048,2,1,128]{3,0,2,1:T(8,128)(2,1)S(1)} %copy_select_fusion), kind=kOutput, calls=%fused_computation.3 | convolution fusion | flops 1086322688 | bytes 17836032 | tf_op jit(solution)/shard_map/kgnd,kjd->kgnj/dot_general | solution.py:54
  84.4 0.4 convert_reduce_fusion.1
  84.8 4.9 %convert_reduce_fusion = (f32[8,256]{1,0:T(8,128)S(1)}, bf16[8,256,2048]{1,2,0:T(8,128)(2,1)S(1)}) fusion(f32[8,256]{1,0:T(8,128)S(1)} %max.9, f32[2048,8,256]{2,0,1:T(8,128)S(1)} %get-tuple-element.14, pred[2048]{0:T(1024)(128)(4,1)S(1)} %iota_compare_fusion.1), kind=kLoop, calls=%fused_computation.1 | loop fusion | flops 25163776 | bytes 25184256 | tf_op jit(solution)/shard_map/reduce_sum | solution.py:66
  89.7 1.3 fusion.3
  91.1 0.6 fusion.2
  91.6 0.2 copy.30
  91.8 0.3 broadcast_in_dim.85
  92.1 29.6 %all_to_all.16 = bf16[4,256,1024]{2,1,0:T(8,128)(2,1)S(1)} all-to-all(bf16[4,256,1024]{2,1,0:T(8,128)(2,1)S(1)} %broadcast_in_dim.85), channel_id=1, replica_groups=mesh['branch'=2,'head'=4,'y'=4,'zl'=4,'core'=2] {'y'}, dimensions={0} | all-to-all | bytes 4194304 | tf_op jit(solution)/shard_map/all_to_all | solution.py:88
  121.7 3.5 %all-gather.2.cloned.1.call-done = bf16[1024,2048]{1,0:T(8,128)(2,1)} async-done(((bf16[1024,256]{1,0:T(8,128)(2,1)}), bf16[1024,2048]{1,0:T(8,128)(2,1)}) %all-gather.2.cloned.1.call-update) | async-done | bytes 4194320 | tf_op jit(solution)/shard_map/all_gather | solution.py:38
  125.2 8.2 %convolution_convert_fusion = bf16[1024,2048]{1,0:T(8,128)(2,1)} fusion(bf16[1024,1024]{1,0:T(8,128)(2,1)S(1)} %bitcast.96, bf16[1024,2048]{1,0:T(8,128)(2,1)} %all-gather.2.cloned.1.call-done), kind=kOutput, calls=%fused_computation.6 | convolution fusion | flops 4297064448 | bytes 10485760 | tf_op jit(solution)/shard_map/dot_general | solution.py:74
  133.4 50.1 %reduce-scatter.2.cloned.1.call-done = bf16[256,2048]{1,0:T(8,128)(2,1)} async-done(((bf16[1024,2048]{1,0:T(8,128)(2,1)}), bf16[256,2048]{1,0:T(8,128)(2,1)}) %reduce-scatter.2.cloned.1.call-update) | async-done | bytes 1048592 | tf_op jit(solution)/shard_map/reduce_scatter | solution.py:77
  183.5 1.3 copy.54
  184.8 31.2 %all_to_all.17 = bf16[8,256,256]{2,1,0:T(8,128)(2,1)S(1)} all-to-all(bf16[8,256,256]{2,1,0:T(8,128)(2,1)S(1)} %bitcast.92), channel_id=1, replica_groups=mesh['branch'=2,'head'=4,'y'=4,'zl'=4,'core'=2] {'zl','core'}, dimensions={0} | all-to-all | bytes 2097152 | tf_op jit(solution)/shard_map/all_to_all | solution.py:81
  216.0 1.0 copy.57
  (24 shorter events, 0.4 us)
Async XLA Ops:
  6.5 69.4 %copy-start = (bf16[256,128]{1,0:T(8,128)(2,1)S(1)}, bf16[256,128]{1,0:T(8,128)(2,1)}, u32[]{:S(2)}) copy-start(bf16[256,128]{1,0:T(8,128)(2,1)} %param.9) | copy-start | bytes 196612
  6.5 118.7 %all-gather.2.cloned.1.call-start = ((), (), s32[]{:S(2)}) async-start(), calls=%async_computation.4 | async-start | bytes 4718592 | tf_op jit(solution)/shard_map/all_gather | solution.py:38
  68.3 6.6 %copy-start.4 = (s32[1,32]{1,0:T(1,128)S(1)}, s32[1,32]{1,0:T(1,128)}, u32[]{:S(2)}) copy-start(s32[1,32]{1,0:T(1,128)} %param.13) | copy-start | bytes 388
  68.3 6.8 %copy-start.2 = (bf16[256,1024]{1,0:T(8,128)(2,1)S(1)}, bf16[256,1024]{1,0:T(8,128)(2,1)}, u32[]{:S(2)}) copy-start(bf16[256,1024]{1,0:T(8,128)(2,1)} %param.8) | copy-start | bytes 1572868
  68.3 4.2 %collective-permute-start = (bf16[64,64,256]{2,1,0:T(8,128)(2,1)S(1)}, bf16[64,64,256]{2,1,0:T(8,128)(2,1)S(1)}, u32[]{:S(2)}, u32[]{:S(2)}) collective-permute-start(bf16[64,64,256]{2,1,0:T(8,128)(2,1)S(1)} %bitcast.90), channel_id=1, source_target_pairs={{0,1},{1,0},{2,3},{3,2},{4,5},{5,4},{6,7},{7,6},{8,9},{9,8},{10,11... | collective-permute-start | bytes 6291464 | tf_op jit(solution)/shard_map/ppermute | solution.py:35
  74.8 108.7 %reduce-scatter.2.cloned.1.call-start = ((), (), s32[]{:S(2)}) async-start(), calls=%async_computation.5 | async-start | bytes 5242880 | tf_op jit(solution)/shard_map/reduce_scatter | solution.py:77
  81.6 2.8 %copy-start.1 = (f32[8,256,256]{1,2,0:T(8,128)S(1)}, f32[8,256,256]{1,2,0:T(8,128)}, u32[]{:S(2)}) copy-start(f32[8,256,256]{1,2,0:T(8,128)} %get-tuple-element.12) | copy-start | bytes 6291460
  89.7 1.3 copy-start.3
Sparse Core Ops, SparseCore 0:
  74.9 50.2 all-gather.1
  133.6 49.9 reduce-scatter.1

commit v14 on v13

--- a/solution.py
+++ b/solution.py
@@ -74,12 +74,37 @@
     partial_term = jnp.dot(attn_rows, w_cols, preferred_element_type=jnp.float32).astype(
         jnp.bfloat16
     )
-    summed = lax.psum_scatter(partial_term, "head", scatter_dimension=0, tiled=True)
+    summed = ring_reduce_scatter(partial_term, "head")
     n_zc = lax.axis_size(ZC)
     cols = out_weight.shape[1]
     summed = summed.reshape(row_count, n_zc, cols).transpose(1, 0, 2)
     arrived = lax.all_to_all(summed, ZC, 0, 0, tiled=True)
     return arrived.reshape(n_zc * row_count, cols)
+
+
+def ring_reduce_scatter(x, axis):
+    n = lax.axis_size(axis)
+    i = lax.axis_index(axis)
+    blocks = x.reshape(n, x.shape[0] // n, x.shape[1])
+    half = x.shape[1] // 2
+    ahead, behind = blocks[:, :, :half], blocks[:, :, half:]
+
+    def block(part, offset):
+        return lax.dynamic_index_in_dim(part, (i + offset + 2 * n) % n, axis=0, keepdims=False)
+
+    forward = [(j, (j + 1) % n) for j in range(n)]
+    backward = [(j, (j - 1) % n) for j in range(n)]
+    up, down = block(ahead, -1), block(behind, 1)
+    for step in range(n - 1):
+        came_up = lax.ppermute(up, axis, forward)
+        came_down = lax.ppermute(down, axis, backward)
+        up = (came_up.astype(jnp.float32) + block(ahead, -step - 2).astype(jnp.float32)).astype(
+            jnp.bfloat16
+        )
+        down = (came_down.astype(jnp.float32) + block(behind, step + 2).astype(jnp.float32)).astype(
+            jnp.bfloat16
+        )
+    return jnp.concatenate([up, down], axis=1)
 
 
 def gather_by_all_to_all(x, axes):

time: 225 us -> 228 us (1.013)
  blocking collectives: 121 us -> 90.5 us
  starting transfers between devices: 0.05 us -> 15.8 us
  other arithmetic: 9.25 us -> 18.5 us
  waiting for transfers between devices: 57.7 us -> 65.4 us
  local copies, waits for them, and re-layouts: 6.36 us -> 9.11 us
    reduce_scatter x1 -> x0, waiting for transfers between devices: 50.1 us -> none  [shards(): lax.psum_scatter(partial_term, 'head', scatter_dimension=0, tiled=True)]
    ppermute x0 -> x6, waiting for transfers between devices: none -> 34.8 us  [the longest x3 29 us: ring_reduce_scatter(): came_down = lax.ppermute(down, axis, backward)]
    all_to_all x2 -> x1, blocking collectives: 90.3 us -> 60.7 us  [gather_by_all_to_all(): arrived = lax.all_to_all(spread, axes, 0, 0, tiled=True)]
    all_to_all x0 -> x1, waiting for transfers between devices: none -> 24.8 us  [gather_by_all_to_all(): arrived = lax.all_to_all(spread, axes, 0, 0, tiled=True)]
    ppermute x0 -> x6, starting transfers between devices: none -> 10.4 us  [the longest x3 10.4 us: ring_reduce_scatter(): came_down = lax.ppermute(down, axis, backward)]
    convert_element_type x0 -> x6, other arithmetic: none -> 9.14 us  [the longest x3 5.29 us: ring_reduce_scatter(): (came_up.astype(jnp.float32) + block(ahead, -step - 2).astype(jnp.float32...]
    all_to_all x0 -> x1, starting transfers between devices: none -> 5.34 us  [gather_by_all_to_all(): arrived = lax.all_to_all(spread, axes, 0, 0, tiled=True)]
  transfers between devices with their start and end apart: 3 -> 9, of which waited for: 3 -> 9; matrix products, arithmetic and copies ran while one was open for 7% -> 12% of each run, Pallas kernels for 0% -> 0%
where the time goes in v14:
time: 228 us; the launch traced here: 227 us
  blocking collectives  90.5 us (40%)
  waiting for transfers between devices  65.4 us (29%)
  other arithmetic  18.5 us (8%)
  starting transfers between devices  15.8 us (7%)
  between operations  14.3 us (6%)
  matrix products  13.4 us (6%)
  local copies, waits for them, and re-layouts  9.11 us (4%)
    all_to_all x1, blocking collectives, gather_by_all_to_all(): arrived = lax.all_to_all(spread, axes, 0, 0, tiled=True)  60.7 us
    all_to_all x1, blocking collectives, shards(): arrived = lax.all_to_all(summed, ZC, 0, 0, tiled=True)  29.8 us
    ppermute x3, waiting for transfers between devices, ring_reduce_scatter(): came_down = lax.ppermute(down, axis, backward)  29 us
    all_to_all x1, waiting for transfers between devices, gather_by_all_to_all(): arrived = lax.all_to_all(spread, axes, 0, 0, tiled=True)  24.8 us
    ppermute x3, starting transfers between devices, ring_reduce_scatter(): came_down = lax.ppermute(down, axis, backward)  10.4 us
    dot_general x1, matrix products, shards(): jnp.dot(attn_rows, w_cols, preferred_element_type=jnp.float32)  6.88 us
    ppermute x3, waiting for transfers between devices, ring_reduce_scatter(): came_up = lax.ppermute(up, axis, forward)  5.81 us
    all_to_all x1, starting transfers between devices, gather_by_all_to_all(): arrived = lax.all_to_all(spread, axes, 0, 0, tiled=True)  5.34 us
  transfers between devices with their start and end apart: 9, of which 9 were waited for; matrix products, arithmetic and copies ran while one was open for 12% of the time, Pallas kernels for 0%

profile of v14, /device:TPU:24, one launch (start us, length us, event | category | flops | bytes accessed | tf_op | source)
XLA Modules:
  0.0 226.9 jit_solution(9180773469412216024)
XLA Ops:
  7.6 60.7 %all_to_all.15 = bf16[32,2,64,256]{3,2,1,0:T(8,128)(2,1)S(1)} all-to-all(bf16[32,2,64,256]{3,2,1,0:T(8,128)(2,1)S(1)} %broadcast_in_dim.79), channel_id=1, replica_groups=mesh['branch'=2,'head'=4,'y'=4,'zl'=4,'core'=2] {'branch','y','zl'}, dimensions={0} | all-to-all | bytes 4194304 | tf_op jit(solution)/shard_map/all_to_all | solution.py:113
  68.3 4.2 %collective-permute-done = bf16[64,64,256]{2,1,0:T(8,128)(2,1)S(1)} collective-permute-done((bf16[64,64,256]{2,1,0:T(8,128)(2,1)S(1)}, bf16[64,64,256]{2,1,0:T(8,128)(2,1)S(1)}, u32[]{:S(2)}, u32[]{:S(2)}) %collective-permute-start) | collective-permute-done | bytes 2097184 | tf_op jit(solution)/shard_map/ppermute | solution.py:35
  72.5 2.3 %pad_maximum_fusion = bf16[128,64,256]{2,1,0:T(8,128)(2,1)} fusion(bf16[64,64,256]{2,1,0:T(8,128)(2,1)S(1)} %collective-permute-done, bf16[64,64,256]{2,1,0:T(8,128)(2,1)S(1)} %bitcast.114), kind=kLoop, calls=%fused_computation.5 | loop fusion | flops 2097152 | bytes 8388608 | tf_op jit(solution)/shard_map/concatenate | solution.py:36
  75.9 1.9 select_reduce_fusion.1
  77.7 2.8 %gather_fusion = bf16[32,64,256]{2,1,0:T(8,128)(2,1)S(1)} fusion(bf16[128,64,256]{2,1,0:T(8,128)(2,1)} %pad_maximum_fusion, s32[1024]{0:T(1024)S(1)} %pad_clamp_fusion), kind=kCustom, calls=%fused_computation | custom fusion | bytes 2097280 | tf_op jit(solution)/shard_map/jit(_take)/gather | solution.py:44
  81.5 2.7 %select_reduce_fusion = (f32[8,256]{1,0:T(8,128)S(1)}, f32[2048,8,256]{2,0,1:T(8,128)S(1)}) fusion(pred[2048]{0:T(1024)(128)(4,1)S(1)} %iota_compare_fusion.1, bf16[256,1,8,128]{3,2,0,1:T(8,128)(2,1)S(1)} %bitcast.120, bf16[2048,2,1,128]{3,0,2,1:T(8,128)(2,1)S(1)} %copy_select_fusion), kind=kOutput, calls=%fused_computation.3 | convolution fusion | flops 1086322688 | bytes 17836032 | tf_op jit(solution)/shard_map/kgnd,kjd->kgnj/dot_general | solution.py:54
  84.8 4.9 %convert_reduce_fusion = (f32[8,256]{1,0:T(8,128)S(1)}, bf16[8,256,2048]{1,2,0:T(8,128)(2,1)S(1)}) fusion(f32[8,256]{1,0:T(8,128)S(1)} %max.9, f32[2048,8,256]{2,0,1:T(8,128)S(1)} %get-tuple-element.16, pred[2048]{0:T(1024)(128)(4,1)S(1)} %iota_compare_fusion.1), kind=kLoop, calls=%fused_computation.1 | loop fusion | flops 25163776 | bytes 25184256 | tf_op jit(solution)/shard_map/reduce_sum | solution.py:66
  89.7 1.3 fusion.9
  91.8 1.6 broadcast_in_dim.85
  93.4 5.3 %all-to-all-start.1 = ((bf16[4,256,1024]{2,1,0:T(8,128)(2,1)}), bf16[4,256,1024]{2,1,0:T(8,128)(2,1)S(1)}, u32[]{:S(2)}, u32[]{:S(2)}) async-start(bf16[4,256,1024]{2,1,0:T(8,128)(2,1)} %broadcast_in_dim.85), calls=%async_computation.1 | async-start | bytes 4194304 | tf_op jit(solution)/shard_map/all_to_all | solution.py:113
  98.7 24.8 %all-to-all-done.1 = bf16[4,256,1024]{2,1,0:T(8,128)(2,1)S(1)} async-done(((bf16[4,256,1024]{2,1,0:T(8,128)(2,1)}), bf16[4,256,1024]{2,1,0:T(8,128)(2,1)S(1)}, u32[]{:S(2)}, u32[]{:S(2)}) %all-to-all-start.1) | async-done | bytes 2097184 | tf_op jit(solution)/shard_map/all_to_all | solution.py:113
  123.6 1.7 all-gather.2.cloned.1.call-done
  125.2 6.9 %convolution_convert_fusion = bf16[1024,2048]{1,0:T(8,128)(2,1)S(1)} fusion(bf16[1024,1024]{1,0:T(8,128)(2,1)S(1)} %bitcast.121, bf16[1024,2048]{1,0:T(8,128)(2,1)} %all-gather.2.cloned.1.call-done), kind=kOutput, calls=%fused_computation.6 | convolution fusion | flops 4297064448 | bytes 10485760 | tf_op jit(solution)/shard_map/dot_general | solution.py:74
  134.0 2.8 %collective-permute-start.4 = (bf16[256,1024]{1,0:T(8,128)(2,1)S(1)}, bf16[256,1024]{1,0:T(8,128)(2,1)S(1)}, u32[]{:S(2)}, u32[]{:S(2)}) collective-permute-start(bf16[256,1024]{1,0:T(8,128)(2,1)S(1)} %dynamic-slice_bitcast_fusion), channel_id=1, source_target_pairs={{0,96},{32,0},{64,32},{96,64},{1,97},{33,1},{65,33},{97,65},{2,98}... | collective-permute-start | bytes 1572872 | tf_op jit(solution)/shard_map/ppermute | solution.py:100
  137.6 10.7 %collective-permute-done.4 = bf16[256,1024]{1,0:T(8,128)(2,1)S(1)} collective-permute-done((bf16[256,1024]{1,0:T(8,128)(2,1)S(1)}, bf16[256,1024]{1,0:T(8,128)(2,1)S(1)}, u32[]{:S(2)}, u32[]{:S(2)}) %collective-permute-start.4) | collective-permute-done | bytes 524320 | tf_op jit(solution)/shard_map/ppermute | solution.py:100
  149.5 3.8 %collective-permute-start.5 = (bf16[256,1024]{1,0:T(8,128)(2,1)S(1)}, bf16[256,1024]{1,0:T(8,128)(2,1)}, u32[]{:S(2)}, u32[]{:S(2)}) collective-permute-start(bf16[256,1024]{1,0:T(8,128)(2,1)S(1)} %fusion.5), channel_id=1, source_target_pairs={{0,96},{32,0},{64,32},{96,64},{1,97},{33,1},{65,33},{97,65},{2,98}... | collective-permute-start | bytes 1572872 | tf_op jit(solution)/shard_map/ppermute | solution.py:100
  153.4 2.0 fusion.8
  155.4 9.8 %collective-permute-done.5 = bf16[256,1024]{1,0:T(8,128)(2,1)} collective-permute-done((bf16[256,1024]{1,0:T(8,128)(2,1)S(1)}, bf16[256,1024]{1,0:T(8,128)(2,1)}, u32[]{:S(2)}, u32[]{:S(2)}) %collective-permute-start.5) | collective-permute-done | bytes 524320 | tf_op jit(solution)/shard_map/ppermute | solution.py:100
  165.2 1.4 fusion.4
  166.6 3.9 %collective-permute-start.6 = (bf16[256,1024]{1,0:T(8,128)(2,1)S(1)}, bf16[256,1024]{1,0:T(8,128)(2,1)S(1)}, u32[]{:S(2)}, u32[]{:S(2)}) collective-permute-start(bf16[256,1024]{1,0:T(8,128)(2,1)S(1)} %fusion.4), channel_id=1, source_target_pairs={{0,96},{32,0},{64,32},{96,64},{1,97},{33,1},{65,33},{97,65},{2,98}... | collective-permute-start | bytes 1572872 | tf_op jit(solution)/shard_map/ppermute | solution.py:100
  171.1 2.0 fusion.7
  173.1 8.5 %collective-permute-done.6 = bf16[256,1024]{1,0:T(8,128)(2,1)S(1)} collective-permute-done((bf16[256,1024]{1,0:T(8,128)(2,1)S(1)}, bf16[256,1024]{1,0:T(8,128)(2,1)S(1)}, u32[]{:S(2)}, u32[]{:S(2)}) %collective-permute-start.6) | collective-permute-done | bytes 524320 | tf_op jit(solution)/shard_map/ppermute | solution.py:100
  182.8 5.1 %collective-permute-done.3 = bf16[256,1024]{1,0:T(8,128)(2,1)} collective-permute-done((bf16[256,1024]{1,0:T(8,128)(2,1)}, bf16[256,1024]{1,0:T(8,128)(2,1)}, u32[]{:S(2)}, u32[]{:S(2)}) %collective-permute-start.3) | collective-permute-done | bytes 524320 | tf_op jit(solution)/shard_map/ppermute | solution.py:99
  189.3 29.8 %all_to_all.16 = bf16[8,256,256]{2,1,0:T(8,128)(2,1)S(1)} all-to-all(bf16[8,256,256]{2,1,0:T(8,128)(2,1)S(1)} %bitcast.117), channel_id=1, replica_groups=mesh['branch'=2,'head'=4,'y'=4,'zl'=4,'core'=2] {'zl','core'}, dimensions={0} | all-to-all | bytes 2097152 | tf_op jit(solution)/shard_map/all_to_all | solution.py:81
  (48 shorter events, 11.8 us)
Async XLA Ops:
  6.5 69.3 %copy-start = (bf16[256,128]{1,0:T(8,128)(2,1)S(1)}, bf16[256,128]{1,0:T(8,128)(2,1)}, u32[]{:S(2)}) copy-start(bf16[256,128]{1,0:T(8,128)(2,1)} %param.9) | copy-start | bytes 196612
  6.5 118.7 %all-gather.2.cloned.1.call-start = ((), (), s32[]{:S(2)}) async-start(), calls=%async_computation.3 | async-start | bytes 4718592 | tf_op jit(solution)/shard_map/all_gather | solution.py:38
  68.3 6.5 %copy-start.4 = (bf16[256,1024]{1,0:T(8,128)(2,1)S(1)}, bf16[256,1024]{1,0:T(8,128)(2,1)}, u32[]{:S(2)}) copy-start(bf16[256,1024]{1,0:T(8,128)(2,1)} %param.8) | copy-start | bytes 1572868
  68.3 7.3 %copy-start.6 = (s32[1,32]{1,0:T(1,128)S(1)}, s32[1,32]{1,0:T(1,128)}, u32[]{:S(2)}) copy-start(s32[1,32]{1,0:T(1,128)} %param.13) | copy-start | bytes 388
  68.3 4.2 %collective-permute-start = (bf16[64,64,256]{2,1,0:T(8,128)(2,1)S(1)}, bf16[64,64,256]{2,1,0:T(8,128)(2,1)S(1)}, u32[]{:S(2)}, u32[]{:S(2)}) collective-permute-start(bf16[64,64,256]{2,1,0:T(8,128)(2,1)S(1)} %bitcast.113), channel_id=1, source_target_pairs={{0,1},{1,0},{2,3},{3,2},{4,5},{5,4},{6,7},{7,6},{8,9},{9,8},{10,11... | collective-permute-start | bytes 6291464 | tf_op jit(solution)/shard_map/ppermute | solution.py:35
  81.5 2.8 %copy-start.3 = (f32[8,256,256]{1,2,0:T(8,128)S(1)}, f32[8,256,256]{1,2,0:T(8,128)}, u32[]{:S(2)}) copy-start(f32[8,256,256]{1,2,0:T(8,128)} %get-tuple-element.14) | copy-start | bytes 6291460
  89.7 1.4 copy-start.5
  93.4 30.2 %all-to-all-start.1 = ((bf16[4,256,1024]{2,1,0:T(8,128)(2,1)}), bf16[4,256,1024]{2,1,0:T(8,128)(2,1)S(1)}, u32[]{:S(2)}, u32[]{:S(2)}) async-start(bf16[4,256,1024]{2,1,0:T(8,128)(2,1)} %broadcast_in_dim.85), calls=%async_computation.1 | async-start | bytes 4194304 | tf_op jit(solution)/shard_map/all_to_all | solution.py:113
  132.6 1.3 copy-start.2
  134.0 14.3 %collective-permute-start.4 = (bf16[256,1024]{1,0:T(8,128)(2,1)S(1)}, bf16[256,1024]{1,0:T(8,128)(2,1)S(1)}, u32[]{:S(2)}, u32[]{:S(2)}) collective-permute-start(bf16[256,1024]{1,0:T(8,128)(2,1)S(1)} %dynamic-slice_bitcast_fusion), channel_id=1, source_target_pairs={{0,96},{32,0},{64,32},{96,64},{1,97},{33,1},{65,33},{97,65},{2,98}... | collective-permute-start | bytes 1572872 | tf_op jit(solution)/shard_map/ppermute | solution.py:100
  137.6 15.8 %collective-permute-start.1 = (bf16[256,1024]{1,0:T(8,128)(2,1)}, bf16[256,1024]{1,0:T(8,128)(2,1)}, u32[]{:S(2)}, u32[]{:S(2)}) collective-permute-start(bf16[256,1024]{1,0:T(8,128)(2,1)} %dynamic-slice_bitcast_fusion.1), channel_id=1, source_target_pairs={{0,32},{32,64},{64,96},{96,0},{1,33},{33,65},{65,97},{97,1},{2,34}... | collective-permute-start | bytes 1572872 | tf_op jit(solution)/shard_map/ppermute | solution.py:99
  149.5 15.7 %collective-permute-start.5 = (bf16[256,1024]{1,0:T(8,128)(2,1)S(1)}, bf16[256,1024]{1,0:T(8,128)(2,1)}, u32[]{:S(2)}, u32[]{:S(2)}) collective-permute-start(bf16[256,1024]{1,0:T(8,128)(2,1)S(1)} %fusion.5), channel_id=1, source_target_pairs={{0,96},{32,0},{64,32},{96,64},{1,97},{33,1},{65,33},{97,65},{2,98}... | collective-permute-start | bytes 1572872 | tf_op jit(solution)/shard_map/ppermute | solution.py:100
  155.4 15.7 %collective-permute-start.2 = (bf16[256,1024]{1,0:T(8,128)(2,1)}, bf16[256,1024]{1,0:T(8,128)(2,1)}, u32[]{:S(2)}, u32[]{:S(2)}) collective-permute-start(bf16[256,1024]{1,0:T(8,128)(2,1)} %fusion.8), channel_id=1, source_target_pairs={{0,32},{32,64},{64,96},{96,0},{1,33},{33,65},{65,97},{97,1},{2,34}... | collective-permute-start | bytes 1572872 | tf_op jit(solution)/shard_map/ppermute | solution.py:99
  166.6 15.0 %collective-permute-start.6 = (bf16[256,1024]{1,0:T(8,128)(2,1)S(1)}, bf16[256,1024]{1,0:T(8,128)(2,1)S(1)}, u32[]{:S(2)}, u32[]{:S(2)}) collective-permute-start(bf16[256,1024]{1,0:T(8,128)(2,1)S(1)} %fusion.4), channel_id=1, source_target_pairs={{0,96},{32,0},{64,32},{96,64},{1,97},{33,1},{65,33},{97,65},{2,98}... | collective-permute-start | bytes 1572872 | tf_op jit(solution)/shard_map/ppermute | solution.py:100
  173.1 14.8 %collective-permute-start.3 = (bf16[256,1024]{1,0:T(8,128)(2,1)}, bf16[256,1024]{1,0:T(8,128)(2,1)}, u32[]{:S(2)}, u32[]{:S(2)}) collective-permute-start(bf16[256,1024]{1,0:T(8,128)(2,1)} %fusion.7), channel_id=1, source_target_pairs={{0,32},{32,64},{64,96},{96,0},{1,33},{33,65},{65,97},{97,1},{2,34}... | collective-permute-start | bytes 1572872 | tf_op jit(solution)/shard_map/ppermute | solution.py:99
  189.3 30.8 %copy-start.1 = (bf16[256,128]{1,0:T(8,128)(2,1)S(1)}, bf16[256,128]{1,0:T(8,128)(2,1)}, u32[]{:S(2)}) copy-start(bf16[256,128]{1,0:T(8,128)(2,1)} %param.9) | copy-start | bytes 196612
Sparse Core Ops, SparseCore 0:
  74.9 50.2 all-gather.1

commit v15 on v9

--- a/solution.py
+++ b/solution.py
@@ -30,10 +30,20 @@
     own_v = new_values.reshape(row_count, kv_here, HD).transpose(1, 0, 2)
 
     kv_local = jnp.concatenate([cache_keys, cache_values], axis=-1)
-    kv_all = gather_by_all_to_all(kv_local, ("branch",) + PAGE_AXES)
-    out_weight, kv_all = lax.optimization_barrier((out_weight, kv_all))
+    kv_chips = gather_by_all_to_all(kv_local, ("branch", "y", "zl"))
+    n_core = lax.axis_size("core")
+    pages_here = cache_keys.shape[0]
+    swap = [(c, (c + 1) % n_core) for c in range(n_core)]
+    partner_row = lax.ppermute(block_table, "core", swap)[0]
+    partner_pos = (partner_row // pages_here // n_core) * pages_here + partner_row % pages_here
+    from_partner = lax.ppermute(jnp.take(kv_chips, partner_pos, axis=0), "core", swap)
+    own_row = block_table[0]
+    owner = own_row // pages_here
+    own_pos = (owner // n_core) * pages_here + own_row % pages_here
+    other_core = owner % n_core != lax.axis_index("core")
+    kv_sel = jnp.where(other_core[:, None, None], from_partner, jnp.take(kv_chips, own_pos, axis=0))
+    out_weight, kv_sel = lax.optimization_barrier((out_weight, kv_sel))
     w_cols = lax.all_gather(out_weight, ZC, axis=1, tiled=True)
-    kv_sel = jnp.take(kv_all, block_table[0], axis=0)
     anc_len = slot_count * PAGE_TOK
     kv_sel = kv_sel.reshape(anc_len, 2, kv_here, HD)
     anc_k = kv_sel[:, 0].transpose(1, 0, 2)

time: 265 us -> 226 us (0.85)
  blocking collectives: 167 us -> 61.1 us
  waiting for transfers between devices: 54 us -> 104 us
  starting transfers between devices: 0.04 us -> 11.8 us
    all_to_all x2 -> x1, blocking collectives: 136 us -> 29.9 us  [gather_by_all_to_all(): arrived = lax.all_to_all(spread, axes, 0, 0, tiled=True)]
    all_to_all x0 -> x1, waiting for transfers between devices: none -> 48.5 us  [gather_by_all_to_all(): arrived = lax.all_to_all(spread, axes, 0, 0, tiled=True)]
    all_to_all x0 -> x1, starting transfers between devices: none -> 11.6 us  [gather_by_all_to_all(): arrived = lax.all_to_all(spread, axes, 0, 0, tiled=True)]
    ppermute x0 -> x2, waiting for transfers between devices: none -> 3.46 us  [the longest x1 2.31 us: shards(): lax.ppermute(jnp.take(kv_chips, partner_pos, axis=0), 'core', swap)]
  transfers between devices with their start and end apart: 2 -> 5, of which waited for: 2 -> 5; matrix products, arithmetic and copies ran while one was open for 6% -> 8% of each run, Pallas kernels for 0% -> 0%
where the time goes in v15:
time: 226 us; the launch traced here: 225 us
  waiting for transfers between devices  104 us (46%)
  blocking collectives  61.1 us (27%)
  matrix products  15.9 us (7%)
  between operations  14.3 us (6%)
  starting transfers between devices  11.8 us (5%)
  local copies, waits for them, and re-layouts  8.91 us (4%)
  other arithmetic  8.84 us (4%)
    reduce_scatter x1, waiting for transfers between devices, shards(): lax.psum_scatter(partial_term, 'head', scatter_dimension=0, tiled=True)  50.1 us
    all_to_all x1, waiting for transfers between devices, gather_by_all_to_all(): arrived = lax.all_to_all(spread, axes, 0, 0, tiled=True)  48.5 us
    all_to_all x1, blocking collectives, shards(): arrived = lax.all_to_all(summed, ZC, 0, 0, tiled=True)  31.2 us
    all_to_all x1, blocking collectives, gather_by_all_to_all(): arrived = lax.all_to_all(spread, axes, 0, 0, tiled=True)  29.9 us
    all_to_all x1, starting transfers between devices, gather_by_all_to_all(): arrived = lax.all_to_all(spread, axes, 0, 0, tiled=True)  11.6 us
    dot_general x1, matrix products, shards(): jnp.dot(attn_rows, w_cols, preferred_element_type=jnp.float32)  8.23 us
    reduce_sum x1, other arithmetic, shards(): jnp.sum(anc_w.astype(jnp.float32), axis=-1)  4.89 us
  transfers between devices with their start and end apart: 5, of which 5 were waited for; matrix products, arithmetic and copies ran while one was open for 8% of the time, Pallas kernels for 0%

profile of v15, /device:TPU:24, one launch (start us, length us, event | category | flops | bytes accessed | tf_op | source)
XLA Modules:
  0.0 225.3 jit_solution(2938527863047704503)
XLA Ops:
  6.5 0.8 pad_maximum_fusion
  7.4 1.6 broadcast_in_dim.81
  9.0 11.6 %all-to-all-start = ((bf16[32,2,64,256]{3,2,1,0:T(8,128)(2,1)}), bf16[32,2,64,256]{3,2,1,0:T(8,128)(2,1)S(1)}, u32[]{:S(2)}, u32[]{:S(2)}) async-start(bf16[32,2,64,256]{3,2,1,0:T(8,128)(2,1)} %broadcast_in_dim.81), calls=%async_computation | async-start | bytes 4194304 | tf_op jit(solution)/shard_map/all_to_all | solution.py:90
  20.7 1.1 collective-permute-done
  21.9 48.5 %all-to-all-done = bf16[32,2,64,256]{3,2,1,0:T(8,128)(2,1)S(1)} async-done(((bf16[32,2,64,256]{3,2,1,0:T(8,128)(2,1)}), bf16[32,2,64,256]{3,2,1,0:T(8,128)(2,1)S(1)}, u32[]{:S(2)}, u32[]{:S(2)}) %all-to-all-start) | async-done | bytes 2097184 | tf_op jit(solution)/shard_map/all_to_all | solution.py:90
  70.4 0.6 gather_fusion
  71.0 1.1 broadcast_select_fusion
  72.2 0.6 gather_fusion.1
  72.8 2.3 %collective-permute-done.1 = bf16[32,64,256]{2,1,0:T(8,128)(2,1)} collective-permute-done((bf16[32,64,256]{2,1,0:T(8,128)(2,1)}, bf16[32,64,256]{2,1,0:T(8,128)(2,1)}, u32[]{:S(2)}, u32[]{:S(2)}) %collective-permute-start.1) | collective-permute-done | bytes 1048608 | tf_op jit(solution)/shard_map/ppermute | solution.py:39
  75.2 1.4 select_select_fusion
  77.5 1.8 select_reduce_fusion.1
  79.6 2.3 %fusion.17 = (bf16[2048,1,1,128]{3,1,0,2:T(2,128)(2,1)S(1)}, bf16[2048,1,1,128]{3,1,0,2:T(2,128)(2,1)}) fusion(bf16[2048,2,1,128]{3,1,0,2:T(2,128)(2,1)S(1)} %reshape.159), kind=kLoop, calls=%fused_computation.60 | loop fusion | bytes 2097152 | tf_op jit(solution)/shard_map/slice | solution.py:50
  81.9 0.7 copy.37
  82.6 4.0 %select_reduce_fusion = (f32[8,256]{1,0:T(8,128)S(1)}, f32[2048,8,256]{2,0,1:T(8,128)S(1)}) fusion(pred[2048]{0:T(1024)(128)(4,1)S(1)} %iota_compare_fusion.1, bf16[256,1,8,128]{3,2,0,1:T(8,128)(2,1)S(1)} %bitcast.96, bf16[2048,1,1,128]{3,1,0,2:T(2,128)(2,1)} %get-tuple-element.19), kind=kOutput, calls=%fused_computation.4 | convolution fusion | flops 1086322688 | bytes 17836032 | tf_op jit(solution)/shard_map/kgnd,kjd->kgnj/dot_general | solution.py:56
  87.1 4.9 %convert_reduce_fusion = (f32[8,256]{1,0:T(8,128)S(1)}, bf16[8,256,2048]{1,2,0:T(8,128)(2,1)S(1)}) fusion(f32[8,256]{1,0:T(8,128)S(1)} %max.9, f32[2048,8,256]{2,0,1:T(8,128)S(1)} %get-tuple-element.23, pred[2048]{0:T(1024)(128)(4,1)S(1)} %iota_compare_fusion.1), kind=kLoop, calls=%fused_computation.2 | loop fusion | flops 25163776 | bytes 25184256 | tf_op jit(solution)/shard_map/reduce_sum | solution.py:68
  92.0 1.3 fusion.4
  93.3 0.6 fusion.2
  94.3 29.9 %all_to_all.15 = bf16[4,256,1024]{2,1,0:T(8,128)(2,1)S(1)} all-to-all(bf16[4,256,1024]{2,1,0:T(8,128)(2,1)S(1)} %broadcast_in_dim.86), channel_id=1, replica_groups=mesh['branch'=2,'head'=4,'y'=4,'zl'=4,'core'=2] {'y'}, dimensions={0} | all-to-all | bytes 4194304 | tf_op jit(solution)/shard_map/all_to_all | solution.py:90
  124.3 2.4 %all-gather.2.cloned.1.call-done = bf16[1024,2048]{1,0:T(8,128)(2,1)} async-done(((bf16[1024,256]{1,0:T(8,128)(2,1)}), bf16[1024,2048]{1,0:T(8,128)(2,1)}) %all-gather.2.cloned.1.call-update) | async-done | bytes 4194320 | tf_op jit(solution)/shard_map/all_gather | solution.py:46
  126.7 8.2 %convolution_convert_fusion = bf16[1024,2048]{1,0:T(8,128)(2,1)} fusion(bf16[1024,1024]{1,0:T(8,128)(2,1)S(1)} %bitcast.97, bf16[1024,2048]{1,0:T(8,128)(2,1)} %all-gather.2.cloned.1.call-done), kind=kOutput, calls=%fused_computation.6 | convolution fusion | flops 4297064448 | bytes 10485760 | tf_op jit(solution)/shard_map/dot_general | solution.py:76
  135.0 50.1 %reduce-scatter.2.cloned.1.call-done = bf16[256,2048]{1,0:T(8,128)(2,1)} async-done(((bf16[1024,2048]{1,0:T(8,128)(2,1)}), bf16[256,2048]{1,0:T(8,128)(2,1)}) %reduce-scatter.2.cloned.1.call-update) | async-done | bytes 1048592 | tf_op jit(solution)/shard_map/reduce_scatter | solution.py:79
  185.0 1.3 copy.57
  186.3 31.2 %all_to_all.16 = bf16[8,256,256]{2,1,0:T(8,128)(2,1)S(1)} all-to-all(bf16[8,256,256]{2,1,0:T(8,128)(2,1)S(1)} %bitcast.93), channel_id=1, replica_groups=mesh['branch'=2,'head'=4,'y'=4,'zl'=4,'core'=2] {'zl','core'}, dimensions={0} | all-to-all | bytes 2097152 | tf_op jit(solution)/shard_map/all_to_all | solution.py:83
  217.5 1.0 copy.60
  (30 shorter events, 1.6 us)
Async XLA Ops:
  6.5 71.0 %copy-start = (bf16[256,128]{1,0:T(8,128)(2,1)S(1)}, bf16[256,128]{1,0:T(8,128)(2,1)}, u32[]{:S(2)}) copy-start(bf16[256,128]{1,0:T(8,128)(2,1)} %param.11) | copy-start | bytes 196612
  9.0 11.7 %copy-start.3 = (s32[1,32]{1,0:T(1,128)S(1)}, s32[1,32]{1,0:T(1,128)}, u32[]{:S(2)}) copy-start(s32[1,32]{1,0:T(1,128)} %param.15) | copy-start | bytes 388
  9.0 61.4 %all-to-all-start = ((bf16[32,2,64,256]{3,2,1,0:T(8,128)(2,1)}), bf16[32,2,64,256]{3,2,1,0:T(8,128)(2,1)S(1)}, u32[]{:S(2)}, u32[]{:S(2)}) async-start(bf16[32,2,64,256]{3,2,1,0:T(8,128)(2,1)} %broadcast_in_dim.81), calls=%async_computation | async-start | bytes 4194304 | tf_op jit(solution)/shard_map/all_to_all | solution.py:90
  20.6 106.1 %all-gather.2.cloned.1.call-start = ((), (), s32[]{:S(2)}) async-start(), calls=%async_computation.4 | async-start | bytes 4718592 | tf_op jit(solution)/shard_map/all_gather | solution.py:46
  20.6 1.2 collective-permute-start
  72.2 3.0 %collective-permute-start.1 = (bf16[32,64,256]{2,1,0:T(8,128)(2,1)}, bf16[32,64,256]{2,1,0:T(8,128)(2,1)}, u32[]{:S(2)}, u32[]{:S(2)}) collective-permute-start(bf16[32,64,256]{2,1,0:T(8,128)(2,1)} %broadcast_select_fusion), channel_id=1, source_target_pairs={{0,1},{1,0},{2,3},{3,2},{4,5},{5,4},{6,7},{7,6},{8,9},{9,8},{10,11... | collective-permute-start | bytes 3145736 | tf_op jit(solution)/shard_map/ppermute | solution.py:39
  72.8 3.9 %copy-start.2 = (bf16[256,1024]{1,0:T(8,128)(2,1)S(1)}, bf16[256,1024]{1,0:T(8,128)(2,1)}, u32[]{:S(2)}) copy-start(bf16[256,1024]{1,0:T(8,128)(2,1)} %param.10) | copy-start | bytes 1572868
  76.6 108.4 %reduce-scatter.2.cloned.1.call-start = ((), (), s32[]{:S(2)}) async-start(), calls=%async_computation.5 | async-start | bytes 5242880 | tf_op jit(solution)/shard_map/reduce_scatter | solution.py:79
  82.5 4.1 %copy-start.1 = (f32[8,256,256]{1,2,0:T(8,128)S(1)}, f32[8,256,256]{1,2,0:T(8,128)}, u32[]{:S(2)}) copy-start(f32[8,256,256]{1,2,0:T(8,128)} %get-tuple-element.21) | copy-start | bytes 6291460
  92.0 1.3 copy-start.4
Sparse Core Ops, SparseCore 0:
  76.8 49.8 all-gather.1
  135.1 49.9 reduce-scatter.1

commit v16 on v13

--- a/solution.py
+++ b/solution.py
@@ -31,11 +31,11 @@
 
     kv_local = jnp.concatenate([cache_keys, cache_values], axis=-1)
     kv_chips = gather_by_all_to_all(kv_local, ("branch", "y", "zl"))
+    out_weight, kv_chips = lax.optimization_barrier((out_weight, kv_chips))
+    w_cols = lax.all_gather(out_weight, ZC, axis=1, tiled=True)
     n_core = lax.axis_size("core")
     kv_other = lax.ppermute(kv_chips, "core", [(c, (c + 1) % n_core) for c in range(n_core)])
     kv_all = jnp.concatenate([kv_chips, kv_other], axis=0)
-    out_weight, kv_all = lax.optimization_barrier((out_weight, kv_all))
-    w_cols = lax.all_gather(out_weight, ZC, axis=1, tiled=True)
     pages_here = cache_keys.shape[0]
     n_chips = lax.axis_size(("branch", "y", "zl"))
     owner = block_table[0] // pages_here

time: 225 us -> 219 us (0.973)
  waiting for transfers between devices: 57.7 us -> 49.8 us
    all_gather x1, waiting for transfers between devices: 3.48 us -> 0.01 us  [shards(): w_cols = lax.all_gather(out_weight, ZC, axis=1, tiled=True)]
    ppermute x1, waiting for transfers between devices: 4.16 us -> 1.27 us  [shards(): lax.ppermute(kv_chips, 'core', [(c, (c + 1) % n_core) for c in range(n_co...]
  transfers between devices with their start and end apart: 3 -> 3, of which waited for: 3 -> 2; matrix products, arithmetic and copies ran while one was open for 7% -> 9% of each run, Pallas kernels for 0% -> 0%
where the time goes in v16:
time: 219 us; the launch traced here: 217 us
  blocking collectives  121 us (55%)
  waiting for transfers between devices  49.8 us (23%)
  matrix products  14.7 us (7%)
  between operations  14.3 us (7%)
  other arithmetic  10.9 us (5%)
  local copies, waits for them, and re-layouts  6.48 us (3%)
    all_to_all x2, blocking collectives, gather_by_all_to_all(): arrived = lax.all_to_all(spread, axes, 0, 0, tiled=True)  90.2 us
    reduce_scatter x1, waiting for transfers between devices, shards(): lax.psum_scatter(partial_term, 'head', scatter_dimension=0, tiled=True)  48.5 us
    all_to_all x1, blocking collectives, shards(): arrived = lax.all_to_all(summed, ZC, 0, 0, tiled=True)  31.2 us
    dot_general x1, matrix products, shards(): jnp.dot(attn_rows, w_cols, preferred_element_type=jnp.float32)  8.21 us
    reduce_sum x1, other arithmetic, shards(): jnp.sum(anc_w.astype(jnp.float32), axis=-1)  4.9 us
  transfers between devices with their start and end apart: 3, of which 2 were waited for; matrix products, arithmetic and copies ran while one was open for 9% of the time, Pallas kernels for 0%

profile of v16, /device:TPU:24, one launch (start us, length us, event | category | flops | bytes accessed | tf_op | source)
XLA Modules:
  0.0 217.5 jit_solution(2790982630411707950)
XLA Ops:
  6.5 0.8 pad_maximum_fusion.1
  7.4 0.2 broadcast_in_dim.79
  7.6 60.7 %all_to_all.15 = bf16[32,2,64,256]{3,2,1,0:T(8,128)(2,1)S(1)} all-to-all(bf16[32,2,64,256]{3,2,1,0:T(8,128)(2,1)S(1)} %broadcast_in_dim.79), channel_id=1, replica_groups=mesh['branch'=2,'head'=4,'y'=4,'zl'=4,'core'=2] {'branch','y','zl'}, dimensions={0} | all-to-all | bytes 4194304 | tf_op jit(solution)/shard_map/all_to_all | solution.py:88
  68.5 0.1 broadcast_in_dim.77
  68.6 0.1 copy.39
  69.5 1.9 select_reduce_fusion.1
  71.4 1.3 collective-permute-done
  72.6 3.9 %pad_maximum_fusion = bf16[128,64,256]{2,1,0:T(8,128)(2,1)} fusion(bf16[64,64,256]{2,1,0:T(8,128)(2,1)} %collective-permute-done, bf16[64,64,256]{2,1,0:T(8,128)(2,1)S(1)} %bitcast.91), kind=kLoop, calls=%fused_computation.5 | loop fusion | flops 2097152 | bytes 8388608 | tf_op jit(solution)/shard_map/concatenate | solution.py:38
  76.5 2.9 %gather_fusion = bf16[32,64,256]{2,1,0:T(8,128)(2,1)S(1)} fusion(bf16[128,64,256]{2,1,0:T(8,128)(2,1)} %pad_maximum_fusion, s32[1024]{0:T(1024)S(1)} %pad_clamp_fusion), kind=kCustom, calls=%fused_computation | custom fusion | bytes 2097280 | tf_op jit(solution)/shard_map/jit(_take)/gather | solution.py:44
  79.5 0.3 gather.7
  79.8 0.7 copy_select_fusion
  80.5 2.7 %select_reduce_fusion = (f32[8,256]{1,0:T(8,128)S(1)}, f32[2048,8,256]{2,0,1:T(8,128)S(1)}) fusion(pred[2048]{0:T(1024)(128)(4,1)S(1)} %iota_compare_fusion.1, bf16[256,1,8,128]{3,2,0,1:T(8,128)(2,1)S(1)} %bitcast.95, bf16[2048,2,1,128]{3,0,2,1:T(8,128)(2,1)S(1)} %copy_select_fusion), kind=kOutput, calls=%fused_computation.3 | convolution fusion | flops 1086322688 | bytes 17836032 | tf_op jit(solution)/shard_map/kgnd,kjd->kgnj/dot_general | solution.py:54
  83.2 0.4 convert_reduce_fusion.1
  83.7 4.9 %convert_reduce_fusion = (f32[8,256]{1,0:T(8,128)S(1)}, bf16[8,256,2048]{1,2,0:T(8,128)(2,1)S(1)}) fusion(f32[8,256]{1,0:T(8,128)S(1)} %max.9, f32[2048,8,256]{2,0,1:T(8,128)S(1)} %get-tuple-element.14, pred[2048]{0:T(1024)(128)(4,1)S(1)} %iota_compare_fusion.1), kind=kLoop, calls=%fused_computation.1 | loop fusion | flops 25163776 | bytes 25184256 | tf_op jit(solution)/shard_map/reduce_sum | solution.py:66
  88.6 1.3 fusion.3
  89.9 0.6 fusion.2
  90.5 0.2 copy.30
  90.7 0.3 broadcast_in_dim.85
  91.0 29.5 %all_to_all.16 = bf16[4,256,1024]{2,1,0:T(8,128)(2,1)S(1)} all-to-all(bf16[4,256,1024]{2,1,0:T(8,128)(2,1)S(1)} %broadcast_in_dim.85), channel_id=1, replica_groups=mesh['branch'=2,'head'=4,'y'=4,'zl'=4,'core'=2] {'y'}, dimensions={0} | all-to-all | bytes 4194304 | tf_op jit(solution)/shard_map/all_to_all | solution.py:88
  120.5 8.2 %convolution_convert_fusion = bf16[1024,2048]{1,0:T(8,128)(2,1)} fusion(bf16[1024,1024]{1,0:T(8,128)(2,1)S(1)} %bitcast.96, bf16[1024,2048]{1,0:T(8,128)(2,1)} %all-gather.2.cloned.1.call-done), kind=kOutput, calls=%fused_computation.6 | convolution fusion | flops 4297064448 | bytes 10485760 | tf_op jit(solution)/shard_map/dot_general | solution.py:74
  128.7 48.5 %reduce-scatter.2.cloned.1.call-done = bf16[256,2048]{1,0:T(8,128)(2,1)} async-done(((bf16[1024,2048]{1,0:T(8,128)(2,1)}), bf16[256,2048]{1,0:T(8,128)(2,1)}) %reduce-scatter.2.cloned.1.call-update) | async-done | bytes 1048592 | tf_op jit(solution)/shard_map/reduce_scatter | solution.py:77
  177.2 1.3 copy.54
  178.5 31.2 %all_to_all.17 = bf16[8,256,256]{2,1,0:T(8,128)(2,1)S(1)} all-to-all(bf16[8,256,256]{2,1,0:T(8,128)(2,1)S(1)} %bitcast.92), channel_id=1, replica_groups=mesh['branch'=2,'head'=4,'y'=4,'zl'=4,'core'=2] {'zl','core'}, dimensions={0} | all-to-all | bytes 2097152 | tf_op jit(solution)/shard_map/all_to_all | solution.py:81
  209.7 1.0 copy.57
  (24 shorter events, 0.3 us)
Async XLA Ops:
  6.5 62.9 %copy-start = (bf16[256,128]{1,0:T(8,128)(2,1)S(1)}, bf16[256,128]{1,0:T(8,128)(2,1)}, u32[]{:S(2)}) copy-start(bf16[256,128]{1,0:T(8,128)(2,1)} %param.9) | copy-start | bytes 196612
  6.5 61.9 %copy-start.4 = (s32[1,32]{1,0:T(1,128)S(1)}, s32[1,32]{1,0:T(1,128)}, u32[]{:S(2)}) copy-start(s32[1,32]{1,0:T(1,128)} %param.13) | copy-start | bytes 388
  6.5 62.1 %copy-start.2 = (bf16[256,1024]{1,0:T(8,128)(2,1)S(1)}, bf16[256,1024]{1,0:T(8,128)(2,1)}, u32[]{:S(2)}) copy-start(bf16[256,1024]{1,0:T(8,128)(2,1)} %param.8) | copy-start | bytes 1572868
  6.5 114.0 %all-gather.2.cloned.1.call-start = ((), (), s32[]{:S(2)}) async-start(), calls=%async_computation.4 | async-start | bytes 4718592 | tf_op jit(solution)/shard_map/all_gather | solution.py:35
  68.3 4.3 %collective-permute-start = (bf16[64,64,256]{2,1,0:T(8,128)(2,1)S(1)}, bf16[64,64,256]{2,1,0:T(8,128)(2,1)}, u32[]{:S(2)}, u32[]{:S(2)}) collective-permute-start(bf16[64,64,256]{2,1,0:T(8,128)(2,1)S(1)} %bitcast.90), channel_id=1, source_target_pairs={{0,1},{1,0},{2,3},{3,2},{4,5},{5,4},{6,7},{7,6},{8,9},{9,8},{10,11... | collective-permute-start | bytes 6291464 | tf_op jit(solution)/shard_map/ppermute | solution.py:37
  68.4 108.8 %reduce-scatter.2.cloned.1.call-start = ((), (), s32[]{:S(2)}) async-start(), calls=%async_computation.5 | async-start | bytes 5242880 | tf_op jit(solution)/shard_map/reduce_scatter | solution.py:77
  80.5 2.8 %copy-start.1 = (f32[8,256,256]{1,2,0:T(8,128)S(1)}, f32[8,256,256]{1,2,0:T(8,128)}, u32[]{:S(2)}) copy-start(f32[8,256,256]{1,2,0:T(8,128)} %get-tuple-element.12) | copy-start | bytes 6291460
  88.6 1.3 copy-start.3
Sparse Core Ops, SparseCore 0:
  68.5 50.5 all-gather.1
  128.9 48.3 reduce-scatter.1
